TPU v7x, 128 devices: a whole 4x4x4 slice. The times are simulated.
128 devices in a mesh: ep: 128 (over y, z, x, core).
Axes of the slice: x: 4, y: 4, z: 4, core: 2. Of those that a mesh axis runs over, the one named last changes fastest.
Arguments:
- tokens: bfloat16 [16384, 2048], P('ep'), may hold values from -6 to 6
- cotangent: bfloat16 [16384, 2048], P('ep'), may hold values from -1 to 1
- gates: float32 [16384, 8], P('ep'), may hold values from 0.1 to 1
- experts: int32 [16384, 8], P('ep'), may hold values from 0 to 127, all different within a row; in each aligned block of 128 rows (0 to 127, 128 to 255, ...) at most 12 rows name the same one
- owner: int32 [128], replicated, may hold values from 0 to 127, each once
- swapped: int32 [64], replicated, may hold values 0 or 1
- w_gate: bfloat16 [128, 2048, 768], P('ep'), may hold values from -0.125 to 0.125
- w_up: bfloat16 [128, 2048, 768], P('ep'), may hold values from -0.125 to 0.125
- w_down: bfloat16 [128, 768, 2048], P('ep'), may hold values from -0.21875 to 0.21875
Outputs:
- mixed: bfloat16 [16384, 2048], P('ep')
- in_grad: bfloat16 [16384, 2048], P('ep')
- gate_grad: float32 [16384, 8], P('ep')
Inputs may be any that keep to these rules, and one draw needn't show every extreme that they name: Each row names 8 different experts. In the rows of one device no expert is named by more than 12 rows, and in every draw some expert is named by exactly 12 rows of some device. `owner`: names each device index once.
All inputs are finite; a program needn't handle non-finite values.
Results may differ from a plain program's by a relative error of at most 0.0065.
Values may be sent and summed in bfloat16 or wider, within the bound.
No kernel may reach another device: no remote copies, remote signals or barrier semaphores. Data moves between devices by JAX's collectives and lax.ppermute only.
A program may use at most 192 MiB of HBM per device.

v0:
```python
import jax
import jax.numpy as jnp
from jax import lax
from jax.sharding import PartitionSpec as P


def project_in(flat, wg, wu):
    act_a = jnp.dot(flat, wg, preferred_element_type=jnp.float32)
    act_b = jnp.dot(flat, wu, preferred_element_type=jnp.float32)
    return (act_a, act_b)


def project_out(act_a, act_b, wd):
    sig = jax.nn.sigmoid(act_a)
    hidden = (act_a * sig * act_b).astype(jnp.bfloat16)
    return jnp.dot(hidden, wd, preferred_element_type=jnp.float32).astype(jnp.bfloat16)


def project_back(cots, act_a, act_b, wg, wu, wd):
    sig = jax.nn.sigmoid(act_a)
    back_hidden = lax.dot_general(
        cots, wd, (((1,), (1,)), ((), ())), preferred_element_type=jnp.float32
    )
    grad_a = (back_hidden * act_b * sig * (1.0 + act_a * (1.0 - sig))).astype(jnp.bfloat16)
    grad_b = (back_hidden * act_a * sig).astype(jnp.bfloat16)
    pair_grad = lax.dot_general(
        grad_a, wg, (((1,), (1,)), ((), ())), preferred_element_type=jnp.float32
    )
    pair_grad = pair_grad + lax.dot_general(
        grad_b, wu, (((1,), (1,)), ((), ())), preferred_element_type=jnp.float32
    )
    return pair_grad.astype(jnp.bfloat16)


def body(tokens, cotangent, gates, experts, owner, swapped, w_gate, w_up, w_down):
    tok_rows, width = tokens.shape
    top_count = experts.shape[1]
    expert_total = owner.shape[0]
    hidden_width = w_gate.shape[2]
    count = lax.axis_size("ep")
    slots = tok_rows * top_count * 3 // (2 * expert_total)
    pairs = tok_rows * top_count
    devices = jnp.arange(count, dtype=jnp.int32)
    dev_flag = jnp.repeat(swapped, 2)
    step_dev = dev_flag * (1 - 2 * (devices % 2))
    holder = owner + jnp.sum(
        jnp.where(owner[:, None] == devices[None, :], step_dev[None, :], 0), axis=1
    )
    wg = w_gate[0]
    wu = w_up[0]
    wd = w_down[0]
    flat_e = experts.reshape(-1)
    chosen = flat_e[:, None] == jnp.arange(expert_total, dtype=jnp.int32)[None, :]
    target = jnp.sum(jnp.where(chosen, holder[None, :], 0), axis=1)
    hot = target[:, None] == devices[None, :]
    running = jnp.cumsum(hot.astype(jnp.int32), axis=0)
    rank = jnp.sum(jnp.where(hot, running, 0), axis=1) - 1
    place = target * slots + rank
    source = (
        jnp.full((count * slots,), pairs, jnp.int32)
        .at[place]
        .set(jnp.arange(pairs, dtype=jnp.int32))
    )
    row_of = source // top_count
    tok_pad = jnp.concatenate([tokens, jnp.zeros((1, width), jnp.bfloat16)], axis=0)
    cot_pad = jnp.concatenate([cotangent, jnp.zeros((1, width), jnp.bfloat16)], axis=0)
    gate_pad = jnp.concatenate([gates.reshape(-1), jnp.zeros((1,), jnp.float32)], axis=0)
    send_x = tok_pad[row_of].reshape(count, slots, width)
    send_c = (cot_pad[row_of].astype(jnp.float32) * gate_pad[source][:, None]).astype(jnp.bfloat16)
    send_c = send_c.reshape(count, slots, width)
    received = lax.all_to_all(send_x, "ep", split_axis=0, concat_axis=0, tiled=True)
    flat = received.reshape(-1, width)
    act_a, act_b = project_in(flat, wg, wu)
    out_rows = project_out(act_a, act_b, wd)
    back = lax.all_to_all(
        out_rows.reshape(received.shape), "ep", split_axis=0, concat_axis=0, tiled=True
    )
    returned = (
        back,
        act_a.reshape(received.shape[0], received.shape[1], hidden_width),
        act_b.reshape(received.shape[0], received.shape[1], hidden_width),
    )
    back = returned[0]
    cot_recv = lax.all_to_all(send_c, "ep", split_axis=0, concat_axis=0, tiled=True)
    act_a = returned[1].reshape(-1, hidden_width)
    act_b = returned[2].reshape(-1, hidden_width)
    pair_grad = project_back(cot_recv.reshape(-1, width), act_a, act_b, wg, wu, wd)
    grad_back = lax.all_to_all(
        pair_grad.reshape(cot_recv.shape), "ep", split_axis=0, concat_axis=0, tiled=True
    )
    out_pairs = (
        back.reshape(-1, width)[place].reshape(tok_rows, top_count, width).astype(jnp.float32)
    )
    grad_pairs = (
        grad_back.reshape(-1, width)[place].reshape(tok_rows, top_count, width).astype(jnp.float32)
    )
    mixed = jnp.sum(gates[:, :, None] * out_pairs, axis=1).astype(jnp.bfloat16)
    gate_grad = jnp.sum(cotangent.astype(jnp.float32)[:, None, :] * out_pairs, axis=2)
    in_grad = jnp.sum(grad_pairs, axis=1).astype(jnp.bfloat16)
    return (mixed, in_grad, gate_grad)


def solution(mesh):
    return jax.shard_map(
        body,
        mesh=mesh,
        in_specs=(
            P("ep", None),
            P("ep", None),
            P("ep", None),
            P("ep", None),
            P(),
            P(),
            P("ep", None, None),
            P("ep", None, None),
            P("ep", None, None),
        ),
        out_specs=(P("ep", None), P("ep", None), P("ep", None)),
        check_vma=False,
    )
```

profile of v0, /device:TPU:27, one launch (start us, length us, event | category | flops | bytes accessed | tf_op | source)
XLA Modules:
  0.0 576.1 jit_solution(12071810358548963593)
XLA Ops:
  0.6 0.9 copy.25
  1.7 0.7 broadcast_in_dim.35
  2.4 0.1 reshape.127
  2.6 0.8 select_reduce_fusion.1
  3.4 0.7 add.73
  4.1 0.4 select_reduce_fusion
  4.4 0.1 copy.26
  4.5 0.2 fusion.16
  4.7 0.8 copy-done.3
  5.6 1.1 broadcast_add_fusion
  6.6 0.1 copy.27
  6.8 0.4 fusion.15
  7.2 4.3 scatter_custom_fusion
  11.5 1.9 concatenate.9
  13.4 13.8 %gather_fusion = bf16[1536,2048]{1,0:T(8,128)(2,1)} fusion(bf16[129,2048]{1,0:T(8,128)(2,1)} %concatenate.9, s32[2048]{0:T(1024)S(1)} %get-tuple-element.14), kind=kCustom, calls=%fused_computation | custom fusion | bytes 12589056 | tf_op jit(solution)/shard_map/gather | solution.py:68
  27.3 10.6 %reshape.129 = bf16[128,12,2048]{2,1,0:T(8,128)(2,1)} reshape(bf16[1536,2048]{1,0:T(8,128)(2,1)} %gather_fusion) | data formatting | bytes 12582912 | tf_op jit(solution)/shard_map/reshape | solution.py:68
  37.9 11.0 %all-to-all-start = ((bf16[128,12,2048]{2,1,0:T(8,128)(2,1)}), bf16[128,12,2048]{2,1,0:T(8,128)(2,1)}, u32[]{:S(2)}, u32[]{:S(2)}) async-start(bf16[128,12,2048]{2,1,0:T(8,128)(2,1)} %reshape.129), calls=%async_computation | async-start | bytes 16777216 | tf_op jit(solution)/shard_map/all_to_all | solution.py:71
  48.9 1.9 concatenate.10
  50.8 13.8 %gather_fusion.2 = bf16[1536,2048]{1,0:T(8,128)(2,1)} fusion(bf16[129,2048]{1,0:T(8,128)(2,1)} %concatenate.10, s32[2048]{0:T(1024)S(1)} %get-tuple-element.14), kind=kCustom, calls=%fused_computation.2 | custom fusion | bytes 12589056 | tf_op jit(solution)/shard_map/gather | solution.py:69
  64.6 11.5 %reshape.139 = f32[128,12,2048]{2,1,0:T(8,128)} reshape(bf16[1536,2048]{1,0:T(8,128)(2,1)} %gather_fusion.2) | data formatting | bytes 18874368 | tf_op jit(solution)/shard_map/convert_element_type | solution.py:69
  76.1 0.1 copy.24
  76.3 8.4 %gather_fusion.3 = f32[1536]{0:T(1024)S(1)} fusion(f32[1025]{0:T(1024)S(1)} %pad_maximum_fusion, s32[2048]{0:T(1024)S(1)} %get-tuple-element.13), kind=kCustom, calls=%fused_computation.3 | custom fusion | bytes 18432 | tf_op jit(solution)/shard_map/gather | solution.py:69
  84.8 9.0 %multiply_convert_fusion = bf16[128,12,2048]{2,1,0:T(8,128)(2,1)} fusion(f32[128,12,2048]{2,1,0:T(8,128)} %reshape.139, f32[128,12]{1,0:T(8,128)S(1)} %mul.92), kind=kLoop, calls=%fused_computation.6 | loop fusion | flops 6291456 | bytes 18880512 | tf_op jit(solution)/shard_map/convert_element_type | solution.py:69
  93.8 58.7 %all-to-all-done = bf16[128,12,2048]{2,1,0:T(8,128)(2,1)} async-done(((bf16[128,12,2048]{2,1,0:T(8,128)(2,1)}), bf16[128,12,2048]{2,1,0:T(8,128)(2,1)}, u32[]{:S(2)}, u32[]{:S(2)}) %all-to-all-start) | async-done | bytes 6291488 | tf_op jit(solution)/shard_map/all_to_all | solution.py:71
  152.5 8.8 %all-to-all-start.2 = ((bf16[128,12,2048]{2,1,0:T(8,128)(2,1)}), bf16[128,12,2048]{2,1,0:T(8,128)(2,1)}, u32[]{:S(2)}, u32[]{:S(2)}) async-start(bf16[128,12,2048]{2,1,0:T(8,128)(2,1)} %multiply_convert_fusion), calls=%async_computation.2 | async-start | bytes 16777216 | tf_op jit(solution)/shard_map/all_to_all | solution.py:84
  161.4 10.7 %reshape.130 = bf16[1536,2048]{1,0:T(8,128)(2,1)} reshape(bf16[128,12,2048]{2,1,0:T(8,128)(2,1)} %all-to-all-done) | data formatting | bytes 12582912 | tf_op jit(solution)/shard_map/reshape | solution.py:72
  172.1 9.3 %fusion.10 = f32[1536,768]{1,0:T(8,128)} fusion(bf16[1536,2048]{1,0:T(8,128)(2,1)} %reshape.130, bf16[1,2048,768]{2,1,0:T(8,128)(2,1)S(1)} %copy-done), kind=kOutput, calls=%fused_computation.26 | convolution fusion | flops 4831838208 | bytes 14155776 | tf_op jit(solution)/shard_map/dot_general | solution.py:8
  181.4 6.7 %fusion.6 = f32[1536,768]{1,0:T(8,128)} fusion(bf16[1536,2048]{1,0:T(8,128)(2,1)S(1)} %copy-done.2, bf16[1,2048,768]{2,1,0:T(8,128)(2,1)S(1)} %copy-done.8), kind=kOutput, calls=%fused_computation.22 | convolution fusion | flops 4831838208 | bytes 14155776 | tf_op jit(solution)/shard_map/dot_general | solution.py:9
  188.1 77.2 %all-to-all-done.2 = bf16[128,12,2048]{2,1,0:T(8,128)(2,1)} async-done(((bf16[128,12,2048]{2,1,0:T(8,128)(2,1)}), bf16[128,12,2048]{2,1,0:T(8,128)(2,1)}, u32[]{:S(2)}, u32[]{:S(2)}) %all-to-all-start.2) | async-done | bytes 6291488 | tf_op jit(solution)/shard_map/all_to_all | solution.py:84
  265.3 10.7 %reshape.134 = bf16[1536,2048]{1,0:T(8,128)(2,1)} reshape(bf16[128,12,2048]{2,1,0:T(8,128)(2,1)} %all-to-all-done.2) | data formatting | bytes 12582912 | tf_op jit(solution)/shard_map/reshape | solution.py:87
  276.0 9.7 %fusion.2 = f32[1536,768]{1,0:T(8,128)} fusion(bf16[1536,2048]{1,0:T(8,128)(2,1)} %reshape.134, bf16[1,768,2048]{2,1,0:T(8,128)(2,1)} %param.17), kind=kOutput, calls=%fused_computation.18 | convolution fusion | flops 4831838208 | bytes 14155776 | tf_op jit(solution)/shard_map/dot_general | solution.py:21
  285.7 14.5 %fusion.8 = f32[1536,2048]{1,0:T(8,128)} fusion(bf16[1,2048,768]{2,1,0:T(8,128)(2,1)S(1)} %copy-done, f32[1536,768]{1,0:T(8,128)} %fusion.10, f32[1536,768]{1,0:T(8,128)} %fusion.2, f32[1536,768]{1,0:T(8,128)S(1)} %copy-done.11), kind=kOutput, calls=%fused_computation.24 | convolution fusion | flops 4843634688 | bytes 29884416 | tf_op jit(solution)/shard_map/dot_general | solution.py:26
  300.2 11.5 %add_convert_fusion = bf16[1536,2048]{1,0:T(8,128)(2,1)} fusion(f32[1536,2048]{1,0:T(8,128)} %fusion.8, bf16[1,2048,768]{2,1,0:T(8,128)(2,1)S(1)} %copy-done.9, f32[1536,768]{1,0:T(8,128)} %fusion.2, f32[1536,768]{1,0:T(8,128)S(1)} %bitcast.40), kind=kOutput, calls=%fused_computation.7 | convolution fusion | flops 4845207552 | bytes 31457280 | tf_op jit(solution)/shard_map/dot_general | solution.py:29
  311.7 10.6 %reshape.135 = bf16[128,12,2048]{2,1,0:T(8,128)(2,1)} reshape(bf16[1536,2048]{1,0:T(8,128)(2,1)} %add_convert_fusion) | data formatting | bytes 12582912 | tf_op jit(solution)/shard_map/reshape | solution.py:89
  322.3 7.9 %all-to-all-start.3 = ((bf16[128,12,2048]{2,1,0:T(8,128)(2,1)}), bf16[128,12,2048]{2,1,0:T(8,128)(2,1)}, u32[]{:S(2)}, u32[]{:S(2)}) async-start(bf16[128,12,2048]{2,1,0:T(8,128)(2,1)} %reshape.135), calls=%async_computation.3 | async-start | bytes 16777216 | tf_op jit(solution)/shard_map/all_to_all | solution.py:88
  330.2 11.0 %convolution_convert_fusion = bf16[1536,2048]{1,0:T(8,128)(2,1)} fusion(bf16[1,768,2048]{2,1,0:T(8,128)(2,1)S(1)} %copy-done.10, f32[1536,768]{1,0:T(8,128)} %fusion.6, f32[1536,768]{1,0:T(8,128)} %fusion.10), kind=kOutput, calls=%fused_computation.12 | convolution fusion | flops 4842061824 | bytes 18874368 | tf_op jit(solution)/shard_map/dot_general | solution.py:16
  341.2 10.6 %reshape.131 = bf16[128,12,2048]{2,1,0:T(8,128)(2,1)} reshape(bf16[1536,2048]{1,0:T(8,128)(2,1)} %convolution_convert_fusion) | data formatting | bytes 12582912 | tf_op jit(solution)/shard_map/reshape | solution.py:76
  351.8 82.0 %all-to-all-done.3 = bf16[128,12,2048]{2,1,0:T(8,128)(2,1)} async-done(((bf16[128,12,2048]{2,1,0:T(8,128)(2,1)}), bf16[128,12,2048]{2,1,0:T(8,128)(2,1)}, u32[]{:S(2)}, u32[]{:S(2)}) %all-to-all-start.3) | async-done | bytes 6291488 | tf_op jit(solution)/shard_map/all_to_all | solution.py:88
  433.9 8.8 %all-to-all-start.1 = ((bf16[128,12,2048]{2,1,0:T(8,128)(2,1)}), bf16[128,12,2048]{2,1,0:T(8,128)(2,1)}, u32[]{:S(2)}, u32[]{:S(2)}) async-start(bf16[128,12,2048]{2,1,0:T(8,128)(2,1)} %reshape.131), calls=%async_computation.1 | async-start | bytes 16777216 | tf_op jit(solution)/shard_map/all_to_all | solution.py:75
  442.7 1.1 convert_element_type.61
  443.8 10.7 %reshape.136 = bf16[1536,2048]{1,0:T(8,128)(2,1)} reshape(bf16[128,12,2048]{2,1,0:T(8,128)(2,1)} %all-to-all-done.3) | data formatting | bytes 12582912 | tf_op jit(solution)/shard_map/reshape | solution.py:95
  454.5 12.4 %gather_fusion.4 = bf16[1024,2048]{1,0:T(8,128)(2,1)} fusion(bf16[1536,2048]{1,0:T(8,128)(2,1)} %reshape.136, s32[1024]{0:T(1024)S(1)} %broadcast_clamp_fusion), kind=kCustom, calls=%fused_computation.4 | custom fusion | bytes 8392704 | tf_op jit(solution)/shard_map/gather | solution.py:95
  466.9 5.9 %bitcast_reduce_fusion = bf16[128,2048]{1,0:T(8,128)(2,1)} fusion(bf16[1024,2048]{1,0:T(8,128)(2,1)} %gather_fusion.4), kind=kLoop, calls=%fused_computation.17 | loop fusion | flops 1835008 | bytes 4718592 | tf_op jit(solution)/shard_map/reduce_sum | solution.py:99
  472.8 73.5 %all-to-all-done.1 = bf16[128,12,2048]{2,1,0:T(8,128)(2,1)} async-done(((bf16[128,12,2048]{2,1,0:T(8,128)(2,1)}), bf16[128,12,2048]{2,1,0:T(8,128)(2,1)}, u32[]{:S(2)}, u32[]{:S(2)}) %all-to-all-start.1) | async-done | bytes 6291488 | tf_op jit(solution)/shard_map/all_to_all | solution.py:75
  546.3 10.7 %reshape.132 = bf16[1536,2048]{1,0:T(8,128)(2,1)} reshape(bf16[128,12,2048]{2,1,0:T(8,128)(2,1)} %all-to-all-done.1) | data formatting | bytes 12582912 | tf_op jit(solution)/shard_map/reshape | solution.py:92
  557.0 12.6 %gather_fusion.1 = bf16[1024,2048]{1,0:T(8,128)(2,1)} fusion(bf16[1536,2048]{1,0:T(8,128)(2,1)} %reshape.132, s32[1024]{0:T(1024)S(1)} %broadcast_clamp_fusion), kind=kCustom, calls=%fused_computation.1 | custom fusion | bytes 8392704 | tf_op jit(solution)/shard_map/gather | solution.py:92
  569.6 5.8 %fusion.1 = (f32[128,8]{1,0:T(8,128)S(1)}, bf16[128,2048]{1,0:T(8,128)(2,1)}) fusion(bf16[1024,2048]{1,0:T(8,128)(2,1)} %gather_fusion.1, f32[128,2048]{1,0:T(8,128)} %convert_element_type.61, f32[128,8]{1,0:T(8,128)S(1)} %copy.24), kind=kLoop, calls=%fused_computation.11 | loop fusion | flops 10222592 | bytes 5775360 | tf_op jit(solution)/shard_map/reduce_sum | solution.py:98
  575.4 0.7 copy.29
  (42 shorter events, 0.4 us)
Async XLA Ops:
  0.6 171.4 %copy-start = (bf16[1,2048,768]{2,1,0:T(8,128)(2,1)S(1)}, bf16[1,2048,768]{2,1,0:T(8,128)(2,1)}, u32[]{:S(2)}) copy-start(bf16[1,2048,768]{2,1,0:T(8,128)(2,1)} %param.15) | copy-start | bytes 9437188
  4.7 0.8 copy-start.3
  7.2 20.1 %copy-start.5 = (s32[1024,1]{0,1:T(1,128)}, s32[1024,1]{0,1:T(1,128)S(1)}, u32[]{:S(2)}) copy-start(s32[1024,1]{0,1:T(1,128)S(1)} %compare_select_fusion) | copy-start | bytes 12292
  37.9 114.7 %all-to-all-start = ((bf16[128,12,2048]{2,1,0:T(8,128)(2,1)}), bf16[128,12,2048]{2,1,0:T(8,128)(2,1)}, u32[]{:S(2)}, u32[]{:S(2)}) async-start(bf16[128,12,2048]{2,1,0:T(8,128)(2,1)} %reshape.129), calls=%async_computation | async-start | bytes 16777216 | tf_op jit(solution)/shard_map/all_to_all | solution.py:71
  64.6 11.5 %copy-start.7 = (f32[128,8]{0,1:T(8,128)S(1)}, f32[128,8]{0,1:T(8,128)}, u32[]{:S(2)}) copy-start(f32[128,8]{0,1:T(8,128)} %param.11) | copy-start | bytes 12292
  152.5 112.7 %all-to-all-start.2 = ((bf16[128,12,2048]{2,1,0:T(8,128)(2,1)}), bf16[128,12,2048]{2,1,0:T(8,128)(2,1)}, u32[]{:S(2)}, u32[]{:S(2)}) async-start(bf16[128,12,2048]{2,1,0:T(8,128)(2,1)} %multiply_convert_fusion), calls=%async_computation.2 | async-start | bytes 16777216 | tf_op jit(solution)/shard_map/all_to_all | solution.py:84
  172.1 9.3 %copy-start.2 = (bf16[1536,2048]{1,0:T(8,128)(2,1)S(1)}, bf16[1536,2048]{1,0:T(8,128)(2,1)}, u32[]{:S(2)}) copy-start(bf16[1536,2048]{1,0:T(8,128)(2,1)} %reshape.130) | copy-start | bytes 18874372
  172.1 9.3 %copy-start.8 = (bf16[1,2048,768]{2,1,0:T(8,128)(2,1)S(1)}, bf16[1,2048,768]{2,1,0:T(8,128)(2,1)}, u32[]{:S(2)}) copy-start(bf16[1,2048,768]{2,1,0:T(8,128)(2,1)} %param.16) | copy-start | bytes 9437188
  276.0 9.7 %copy-start.11 = (f32[1536,768]{1,0:T(8,128)S(1)}, f32[1536,768]{1,0:T(8,128)}, u32[]{:S(2)}) copy-start(f32[1536,768]{1,0:T(8,128)} %fusion.6) | copy-start | bytes 14155780
  276.0 24.2 %slice-start = ((s8[4718592]{0:T(1024)(128)(4,1)}), s8[4194304]{0:T(1024)(128)(4,1)S(1)}, s32[]{:S(2)}) async-start(s8[4718592]{0:T(1024)(128)(4,1)} %bitcast.39), calls=%async_computation.4 | async-start | bytes 8388608
  285.7 14.6 %copy-start.9 = (bf16[1,2048,768]{2,1,0:T(8,128)(2,1)S(1)}, bf16[1,2048,768]{2,1,0:T(8,128)(2,1)}, u32[]{:S(2)}) copy-start(bf16[1,2048,768]{2,1,0:T(8,128)(2,1)} %param.16) | copy-start | bytes 9437188
  285.7 14.6 %slice-start.1 = ((s8[4718592]{0:T(1024)(128)(4,1)}), s8[524288]{0:T(1024)(128)(4,1)S(1)}, s32[]{:S(2)}) async-start(s8[4718592]{0:T(1024)(128)(4,1)} %bitcast.39), calls=%async_computation.5 | async-start | bytes 1048576
  322.3 7.9 %copy-start.10 = (bf16[1,768,2048]{2,1,0:T(8,128)(2,1)S(1)}, bf16[1,768,2048]{2,1,0:T(8,128)(2,1)}, u32[]{:S(2)}) copy-start(bf16[1,768,2048]{2,1,0:T(8,128)(2,1)} %param.17) | copy-start | bytes 9437188
  322.3 111.5 %all-to-all-start.3 = ((bf16[128,12,2048]{2,1,0:T(8,128)(2,1)}), bf16[128,12,2048]{2,1,0:T(8,128)(2,1)}, u32[]{:S(2)}, u32[]{:S(2)}) async-start(bf16[128,12,2048]{2,1,0:T(8,128)(2,1)} %reshape.135), calls=%async_computation.3 | async-start | bytes 16777216 | tf_op jit(solution)/shard_map/all_to_all | solution.py:88
  351.8 90.9 %copy-start.4 = (bf16[128,2048]{1,0:T(8,128)(2,1)S(1)}, bf16[128,2048]{1,0:T(8,128)(2,1)}, u32[]{:S(2)}) copy-start(bf16[128,2048]{1,0:T(8,128)(2,1)} %param.10) | copy-start | bytes 1572868
  351.8 92.0 %copy-start.6 = (s32[1024,1]{0,1:T(1,128)S(1)}, s32[1024,1]{0,1:T(1,128)}, u32[]{:S(2)}) copy-start(s32[1024,1]{0,1:T(1,128)} %copy-done.5) | copy-start | bytes 12292
  433.9 112.5 %all-to-all-start.1 = ((bf16[128,12,2048]{2,1,0:T(8,128)(2,1)}), bf16[128,12,2048]{2,1,0:T(8,128)(2,1)}, u32[]{:S(2)}, u32[]{:S(2)}) async-start(bf16[128,12,2048]{2,1,0:T(8,128)(2,1)} %reshape.131), calls=%async_computation.1 | async-start | bytes 16777216 | tf_op jit(solution)/shard_map/all_to_all | solution.py:75
  557.0 19.0 %copy-start.1 = (bf16[1,2048,768]{2,1,0:T(8,128)(2,1)S(1)}, bf16[1,2048,768]{2,1,0:T(8,128)(2,1)}, u32[]{:S(2)}) copy-start(bf16[1,2048,768]{2,1,0:T(8,128)(2,1)} %param.15) | copy-start | bytes 9437188
where the time goes:
time: 579 us; the launch traced here: 576 us
  waiting for transfers between devices  291 us (50%)
  local copies, waits for them, and re-layouts  159 us (27%)
  matrix products  62.7 us (11%)
  starting transfers between devices  36.5 us (6%)
  other arithmetic  25.4 us (4%)
    all_to_all x1, waiting for transfers between devices, body(): lax.all_to_all(pair_grad.reshape(cot_recv.shape), 'ep', split_axis=0, con...  82 us
    all_to_all x1, waiting for transfers between devices, body(): lax.all_to_all(send_c, 'ep', split_axis=0, concat_axis=0, tiled=True)  77.2 us
    all_to_all x1, waiting for transfers between devices, body(): lax.all_to_all(out_rows.reshape(received.shape), 'ep', split_axis=0, conc...  73.5 us
    all_to_all x1, waiting for transfers between devices, body(): lax.all_to_all(send_x, 'ep', split_axis=0, concat_axis=0, tiled=True)  58.7 us
    dot_general x1, matrix products, project_back(): lax.dot_general(grad_a, wg, (((1,), (1,)), ((), ())), preferred_element_t...  14.5 us
    gather x1, local copies, waits for them, and re-layouts, body(): send_x = tok_pad[row_of].reshape(count, slots, width)  13.8 us
    gather x1, local copies, waits for them, and re-layouts, body(): cot_pad[row_of].astype(jnp.float32) * gate_pad[source][:, None]  13.8 us
    gather x1, local copies, waits for them, and re-layouts, body(): back.reshape(-1, width)[place].reshape(tok_rows, top_count, width)  12.6 us
  transfers between devices with their start and end apart: 4, of which 4 were waited for; matrix products, arithmetic and copies ran while one was open for 21% of the time, Pallas kernels for 0%

commit v1 on v0

--- a/solution.py
+++ b/solution.py
@@ -2,6 +2,8 @@
 import jax.numpy as jnp
 from jax import lax
 from jax.sharding import PartitionSpec as P
+
+LANES = 128
 
 
 def project_in(flat, wg, wu):
@@ -36,10 +38,10 @@
     tok_rows, width = tokens.shape
     top_count = experts.shape[1]
     expert_total = owner.shape[0]
-    hidden_width = w_gate.shape[2]
     count = lax.axis_size("ep")
     slots = tok_rows * top_count * 3 // (2 * expert_total)
     pairs = tok_rows * top_count
+    sub = width // LANES
     devices = jnp.arange(count, dtype=jnp.int32)
     dev_flag = jnp.repeat(swapped, 2)
     step_dev = dev_flag * (1 - 2 * (devices % 2))
@@ -65,39 +67,38 @@
     tok_pad = jnp.concatenate([tokens, jnp.zeros((1, width), jnp.bfloat16)], axis=0)
     cot_pad = jnp.concatenate([cotangent, jnp.zeros((1, width), jnp.bfloat16)], axis=0)
     gate_pad = jnp.concatenate([gates.reshape(-1), jnp.zeros((1,), jnp.float32)], axis=0)
-    send_x = tok_pad[row_of].reshape(count, slots, width)
-    send_c = (cot_pad[row_of].astype(jnp.float32) * gate_pad[source][:, None]).astype(jnp.bfloat16)
-    send_c = send_c.reshape(count, slots, width)
-    received = lax.all_to_all(send_x, "ep", split_axis=0, concat_axis=0, tiled=True)
-    flat = received.reshape(-1, width)
+    tok3 = tok_pad.reshape(tok_rows + 1, sub, LANES)
+    cot3 = cot_pad.reshape(tok_rows + 1, sub, LANES)
+    send_x = tok3[row_of].reshape(count, slots, sub, LANES)
+    send_c = (cot3[row_of].astype(jnp.float32) * gate_pad[source][:, None, None]).astype(jnp.bfloat16)
+    send_c = send_c.reshape(count, slots, sub, LANES)
+    recv_x = lax.all_to_all(send_x, "ep", split_axis=0, concat_axis=0, tiled=True)
+    recv_c = lax.all_to_all(send_c, "ep", split_axis=0, concat_axis=0, tiled=True)
+    flat = recv_x.reshape(-1, width)
     act_a, act_b = project_in(flat, wg, wu)
     out_rows = project_out(act_a, act_b, wd)
     back = lax.all_to_all(
-        out_rows.reshape(received.shape), "ep", split_axis=0, concat_axis=0, tiled=True
+        out_rows.reshape(count, slots, sub, LANES), "ep", split_axis=0, concat_axis=0, tiled=True
     )
-    returned = (
-        back,
-        act_a.reshape(received.shape[0], received.shape[1], hidden_width),
-        act_b.reshape(received.shape[0], received.shape[1], hidden_width),
-    )
-    back = returned[0]
-    cot_recv = lax.all_to_all(send_c, "ep", split_axis=0, concat_axis=0, tiled=True)
-    act_a = returned[1].reshape(-1, hidden_width)
-    act_b = returned[2].reshape(-1, hidden_width)
-    pair_grad = project_back(cot_recv.reshape(-1, width), act_a, act_b, wg, wu, wd)
+    pair_grad = project_back(recv_c.reshape(-1, width), act_a, act_b, wg, wu, wd)
     grad_back = lax.all_to_all(
-        pair_grad.reshape(cot_recv.shape), "ep", split_axis=0, concat_axis=0, tiled=True
+        pair_grad.reshape(count, slots, sub, LANES), "ep", split_axis=0, concat_axis=0, tiled=True
     )
     out_pairs = (
-        back.reshape(-1, width)[place].reshape(tok_rows, top_count, width).astype(jnp.float32)
+        back.reshape(-1, sub, LANES)[place]
+        .reshape(tok_rows, top_count, sub, LANES)
+        .astype(jnp.float32)
     )
     grad_pairs = (
-        grad_back.reshape(-1, width)[place].reshape(tok_rows, top_count, width).astype(jnp.float32)
+        grad_back.reshape(-1, sub, LANES)[place]
+        .reshape(tok_rows, top_count, sub, LANES)
+        .astype(jnp.float32)
     )
-    mixed = jnp.sum(gates[:, :, None] * out_pairs, axis=1).astype(jnp.bfloat16)
-    gate_grad = jnp.sum(cotangent.astype(jnp.float32)[:, None, :] * out_pairs, axis=2)
+    mixed = jnp.sum(gates[:, :, None, None] * out_pairs, axis=1).astype(jnp.bfloat16)
+    cot_f = cotangent.reshape(tok_rows, 1, sub, LANES).astype(jnp.float32)
+    gate_grad = jnp.sum(cot_f * out_pairs, axis=(2, 3))
     in_grad = jnp.sum(grad_pairs, axis=1).astype(jnp.bfloat16)
-    return (mixed, in_grad, gate_grad)
+    return (mixed.reshape(tok_rows, width), in_grad.reshape(tok_rows, width), gate_grad)
 
 
 def solution(mesh):

time: 579 us -> 379 us (0.65)
  waiting for transfers between devices: 291 us -> 194 us
  local copies, waits for them, and re-layouts: 159 us -> 74.4 us
  starting transfers between devices: 36.5 us -> 28.1 us
    reshape x7 -> x2, local copies, waits for them, and re-layouts: 74.6 us -> 1.71 us  [the longest x1 0.88 us: body(): cot3 = cot_pad.reshape(tok_rows + 1, sub, LANES)]
    all_to_all x2, waiting for transfers between devices: 156 us -> 94.1 us  [the longest x1 57.2 us: body(): lax.all_to_all(pair_grad.reshape(count, slots, sub, LANES), 'ep', split_a...]
    all_to_all x1, waiting for transfers between devices: 77.2 us -> 47.1 us  [body(): lax.all_to_all(send_c, 'ep', split_axis=0, concat_axis=0, tiled=True)]
    unnamed x31 -> x32, local copies, waits for them, and re-layouts: 2.54 us -> 18.9 us
    gather x5, local copies, waits for them, and re-layouts: 61.1 us -> 45.8 us  [the longest x1 11.4 us: body(): grad_back.reshape(-1, sub, LANES)[place]]
    convert_element_type x1 -> x0, local copies, waits for them, and re-layouts: 11.5 us -> none  [body(): cot_pad[row_of].astype(jnp.float32) * gate_pad[source][:, None]]
    all_to_all x1, waiting for transfers between devices: 58.7 us -> 52.7 us  [body(): lax.all_to_all(send_x, 'ep', split_axis=0, concat_axis=0, tiled=True)]
  transfers between devices with their start and end apart: 4 -> 4, of which waited for: 4 -> 4; matrix products, arithmetic and copies ran while one was open for 21% -> 30% of each run, Pallas kernels for 0% -> 0%
where the time goes in v1:
time: 379 us; the launch traced here: 378 us
  waiting for transfers between devices  194 us (51%)
  local copies, waits for them, and re-layouts  74.4 us (20%)
  matrix products  58.1 us (15%)
  starting transfers between devices  28.1 us (7%)
  other arithmetic  22.3 us (6%)
    all_to_all x1, waiting for transfers between devices, body(): lax.all_to_all(pair_grad.reshape(count, slots, sub, LANES), 'ep', split_a...  57.2 us
    all_to_all x1, waiting for transfers between devices, body(): lax.all_to_all(send_x, 'ep', split_axis=0, concat_axis=0, tiled=True)  52.7 us
    all_to_all x1, waiting for transfers between devices, body(): lax.all_to_all(send_c, 'ep', split_axis=0, concat_axis=0, tiled=True)  47.1 us
    all_to_all x1, waiting for transfers between devices, body(): lax.all_to_all(out_rows.reshape(count, slots, sub, LANES), 'ep', split_ax...  36.9 us
    unnamed x32, local copies, waits for them, and re-layouts  18.9 us
    dot_general x1, matrix products, project_back(): lax.dot_general(grad_a, wg, (((1,), (1,)), ((), ())), preferred_element_t...  14.7 us
    gather x1, local copies, waits for them, and re-layouts, body(): grad_back.reshape(-1, sub, LANES)[place]  11.4 us
    dot_general x1, matrix products, project_back(): lax.dot_general(grad_b, wu, (((1,), (1,)), ((), ())), preferred_element_t...  11.3 us
  transfers between devices with their start and end apart: 4, of which 4 were waited for; matrix products, arithmetic and copies ran while one was open for 30% of the time, Pallas kernels for 0%

profile of v1, /device:TPU:27, one launch (start us, length us, event | category | flops | bytes accessed | tf_op | source)
XLA Modules:
  0.0 377.7 jit_solution(10853445347131429192)
XLA Ops:
  0.6 0.9 broadcast_in_dim.52
  1.5 0.1 reshape.146
  1.7 0.8 select_reduce_fusion.1
  2.5 0.7 add.73
  3.2 0.8 copy.25
  4.1 0.4 select_reduce_fusion
  4.5 0.2 fusion.29
  4.7 0.8 copy-done.2
  5.6 1.1 broadcast_add_fusion
  6.8 0.4 fusion.28
  7.2 4.3 %scatter_custom_fusion = s32[1536]{0:T(1024)S(1)} fusion(s32[1024]{0:T(1024)S(1)} %bitcast.94, s32[1024]{0:T(1024)S(1)} %iota.18, s32[]{:T(128)} %constant.26.clone.1), kind=kCustom, calls=%fused_computation.70 | custom fusion | bytes 6148 | tf_op jit(solution)/shard_map/scatter | solution.py:64
  11.5 1.1 concatenate.9
  12.6 0.1 copy.30
  12.7 0.8 slice.20
  13.6 7.5 %gather_fusion = bf16[1536,16,128]{2,1,0:T(8,128)(2,1)} fusion(bf16[129,16,128]{2,1,0:T(8,128)(2,1)} %slice.20, s32[2048]{0:T(1024)S(1)} %get-tuple-element.12), kind=kCustom, calls=%fused_computation | custom fusion | bytes 12589056 | tf_op jit(solution)/shard_map/gather | solution.py:72
  21.0 10.9 %all-to-all-start = ((bf16[128,12,16,128]{3,2,1,0:T(8,128)(2,1)}), bf16[128,12,16,128]{3,2,1,0:T(8,128)(2,1)}, u32[]{:S(2)}, u32[]{:S(2)}) async-start(bf16[128,12,16,128]{3,2,1,0:T(8,128)(2,1)} %bitcast.81), calls=%async_computation | async-start | bytes 12582912 | tf_op jit(solution)/shard_map/all_to_all | solution.py:75
  32.2 8.4 %gather_fusion.3 = f32[1536]{0:T(1024)S(1)} fusion(f32[1025]{0:T(1024)S(1)} %pad_maximum_fusion, s32[2048]{0:T(1024)S(1)} %get-tuple-element.11), kind=kCustom, calls=%fused_computation.3 | custom fusion | bytes 18432 | tf_op jit(solution)/shard_map/gather | solution.py:73
  40.7 1.1 concatenate.10
  41.8 0.1 copy.34
  41.9 0.9 slice.21
  42.8 7.4 %gather_fusion.2 = bf16[1536,16,128]{2,1,0:T(8,128)(2,1)} fusion(bf16[129,16,128]{2,1,0:T(8,128)(2,1)} %slice.21, s32[2048]{0:T(1024)S(1)} %get-tuple-element.12), kind=kCustom, calls=%fused_computation.2 | custom fusion | bytes 12589056 | tf_op jit(solution)/shard_map/gather | solution.py:73
  50.2 7.3 %fusion = bf16[128,12,16,128]{3,2,1,0:T(8,128)(2,1)} fusion(bf16[128,12,16,128]{3,2,1,0:T(8,128)(2,1)} %bitcast.82, f32[128,12]{1,0:T(8,128)S(1)} %mul.92), kind=kLoop, calls=%fused_computation.7 | loop fusion | flops 9437184 | bytes 12589056 | tf_op jit(solution)/shard_map/convert_element_type | solution.py:73
  57.5 52.7 %all-to-all-done = bf16[128,12,16,128]{3,2,1,0:T(8,128)(2,1)} async-done(((bf16[128,12,16,128]{3,2,1,0:T(8,128)(2,1)}), bf16[128,12,16,128]{3,2,1,0:T(8,128)(2,1)}, u32[]{:S(2)}, u32[]{:S(2)}) %all-to-all-start) | async-done | bytes 6291488 | tf_op jit(solution)/shard_map/all_to_all | solution.py:75
  110.2 5.8 %all-to-all-start.2 = ((bf16[128,12,16,128]{3,2,1,0:T(8,128)(2,1)}), bf16[128,12,16,128]{3,2,1,0:T(8,128)(2,1)}, u32[]{:S(2)}, u32[]{:S(2)}) async-start(bf16[128,12,16,128]{3,2,1,0:T(8,128)(2,1)} %fusion), calls=%async_computation.2 | async-start | bytes 12582912 | tf_op jit(solution)/shard_map/all_to_all | solution.py:76
  116.0 9.0 %fusion.8 = f32[1536,768]{1,0:T(8,128)S(1)} fusion(bf16[192,8,16,128]{3,2,1,0:T(8,128)(2,1)} %bitcast.22, bf16[1,2048,768]{2,1,0:T(8,128)(2,1)} %param.15), kind=kOutput, calls=%fused_computation.19 | convolution fusion | flops 4831838208 | bytes 14155776 | tf_op jit(solution)/shard_map/dot_general | solution.py:10
  125.1 9.6 %fusion.6 = f32[1536,768]{1,0:T(8,128)S(1)} fusion(bf16[192,8,16,128]{3,2,1,0:T(8,128)(2,1)} %bitcast.22, bf16[1,2048,768]{2,1,0:T(8,128)(2,1)S(1)} %copy-done.6), kind=kOutput, calls=%fused_computation.17 | convolution fusion | flops 4831838208 | bytes 14155776 | tf_op jit(solution)/shard_map/dot_general | solution.py:11
  134.7 2.1 copy-done.9
  136.8 5.4 %fusion.22 = bf16[192,8,16,128]{3,1,2,0:T(8,128)(2,1)S(1)} fusion(bf16[1,768,2048]{2,1,0:T(8,128)(2,1)S(1)} %copy-done, f32[1536,768]{1,0:T(8,128)S(1)} %fusion.6, f32[1536,768]{1,0:T(8,128)S(1)} %fusion.8), kind=kOutput, calls=%fused_computation.36 | convolution fusion | flops 4842061824 | bytes 18874368 | tf_op jit(solution)/shard_map/dot_general | solution.py:18
  142.2 4.9 %copy.32 = bf16[192,8,16,128]{3,2,1,0:T(8,128)(2,1)} copy(bf16[192,8,16,128]{3,1,2,0:T(8,128)(2,1)S(1)} %fusion.22) | data formatting | bytes 12582912
  147.1 47.1 %all-to-all-done.2 = bf16[128,12,16,128]{3,2,1,0:T(8,128)(2,1)} async-done(((bf16[128,12,16,128]{3,2,1,0:T(8,128)(2,1)}), bf16[128,12,16,128]{3,2,1,0:T(8,128)(2,1)}, u32[]{:S(2)}, u32[]{:S(2)}) %all-to-all-start.2) | async-done | bytes 6291488 | tf_op jit(solution)/shard_map/all_to_all | solution.py:76
  194.2 5.7 %all-to-all-start.1 = ((bf16[128,12,16,128]{3,2,1,0:T(8,128)(2,1)}), bf16[128,12,16,128]{3,2,1,0:T(8,128)(2,1)}, u32[]{:S(2)}, u32[]{:S(2)}) async-start(bf16[128,12,16,128]{3,2,1,0:T(8,128)(2,1)} %bitcast.80), calls=%async_computation.1 | async-start | bytes 12582912 | tf_op jit(solution)/shard_map/all_to_all | solution.py:80
  199.9 8.1 %fusion.3 = f32[1536,768]{1,0:T(8,128)S(1)} fusion(bf16[192,8,16,128]{3,2,1,0:T(8,128)(2,1)} %bitcast.33, bf16[1,768,2048]{2,1,0:T(8,128)(2,1)S(1)} %copy-done), kind=kOutput, calls=%fused_computation.14 | convolution fusion | flops 4831838208 | bytes 14155776 | tf_op jit(solution)/shard_map/dot_general | solution.py:23
  208.1 2.2 copy-done.10
  210.2 14.7 %fusion.16 = f32[1536,2048]{1,0:T(8,128)} fusion(bf16[1,2048,768]{2,1,0:T(8,128)(2,1)S(1)} %copy-done.5, f32[1536,768]{1,0:T(8,128)} %copy-done.8, f32[1536,768]{1,0:T(8,128)S(1)} %fusion.3, f32[1536,768]{1,0:T(8,128)} %copy-done.9), kind=kOutput, calls=%fused_computation.32 | convolution fusion | flops 4843634688 | bytes 29884416 | tf_op jit(solution)/shard_map/dot_general | solution.py:28
  224.9 11.3 %fusion.19 = bf16[192,8,16,128]{3,1,2,0:T(8,128)(2,1)S(1)} fusion(f32[1536,2048]{1,0:T(8,128)} %fusion.16, bf16[1,2048,768]{2,1,0:T(8,128)(2,1)S(1)} %copy-done.7, f32[1536,768]{1,0:T(8,128)} %copy-done.10, f32[1536,768]{1,0:T(8,128)} %copy-done.8), kind=kOutput, calls=%fused_computation.35 | convolution fusion | flops 4845207552 | bytes 31457280 | tf_op jit(solution)/shard_map/dot_general | solution.py:31
  236.2 5.0 %copy.36 = bf16[192,8,16,128]{3,2,1,0:T(8,128)(2,1)} copy(bf16[192,8,16,128]{3,1,2,0:T(8,128)(2,1)S(1)} %fusion.19) | data formatting | bytes 12582912
  241.2 36.9 %all-to-all-done.1 = bf16[128,12,16,128]{3,2,1,0:T(8,128)(2,1)} async-done(((bf16[128,12,16,128]{3,2,1,0:T(8,128)(2,1)}), bf16[128,12,16,128]{3,2,1,0:T(8,128)(2,1)}, u32[]{:S(2)}, u32[]{:S(2)}) %all-to-all-start.1) | async-done | bytes 6291488 | tf_op jit(solution)/shard_map/all_to_all | solution.py:80
  278.1 5.7 %all-to-all-start.3 = ((bf16[128,12,16,128]{3,2,1,0:T(8,128)(2,1)}), bf16[128,12,16,128]{3,2,1,0:T(8,128)(2,1)}, u32[]{:S(2)}, u32[]{:S(2)}) async-start(bf16[128,12,16,128]{3,2,1,0:T(8,128)(2,1)} %bitcast.79), calls=%async_computation.3 | async-start | bytes 12582912 | tf_op jit(solution)/shard_map/all_to_all | solution.py:84
  283.9 0.2 copy.38
  284.1 11.2 %gather_fusion.1 = bf16[1024,16,128]{2,1,0:T(8,128)(2,1)} fusion(bf16[1536,16,128]{2,1,0:T(8,128)(2,1)} %bitcast.10, s32[1024]{0:T(1024)S(1)} %broadcast_clamp_fusion), kind=kCustom, calls=%fused_computation.1 | custom fusion | bytes 8392704 | tf_op jit(solution)/shard_map/gather | solution.py:88
  295.3 4.6 %fusion.2 = f32[128,8]{1,0:T(8,128)S(1)} fusion(bf16[128,8,16,128]{3,2,1,0:T(8,128)(2,1)} %bitcast.78, f32[128,16,128]{2,1,0:T(8,128)S(1)} %bitcast.83), kind=kLoop, calls=%fused_computation.12 | loop fusion | flops 6290432 | bytes 5246976 | tf_op jit(solution)/shard_map/reduce_sum | solution.py:99
  299.9 0.7 copy.29
  300.5 3.4 fusion.1
  303.9 0.9 copy.54
  304.8 57.2 %all-to-all-done.3 = bf16[128,12,16,128]{3,2,1,0:T(8,128)(2,1)} async-done(((bf16[128,12,16,128]{3,2,1,0:T(8,128)(2,1)}), bf16[128,12,16,128]{3,2,1,0:T(8,128)(2,1)}, u32[]{:S(2)}, u32[]{:S(2)}) %all-to-all-start.3) | async-done | bytes 6291488 | tf_op jit(solution)/shard_map/all_to_all | solution.py:84
  362.0 11.4 %gather_fusion.4 = bf16[1024,16,128]{2,1,0:T(8,128)(2,1)} fusion(bf16[1536,16,128]{2,1,0:T(8,128)(2,1)} %bitcast.13, s32[1024]{0:T(1024)S(1)} %broadcast_clamp_fusion), kind=kCustom, calls=%fused_computation.4 | custom fusion | bytes 8392704 | tf_op jit(solution)/shard_map/gather | solution.py:93
  373.4 3.3 bitcast_reduce_fusion
  376.8 0.9 copy.53
  (37 shorter events, 0.8 us)
Async XLA Ops:
  0.6 136.2 %copy-start = (bf16[1,768,2048]{2,1,0:T(8,128)(2,1)S(1)}, bf16[1,768,2048]{2,1,0:T(8,128)(2,1)}, u32[]{:S(2)}) copy-start(bf16[1,768,2048]{2,1,0:T(8,128)(2,1)} %param.17) | copy-start | bytes 9437188
  4.7 0.8 copy-start.2
  21.0 11.0 %copy-start.4 = (f32[128,8]{0,1:T(8,128)S(1)}, f32[128,8]{0,1:T(8,128)}, u32[]{:S(2)}) copy-start(f32[128,8]{0,1:T(8,128)} %param.11) | copy-start | bytes 12292
  21.0 89.2 %all-to-all-start = ((bf16[128,12,16,128]{3,2,1,0:T(8,128)(2,1)}), bf16[128,12,16,128]{3,2,1,0:T(8,128)(2,1)}, u32[]{:S(2)}, u32[]{:S(2)}) async-start(bf16[128,12,16,128]{3,2,1,0:T(8,128)(2,1)} %bitcast.81), calls=%async_computation | async-start | bytes 12582912 | tf_op jit(solution)/shard_map/all_to_all | solution.py:75
  110.2 84.0 %all-to-all-start.2 = ((bf16[128,12,16,128]{3,2,1,0:T(8,128)(2,1)}), bf16[128,12,16,128]{3,2,1,0:T(8,128)(2,1)}, u32[]{:S(2)}, u32[]{:S(2)}) async-start(bf16[128,12,16,128]{3,2,1,0:T(8,128)(2,1)} %fusion), calls=%async_computation.2 | async-start | bytes 12582912 | tf_op jit(solution)/shard_map/all_to_all | solution.py:76
  116.0 9.1 %copy-start.6 = (bf16[1,2048,768]{2,1,0:T(8,128)(2,1)S(1)}, bf16[1,2048,768]{2,1,0:T(8,128)(2,1)}, u32[]{:S(2)}) copy-start(bf16[1,2048,768]{2,1,0:T(8,128)(2,1)} %param.16) | copy-start | bytes 9437188
  125.1 9.6 %copy-start.8 = (f32[1536,768]{1,0:T(8,128)}, f32[1536,768]{1,0:T(8,128)S(1)}, u32[]{:S(2)}) copy-start(f32[1536,768]{1,0:T(8,128)S(1)} %fusion.8) | copy-start | bytes 14155780
  134.7 2.1 copy-start.9
  194.2 83.9 %all-to-all-start.1 = ((bf16[128,12,16,128]{3,2,1,0:T(8,128)(2,1)}), bf16[128,12,16,128]{3,2,1,0:T(8,128)(2,1)}, u32[]{:S(2)}, u32[]{:S(2)}) async-start(bf16[128,12,16,128]{3,2,1,0:T(8,128)(2,1)} %bitcast.80), calls=%async_computation.1 | async-start | bytes 12582912 | tf_op jit(solution)/shard_map/all_to_all | solution.py:80
  199.9 10.3 %copy-start.5 = (bf16[1,2048,768]{2,1,0:T(8,128)(2,1)S(1)}, bf16[1,2048,768]{2,1,0:T(8,128)(2,1)}, u32[]{:S(2)}) copy-start(bf16[1,2048,768]{2,1,0:T(8,128)(2,1)} %param.15) | copy-start | bytes 9437188
  208.0 2.2 copy-start.10
  210.2 14.7 %copy-start.7 = (bf16[1,2048,768]{2,1,0:T(8,128)(2,1)S(1)}, bf16[1,2048,768]{2,1,0:T(8,128)(2,1)}, u32[]{:S(2)}) copy-start(bf16[1,2048,768]{2,1,0:T(8,128)(2,1)} %param.16) | copy-start | bytes 9437188
  278.1 5.7 %copy-start.3 = (bf16[128,2048]{1,0:T(8,128)(2,1)S(1)}, bf16[128,2048]{1,0:T(8,128)(2,1)}, u32[]{:S(2)}) copy-start(bf16[128,2048]{1,0:T(8,128)(2,1)} %param.10) | copy-start | bytes 1572868
  278.1 83.9 %all-to-all-start.3 = ((bf16[128,12,16,128]{3,2,1,0:T(8,128)(2,1)}), bf16[128,12,16,128]{3,2,1,0:T(8,128)(2,1)}, u32[]{:S(2)}, u32[]{:S(2)}) async-start(bf16[128,12,16,128]{3,2,1,0:T(8,128)(2,1)} %bitcast.79), calls=%async_computation.3 | async-start | bytes 12582912 | tf_op jit(solution)/shard_map/all_to_all | solution.py:84
  362.0 15.7 %copy-start.1 = (bf16[1,768,2048]{2,1,0:T(8,128)(2,1)S(1)}, bf16[1,768,2048]{2,1,0:T(8,128)(2,1)}, u32[]{:S(2)}) copy-start(bf16[1,768,2048]{2,1,0:T(8,128)(2,1)} %param.17) | copy-start | bytes 9437188

commit v2 on v1

--- a/solution.py
+++ b/solution.py
@@ -2,6 +2,8 @@
 import jax.numpy as jnp
 from jax import lax
 from jax.sharding import PartitionSpec as P
+from jax.experimental import pallas as pl
+from jax.experimental.pallas import tpu as pltpu
 
 LANES = 128
 
@@ -32,6 +34,28 @@
         grad_b, wu, (((1,), (1,)), ((), ())), preferred_element_type=jnp.float32
     )
     return pair_grad.astype(jnp.bfloat16)
+
+
+def combine_rows(place, rows, tok_rows, top_count):
+    def kernel(place_ref, rows_ref, out_ref):
+        def one_token(t, carry):
+            acc = rows_ref[place_ref[t * top_count]].astype(jnp.float32)
+            for k in range(1, top_count):
+                acc = acc + rows_ref[place_ref[t * top_count + k]].astype(jnp.float32)
+            out_ref[t] = acc.astype(out_ref.dtype)
+            return carry
+
+        lax.fori_loop(0, tok_rows, one_token, 0, unroll=4)
+
+    return pl.pallas_call(
+        kernel,
+        out_shape=jax.ShapeDtypeStruct((tok_rows,) + rows.shape[1:], jnp.bfloat16),
+        in_specs=[
+            pl.BlockSpec(memory_space=pltpu.SMEM),
+            pl.BlockSpec(memory_space=pltpu.VMEM),
+        ],
+        out_specs=pl.BlockSpec(memory_space=pltpu.VMEM),
+    )(place, rows)
 
 
 def body(tokens, cotangent, gates, experts, owner, swapped, w_gate, w_up, w_down):
@@ -89,15 +113,10 @@
         .reshape(tok_rows, top_count, sub, LANES)
         .astype(jnp.float32)
     )
-    grad_pairs = (
-        grad_back.reshape(-1, sub, LANES)[place]
-        .reshape(tok_rows, top_count, sub, LANES)
-        .astype(jnp.float32)
-    )
     mixed = jnp.sum(gates[:, :, None, None] * out_pairs, axis=1).astype(jnp.bfloat16)
     cot_f = cotangent.reshape(tok_rows, 1, sub, LANES).astype(jnp.float32)
     gate_grad = jnp.sum(cot_f * out_pairs, axis=(2, 3))
-    in_grad = jnp.sum(grad_pairs, axis=1).astype(jnp.bfloat16)
+    in_grad = combine_rows(place, grad_back.reshape(-1, sub, LANES), tok_rows, top_count)
     return (mixed.reshape(tok_rows, width), in_grad.reshape(tok_rows, width), gate_grad)
 
 

time: 379 us -> 370 us (0.976)
  local copies, waits for them, and re-layouts: 74.4 us -> 64.1 us
  Pallas kernels: 0 us -> 4.92 us
    gather x1 -> x0, local copies, waits for them, and re-layouts: 11.4 us -> none  [body(): grad_back.reshape(-1, sub, LANES)[place]]
    pallas_call x0 -> x1, Pallas kernels: none -> 4.92 us  [combine_rows(): pl.pallas_call(kernel, out_shape=jax.ShapeDtypeStruct((tok_rows,) + rows....]
    unnamed x32 -> x34, local copies, waits for them, and re-layouts: 18.9 us -> 19.9 us
  transfers between devices with their start and end apart: 4 -> 4, of which waited for: 4 -> 4; matrix products, arithmetic and copies ran while one was open for 30% -> 31% of each run, Pallas kernels for 0% -> 0%
where the time goes in v2:
time: 370 us; the launch traced here: 369 us
  waiting for transfers between devices  194 us (52%)
  local copies, waits for them, and re-layouts  64.1 us (17%)
  matrix products  58.1 us (16%)
  starting transfers between devices  28.1 us (8%)
  other arithmetic  19.1 us (5%)
  Pallas kernels  4.92 us (1%)
    all_to_all x1, waiting for transfers between devices, body(): lax.all_to_all(pair_grad.reshape(count, slots, sub, LANES), 'ep', split_a...  57.1 us
    all_to_all x1, waiting for transfers between devices, body(): lax.all_to_all(send_x, 'ep', split_axis=0, concat_axis=0, tiled=True)  52.7 us
    all_to_all x1, waiting for transfers between devices, body(): lax.all_to_all(send_c, 'ep', split_axis=0, concat_axis=0, tiled=True)  47.1 us
    all_to_all x1, waiting for transfers between devices, body(): lax.all_to_all(out_rows.reshape(count, slots, sub, LANES), 'ep', split_ax...  36.9 us
    unnamed x34, local copies, waits for them, and re-layouts  19.9 us
    dot_general x1, matrix products, project_back(): lax.dot_general(grad_a, wg, (((1,), (1,)), ((), ())), preferred_element_t...  14.7 us
    dot_general x1, matrix products, project_back(): lax.dot_general(grad_b, wu, (((1,), (1,)), ((), ())), preferred_element_t...  11.3 us
    gather x1, local copies, waits for them, and re-layouts, body(): back.reshape(-1, sub, LANES)[place].reshape(tok_rows, top_count, sub, LANES)  11.2 us
  transfers between devices with their start and end apart: 4, of which 4 were waited for; matrix products, arithmetic and copies ran while one was open for 31% of the time, Pallas kernels for 0%

profile of v2, /device:TPU:27, one launch (start us, length us, event | category | flops | bytes accessed | tf_op | source)
XLA Modules:
  0.0 368.9 jit_solution(15705481514111852462)
XLA Ops:
  0.6 0.9 broadcast_in_dim.51
  1.5 0.1 reshape.143
  1.7 0.8 select_reduce_fusion.1
  2.5 0.7 add.64
  3.2 0.8 copy.25
  4.1 0.4 select_reduce_fusion
  4.5 0.2 fusion.29
  4.7 0.8 copy-done.2
  5.6 1.1 broadcast_add_fusion
  6.6 0.1 copy.27
  6.8 0.4 fusion.28
  7.2 4.3 %scatter_custom_fusion = s32[1536]{0:T(1024)S(1)} fusion(s32[1024]{0:T(1024)S(1)} %bitcast.92, s32[1024]{0:T(1024)S(1)} %iota.18, s32[]{:T(128)} %constant.25.clone.1), kind=kCustom, calls=%fused_computation.68 | custom fusion | bytes 6148 | tf_op jit(solution)/shard_map/scatter | solution.py:88
  11.5 1.1 concatenate.9
  12.6 0.1 copy.30
  12.7 0.8 slice.18
  13.6 7.5 %gather_fusion = bf16[1536,16,128]{2,1,0:T(8,128)(2,1)} fusion(bf16[129,16,128]{2,1,0:T(8,128)(2,1)} %slice.18, s32[2048]{0:T(1024)S(1)} %get-tuple-element.12), kind=kCustom, calls=%fused_computation | custom fusion | bytes 12589056 | tf_op jit(solution)/shard_map/gather | solution.py:96
  21.0 10.9 %all-to-all-start = ((bf16[128,12,16,128]{3,2,1,0:T(8,128)(2,1)}), bf16[128,12,16,128]{3,2,1,0:T(8,128)(2,1)}, u32[]{:S(2)}, u32[]{:S(2)}) async-start(bf16[128,12,16,128]{3,2,1,0:T(8,128)(2,1)} %bitcast.79), calls=%async_computation | async-start | bytes 12582912 | tf_op jit(solution)/shard_map/all_to_all | solution.py:99
  32.2 8.4 %gather_fusion.3 = f32[1536]{0:T(1024)S(1)} fusion(f32[1025]{0:T(1024)S(1)} %pad_maximum_fusion, s32[2048]{0:T(1024)S(1)} %get-tuple-element.11), kind=kCustom, calls=%fused_computation.3 | custom fusion | bytes 18432 | tf_op jit(solution)/shard_map/gather | solution.py:97
  40.7 1.1 concatenate.10
  41.8 0.1 copy.34
  41.9 0.9 slice.19
  42.8 7.4 %gather_fusion.2 = bf16[1536,16,128]{2,1,0:T(8,128)(2,1)} fusion(bf16[129,16,128]{2,1,0:T(8,128)(2,1)} %slice.19, s32[2048]{0:T(1024)S(1)} %get-tuple-element.12), kind=kCustom, calls=%fused_computation.2 | custom fusion | bytes 12589056 | tf_op jit(solution)/shard_map/gather | solution.py:97
  50.2 7.3 %fusion = bf16[128,12,16,128]{3,2,1,0:T(8,128)(2,1)} fusion(bf16[128,12,16,128]{3,2,1,0:T(8,128)(2,1)} %bitcast.80, f32[128,12]{1,0:T(8,128)S(1)} %mul.92), kind=kLoop, calls=%fused_computation.6 | loop fusion | flops 9437184 | bytes 12589056 | tf_op jit(solution)/shard_map/convert_element_type | solution.py:97
  57.6 52.7 %all-to-all-done = bf16[128,12,16,128]{3,2,1,0:T(8,128)(2,1)} async-done(((bf16[128,12,16,128]{3,2,1,0:T(8,128)(2,1)}), bf16[128,12,16,128]{3,2,1,0:T(8,128)(2,1)}, u32[]{:S(2)}, u32[]{:S(2)}) %all-to-all-start) | async-done | bytes 6291488 | tf_op jit(solution)/shard_map/all_to_all | solution.py:99
  110.2 5.8 %all-to-all-start.2 = ((bf16[128,12,16,128]{3,2,1,0:T(8,128)(2,1)}), bf16[128,12,16,128]{3,2,1,0:T(8,128)(2,1)}, u32[]{:S(2)}, u32[]{:S(2)}) async-start(bf16[128,12,16,128]{3,2,1,0:T(8,128)(2,1)} %fusion), calls=%async_computation.2 | async-start | bytes 12582912 | tf_op jit(solution)/shard_map/all_to_all | solution.py:100
  116.0 9.0 %fusion.8 = f32[1536,768]{1,0:T(8,128)S(1)} fusion(bf16[192,8,16,128]{3,2,1,0:T(8,128)(2,1)} %bitcast.21, bf16[1,2048,768]{2,1,0:T(8,128)(2,1)} %param.15), kind=kOutput, calls=%fused_computation.18 | convolution fusion | flops 4831838208 | bytes 14155776 | tf_op jit(solution)/shard_map/dot_general | solution.py:12
  125.1 9.6 %fusion.6 = f32[1536,768]{1,0:T(8,128)S(1)} fusion(bf16[192,8,16,128]{3,2,1,0:T(8,128)(2,1)} %bitcast.21, bf16[1,2048,768]{2,1,0:T(8,128)(2,1)S(1)} %copy-done.7), kind=kOutput, calls=%fused_computation.16 | convolution fusion | flops 4831838208 | bytes 14155776 | tf_op jit(solution)/shard_map/dot_general | solution.py:13
  134.7 2.1 copy-done.10
  136.8 5.4 %fusion.22 = bf16[192,8,16,128]{3,1,2,0:T(8,128)(2,1)S(1)} fusion(bf16[1,768,2048]{2,1,0:T(8,128)(2,1)S(1)} %copy-done, f32[1536,768]{1,0:T(8,128)S(1)} %fusion.6, f32[1536,768]{1,0:T(8,128)S(1)} %fusion.8), kind=kOutput, calls=%fused_computation.34 | convolution fusion | flops 4842061824 | bytes 18874368 | tf_op jit(solution)/shard_map/dot_general | solution.py:20
  142.2 4.9 %copy.32 = bf16[192,8,16,128]{3,2,1,0:T(8,128)(2,1)} copy(bf16[192,8,16,128]{3,1,2,0:T(8,128)(2,1)S(1)} %fusion.22) | data formatting | bytes 12582912
  147.1 47.1 %all-to-all-done.2 = bf16[128,12,16,128]{3,2,1,0:T(8,128)(2,1)} async-done(((bf16[128,12,16,128]{3,2,1,0:T(8,128)(2,1)}), bf16[128,12,16,128]{3,2,1,0:T(8,128)(2,1)}, u32[]{:S(2)}, u32[]{:S(2)}) %all-to-all-start.2) | async-done | bytes 6291488 | tf_op jit(solution)/shard_map/all_to_all | solution.py:100
  194.2 5.7 %all-to-all-start.1 = ((bf16[128,12,16,128]{3,2,1,0:T(8,128)(2,1)}), bf16[128,12,16,128]{3,2,1,0:T(8,128)(2,1)}, u32[]{:S(2)}, u32[]{:S(2)}) async-start(bf16[128,12,16,128]{3,2,1,0:T(8,128)(2,1)} %bitcast.78), calls=%async_computation.1 | async-start | bytes 12582912 | tf_op jit(solution)/shard_map/all_to_all | solution.py:104
  199.9 8.1 %fusion.3 = f32[1536,768]{1,0:T(8,128)S(1)} fusion(bf16[192,8,16,128]{3,2,1,0:T(8,128)(2,1)} %bitcast.32, bf16[1,768,2048]{2,1,0:T(8,128)(2,1)S(1)} %copy-done), kind=kOutput, calls=%fused_computation.13 | convolution fusion | flops 4831838208 | bytes 14155776 | tf_op jit(solution)/shard_map/dot_general | solution.py:25
  208.1 2.2 copy-done.11
  210.2 14.7 %fusion.16 = f32[1536,2048]{1,0:T(8,128)} fusion(bf16[1,2048,768]{2,1,0:T(8,128)(2,1)S(1)} %copy-done.6, f32[1536,768]{1,0:T(8,128)} %copy-done.9, f32[1536,768]{1,0:T(8,128)S(1)} %fusion.3, f32[1536,768]{1,0:T(8,128)} %copy-done.10), kind=kOutput, calls=%fused_computation.30 | convolution fusion | flops 4843634688 | bytes 29884416 | tf_op jit(solution)/shard_map/dot_general | solution.py:30
  224.9 11.3 %fusion.19 = bf16[192,8,16,128]{3,1,2,0:T(8,128)(2,1)S(1)} fusion(f32[1536,2048]{1,0:T(8,128)} %fusion.16, bf16[1,2048,768]{2,1,0:T(8,128)(2,1)S(1)} %copy-done.8, f32[1536,768]{1,0:T(8,128)} %copy-done.11, f32[1536,768]{1,0:T(8,128)} %copy-done.9), kind=kOutput, calls=%fused_computation.33 | convolution fusion | flops 4845207552 | bytes 31457280 | tf_op jit(solution)/shard_map/dot_general | solution.py:33
  236.2 5.0 %copy.36 = bf16[192,8,16,128]{3,2,1,0:T(8,128)(2,1)} copy(bf16[192,8,16,128]{3,1,2,0:T(8,128)(2,1)S(1)} %fusion.19) | data formatting | bytes 12582912
  241.2 36.9 %all-to-all-done.1 = bf16[128,12,16,128]{3,2,1,0:T(8,128)(2,1)} async-done(((bf16[128,12,16,128]{3,2,1,0:T(8,128)(2,1)}), bf16[128,12,16,128]{3,2,1,0:T(8,128)(2,1)}, u32[]{:S(2)}, u32[]{:S(2)}) %all-to-all-start.1) | async-done | bytes 6291488 | tf_op jit(solution)/shard_map/all_to_all | solution.py:104
  278.1 5.7 %all-to-all-start.3 = ((bf16[128,12,16,128]{3,2,1,0:T(8,128)(2,1)}), bf16[128,12,16,128]{3,2,1,0:T(8,128)(2,1)}, u32[]{:S(2)}, u32[]{:S(2)}) async-start(bf16[128,12,16,128]{3,2,1,0:T(8,128)(2,1)} %bitcast.77), calls=%async_computation.3 | async-start | bytes 12582912 | tf_op jit(solution)/shard_map/all_to_all | solution.py:108
  283.9 0.2 copy.38
  284.1 11.2 %gather_fusion.1 = bf16[1024,16,128]{2,1,0:T(8,128)(2,1)} fusion(bf16[1536,16,128]{2,1,0:T(8,128)(2,1)} %bitcast.10, s32[1024]{0:T(1024)S(1)} %broadcast_clamp_fusion), kind=kCustom, calls=%fused_computation.1 | custom fusion | bytes 8392704 | tf_op jit(solution)/shard_map/gather | solution.py:112
  295.3 4.6 %fusion.2 = f32[128,8]{1,0:T(8,128)S(1)} fusion(bf16[128,8,16,128]{3,2,1,0:T(8,128)(2,1)} %bitcast.76, f32[128,16,128]{2,1,0:T(8,128)S(1)} %bitcast.81), kind=kLoop, calls=%fused_computation.11 | loop fusion | flops 6290432 | bytes 5246976 | tf_op jit(solution)/shard_map/reduce_sum | solution.py:118
  299.9 0.7 copy.29
  300.5 3.5 fusion.1
  304.0 0.9 copy.54
  305.0 57.1 %all-to-all-done.3 = bf16[128,12,16,128]{3,2,1,0:T(8,128)(2,1)} async-done(((bf16[128,12,16,128]{3,2,1,0:T(8,128)(2,1)}), bf16[128,12,16,128]{3,2,1,0:T(8,128)(2,1)}, u32[]{:S(2)}, u32[]{:S(2)}) %all-to-all-start.3) | async-done | bytes 6291488 | tf_op jit(solution)/shard_map/all_to_all | solution.py:108
  362.0 4.9 %shard_map.112 = bf16[128,16,128]{2,1,0:T(8,128)(2,1)} custom-call(s32[1024]{0:T(1024)} %copy-done.4, bf16[1536,16,128]{2,1,0:T(8,128)(2,1)} %bitcast.13.rows_ref), custom_call_target="tpu_custom_call" | custom-call | tf_op jit(solution)/shard_map/pallas_call | solution.py:50
  366.9 2.0 copy.53
  (38 shorter events, 0.7 us)
Async XLA Ops:
  0.6 136.2 %copy-start = (bf16[1,768,2048]{2,1,0:T(8,128)(2,1)S(1)}, bf16[1,768,2048]{2,1,0:T(8,128)(2,1)}, u32[]{:S(2)}) copy-start(bf16[1,768,2048]{2,1,0:T(8,128)(2,1)} %param.17) | copy-start | bytes 9437188
  4.7 0.8 copy-start.2
  7.1 13.9 %copy-start.4 = (s32[1024]{0:T(1024)}, s32[1024]{0:T(1024)S(1)}, u32[]{:S(2)}) copy-start(s32[1024]{0:T(1024)S(1)} %add_add_fusion.place_ref) | copy-start | bytes 12292
  21.0 11.0 %copy-start.5 = (f32[128,8]{0,1:T(8,128)S(1)}, f32[128,8]{0,1:T(8,128)}, u32[]{:S(2)}) copy-start(f32[128,8]{0,1:T(8,128)} %param.11) | copy-start | bytes 12292
  21.0 89.2 %all-to-all-start = ((bf16[128,12,16,128]{3,2,1,0:T(8,128)(2,1)}), bf16[128,12,16,128]{3,2,1,0:T(8,128)(2,1)}, u32[]{:S(2)}, u32[]{:S(2)}) async-start(bf16[128,12,16,128]{3,2,1,0:T(8,128)(2,1)} %bitcast.79), calls=%async_computation | async-start | bytes 12582912 | tf_op jit(solution)/shard_map/all_to_all | solution.py:99
  110.2 84.0 %all-to-all-start.2 = ((bf16[128,12,16,128]{3,2,1,0:T(8,128)(2,1)}), bf16[128,12,16,128]{3,2,1,0:T(8,128)(2,1)}, u32[]{:S(2)}, u32[]{:S(2)}) async-start(bf16[128,12,16,128]{3,2,1,0:T(8,128)(2,1)} %fusion), calls=%async_computation.2 | async-start | bytes 12582912 | tf_op jit(solution)/shard_map/all_to_all | solution.py:100
  116.0 9.1 %copy-start.7 = (bf16[1,2048,768]{2,1,0:T(8,128)(2,1)S(1)}, bf16[1,2048,768]{2,1,0:T(8,128)(2,1)}, u32[]{:S(2)}) copy-start(bf16[1,2048,768]{2,1,0:T(8,128)(2,1)} %param.16) | copy-start | bytes 9437188
  125.1 9.6 %copy-start.9 = (f32[1536,768]{1,0:T(8,128)}, f32[1536,768]{1,0:T(8,128)S(1)}, u32[]{:S(2)}) copy-start(f32[1536,768]{1,0:T(8,128)S(1)} %fusion.8) | copy-start | bytes 14155780
  134.7 2.1 copy-start.10
  194.2 83.9 %all-to-all-start.1 = ((bf16[128,12,16,128]{3,2,1,0:T(8,128)(2,1)}), bf16[128,12,16,128]{3,2,1,0:T(8,128)(2,1)}, u32[]{:S(2)}, u32[]{:S(2)}) async-start(bf16[128,12,16,128]{3,2,1,0:T(8,128)(2,1)} %bitcast.78), calls=%async_computation.1 | async-start | bytes 12582912 | tf_op jit(solution)/shard_map/all_to_all | solution.py:104
  199.9 10.3 %copy-start.6 = (bf16[1,2048,768]{2,1,0:T(8,128)(2,1)S(1)}, bf16[1,2048,768]{2,1,0:T(8,128)(2,1)}, u32[]{:S(2)}) copy-start(bf16[1,2048,768]{2,1,0:T(8,128)(2,1)} %param.15) | copy-start | bytes 9437188
  208.1 2.2 copy-start.11
  210.2 14.7 %copy-start.8 = (bf16[1,2048,768]{2,1,0:T(8,128)(2,1)S(1)}, bf16[1,2048,768]{2,1,0:T(8,128)(2,1)}, u32[]{:S(2)}) copy-start(bf16[1,2048,768]{2,1,0:T(8,128)(2,1)} %param.16) | copy-start | bytes 9437188
  278.1 5.7 %copy-start.3 = (bf16[128,2048]{1,0:T(8,128)(2,1)S(1)}, bf16[128,2048]{1,0:T(8,128)(2,1)}, u32[]{:S(2)}) copy-start(bf16[128,2048]{1,0:T(8,128)(2,1)} %param.10) | copy-start | bytes 1572868
  278.1 83.9 %all-to-all-start.3 = ((bf16[128,12,16,128]{3,2,1,0:T(8,128)(2,1)}), bf16[128,12,16,128]{3,2,1,0:T(8,128)(2,1)}, u32[]{:S(2)}, u32[]{:S(2)}) async-start(bf16[128,12,16,128]{3,2,1,0:T(8,128)(2,1)} %bitcast.77), calls=%async_computation.3 | async-start | bytes 12582912 | tf_op jit(solution)/shard_map/all_to_all | solution.py:108
  300.5 68.4 %copy-start.1 = (bf16[1,768,2048]{2,1,0:T(8,128)(2,1)S(1)}, bf16[1,768,2048]{2,1,0:T(8,128)(2,1)}, u32[]{:S(2)}) copy-start(bf16[1,768,2048]{2,1,0:T(8,128)(2,1)} %param.17) | copy-start | bytes 9437188

commit v3 on v2

--- a/solution.py
+++ b/solution.py
@@ -58,43 +58,94 @@
     )(place, rows)
 
 
+def dispatch_rows(flat_e, owner, swapped, tok3, slots, count, top_count):
+    pairs = flat_e.shape[0]
+    total = count * slots
+
+    def kernel(e_ref, own_ref, sw_ref, tok_ref, place_ref, out_ref, cnt_ref):
+        def clear_count(d, carry):
+            cnt_ref[d] = 0
+            return carry
+
+        lax.fori_loop(0, count, clear_count, 0)
+
+        def clear_row(i, carry):
+            out_ref[i] = jnp.zeros(out_ref.shape[1:], out_ref.dtype)
+            return carry
+
+        lax.fori_loop(0, total, clear_row, 0, unroll=8)
+
+        def one_pair(p, carry):
+            planned = own_ref[e_ref[p]]
+            flip = sw_ref[planned // 2] * (1 - 2 * (planned % 2))
+            tgt = planned + flip
+            rank = cnt_ref[tgt]
+            cnt_ref[tgt] = rank + 1
+            spot = jnp.minimum(tgt * slots + rank, total - 1)
+            place_ref[p] = spot
+            out_ref[spot] = tok_ref[p // top_count]
+            return carry
+
+        lax.fori_loop(0, pairs, one_pair, 0, unroll=4)
+
+    smem = pl.BlockSpec(memory_space=pltpu.SMEM)
+    vmem = pl.BlockSpec(memory_space=pltpu.VMEM)
+    return pl.pallas_call(
+        kernel,
+        out_shape=(
+            jax.ShapeDtypeStruct((pairs,), jnp.int32),
+            jax.ShapeDtypeStruct((total,) + tok3.shape[1:], tok3.dtype),
+        ),
+        in_specs=[smem, smem, smem, vmem],
+        out_specs=(smem, vmem),
+        scratch_shapes=[pltpu.SMEM((count,), jnp.int32)],
+    )(flat_e, owner, swapped, tok3)
+
+
+def dispatch_cots(place, gate_flat, cot3, total, top_count):
+    pairs = place.shape[0]
+
+    def kernel(place_ref, gate_ref, cot_ref, out_ref):
+        def clear_row(i, carry):
+            out_ref[i] = jnp.zeros(out_ref.shape[1:], out_ref.dtype)
+            return carry
+
+        lax.fori_loop(0, total, clear_row, 0, unroll=8)
+
+        def one_pair(p, carry):
+            row = cot_ref[p // top_count].astype(jnp.float32) * gate_ref[p]
+            out_ref[place_ref[p]] = row.astype(out_ref.dtype)
+            return carry
+
+        lax.fori_loop(0, pairs, one_pair, 0, unroll=4)
+
+    smem = pl.BlockSpec(memory_space=pltpu.SMEM)
+    vmem = pl.BlockSpec(memory_space=pltpu.VMEM)
+    return pl.pallas_call(
+        kernel,
+        out_shape=jax.ShapeDtypeStruct((total,) + cot3.shape[1:], cot3.dtype),
+        in_specs=[smem, smem, vmem],
+        out_specs=vmem,
+    )(place, gate_flat, cot3)
+
+
 def body(tokens, cotangent, gates, experts, owner, swapped, w_gate, w_up, w_down):
     tok_rows, width = tokens.shape
     top_count = experts.shape[1]
     expert_total = owner.shape[0]
     count = lax.axis_size("ep")
     slots = tok_rows * top_count * 3 // (2 * expert_total)
-    pairs = tok_rows * top_count
     sub = width // LANES
-    devices = jnp.arange(count, dtype=jnp.int32)
-    dev_flag = jnp.repeat(swapped, 2)
-    step_dev = dev_flag * (1 - 2 * (devices % 2))
-    holder = owner + jnp.sum(
-        jnp.where(owner[:, None] == devices[None, :], step_dev[None, :], 0), axis=1
-    )
     wg = w_gate[0]
     wu = w_up[0]
     wd = w_down[0]
-    flat_e = experts.reshape(-1)
-    chosen = flat_e[:, None] == jnp.arange(expert_total, dtype=jnp.int32)[None, :]
-    target = jnp.sum(jnp.where(chosen, holder[None, :], 0), axis=1)
-    hot = target[:, None] == devices[None, :]
-    running = jnp.cumsum(hot.astype(jnp.int32), axis=0)
-    rank = jnp.sum(jnp.where(hot, running, 0), axis=1) - 1
-    place = target * slots + rank
-    source = (
-        jnp.full((count * slots,), pairs, jnp.int32)
-        .at[place]
-        .set(jnp.arange(pairs, dtype=jnp.int32))
+    tok3 = tokens.reshape(tok_rows, sub, LANES)
+    cot3 = cotangent.reshape(tok_rows, sub, LANES)
+    place, send_x = dispatch_rows(
+        experts.reshape(-1), owner, swapped, tok3, slots, count, top_count
     )
-    row_of = source // top_count
-    tok_pad = jnp.concatenate([tokens, jnp.zeros((1, width), jnp.bfloat16)], axis=0)
-    cot_pad = jnp.concatenate([cotangent, jnp.zeros((1, width), jnp.bfloat16)], axis=0)
-    gate_pad = jnp.concatenate([gates.reshape(-1), jnp.zeros((1,), jnp.float32)], axis=0)
-    tok3 = tok_pad.reshape(tok_rows + 1, sub, LANES)
-    cot3 = cot_pad.reshape(tok_rows + 1, sub, LANES)
-    send_x = tok3[row_of].reshape(count, slots, sub, LANES)
-    send_c = (cot3[row_of].astype(jnp.float32) * gate_pad[source][:, None, None]).astype(jnp.bfloat16)
+    send_c = dispatch_cots(place, gates.reshape(-1), cot3, count * slots, top_count)
+    send_x = send_x.reshape(count, slots, sub, LANES)
     send_c = send_c.reshape(count, slots, sub, LANES)
     recv_x = lax.all_to_all(send_x, "ep", split_axis=0, concat_axis=0, tiled=True)
     recv_c = lax.all_to_all(send_c, "ep", split_axis=0, concat_axis=0, tiled=True)
@@ -114,7 +165,7 @@
         .astype(jnp.float32)
     )
     mixed = jnp.sum(gates[:, :, None, None] * out_pairs, axis=1).astype(jnp.bfloat16)
-    cot_f = cotangent.reshape(tok_rows, 1, sub, LANES).astype(jnp.float32)
+    cot_f = cot3.reshape(tok_rows, 1, sub, LANES).astype(jnp.float32)
     gate_grad = jnp.sum(cot_f * out_pairs, axis=(2, 3))
     in_grad = combine_rows(place, grad_back.reshape(-1, sub, LANES), tok_rows, top_count)
     return (mixed.reshape(tok_rows, width), in_grad.reshape(tok_rows, width), gate_grad)

time: 370 us -> 375 us (1.014)
  Pallas kernels: 4.92 us -> 39.2 us
  local copies, waits for them, and re-layouts: 64.1 us -> 34.8 us
  other arithmetic: 19.1 us -> 8.96 us
  waiting for transfers between devices: 194 us -> 204 us
    pallas_call x0 -> x2, Pallas kernels: none -> 34.3 us  [the longest x1 21.8 us: dispatch_rows(): pl.pallas_call(kernel, out_shape=(jax.ShapeDtypeStruct((pairs,), jnp.int3...]
    gather x3 -> x0, local copies, waits for them, and re-layouts: 23.3 us -> none  [the longest x1 8.39 us: body(): gate_pad[source][:, None, None]]
    all_to_all x1, waiting for transfers between devices: 52.7 us -> 63 us  [body(): lax.all_to_all(send_x, 'ep', split_axis=0, concat_axis=0, tiled=True)]
    convert_element_type x1, other arithmetic: 7.33 us -> 0.11 us  [body(): cot_f = cot3.reshape(tok_rows, 1, sub, LANES).astype(jnp.float32)]
    scatter x1 -> x0, local copies, waits for them, and re-layouts: 4.32 us -> none  [body(): source = jnp.full((count * slots,), pairs, jnp.int32).at[place].set(jnp.a...]
    unnamed x34 -> x29, local copies, waits for them, and re-layouts: 19.9 us -> 19.8 us
  transfers between devices with their start and end apart: 4 -> 4, of which waited for: 4 -> 4; matrix products, arithmetic and copies ran while one was open for 31% -> 24% of each run, Pallas kernels for 0% -> 3%
where the time goes in v3:
time: 375 us; the launch traced here: 374 us
  waiting for transfers between devices  204 us (54%)
  matrix products  58.1 us (15%)
  Pallas kernels  39.2 us (10%)
  local copies, waits for them, and re-layouts  34.8 us (9%)
  starting transfers between devices  28.2 us (8%)
  other arithmetic  8.96 us (2%)
    all_to_all x1, waiting for transfers between devices, body(): lax.all_to_all(send_x, 'ep', split_axis=0, concat_axis=0, tiled=True)  63 us
    all_to_all x1, waiting for transfers between devices, body(): lax.all_to_all(pair_grad.reshape(count, slots, sub, LANES), 'ep', split_a...  57.4 us
    all_to_all x1, waiting for transfers between devices, body(): lax.all_to_all(send_c, 'ep', split_axis=0, concat_axis=0, tiled=True)  47.1 us
    all_to_all x1, waiting for transfers between devices, body(): lax.all_to_all(out_rows.reshape(count, slots, sub, LANES), 'ep', split_ax...  36.9 us
    pallas_call x1, Pallas kernels, dispatch_rows(): pl.pallas_call(kernel, out_shape=(jax.ShapeDtypeStruct((pairs,), jnp.int3...  21.8 us
    unnamed x29, local copies, waits for them, and re-layouts  19.8 us
    dot_general x1, matrix products, project_back(): lax.dot_general(grad_a, wg, (((1,), (1,)), ((), ())), preferred_element_t...  14.7 us
    pallas_call x1, Pallas kernels, dispatch_cots(): pl.pallas_call(kernel, out_shape=jax.ShapeDtypeStruct((total,) + cot3.sha...  12.5 us
  transfers between devices with their start and end apart: 4, of which 4 were waited for; matrix products, arithmetic and copies ran while one was open for 24% of the time, Pallas kernels for 3%

profile of v3, /device:TPU:27, one launch (start us, length us, event | category | flops | bytes accessed | tf_op | source)
XLA Modules:
  0.0 374.5 jit_solution(15617710650437231201)
XLA Ops:
  0.6 0.0 copy-start
  0.6 0.9 copy.17
  1.6 0.7 reshape.69.e_ref
  2.3 1.9 copy.20
  4.2 21.8 %shard_map.112 = (s32[1024]{0:T(1024)}, bf16[1536,16,128]{2,1,0:T(8,128)(2,1)}) custom-call(s32[1024]{0:T(1024)} %reshape.69.e_ref, s32[128]{0:T(128)} %own_ref.1, s32[64]{0:T(128)} %sw_ref.1, bf16[128,16,128]{2,1,0:T(8,128)(2,1)} %bitcast.65), custom_call_target="tpu_custom_call" | custom-call | tf_op jit(solution)/shard_map/pallas_call | solution.py:93
  26.0 0.0 copy-start.4
  26.0 11.0 %all-to-all-start = ((bf16[128,12,16,128]{3,2,1,0:T(8,128)(2,1)}), bf16[128,12,16,128]{3,2,1,0:T(8,128)(2,1)}, u32[]{:S(2)}, u32[]{:S(2)}) async-start(bf16[128,12,16,128]{3,2,1,0:T(8,128)(2,1)} %bitcast.61), calls=%async_computation | async-start | bytes 12582912 | tf_op jit(solution)/shard_map/all_to_all | solution.py:150
  37.0 0.0 copy-done.4
  37.0 0.1 copy.16
  37.1 0.7 reshape.75.gate_ref
  37.8 1.9 copy.24
  39.7 12.5 %shard_map.113 = bf16[1536,16,128]{2,1,0:T(8,128)(2,1)} custom-call(s32[1024]{0:T(1024)} %get-tuple-element.6.place_ref, f32[1024]{0:T(1024)} %reshape.75.gate_ref, bf16[128,16,128]{2,1,0:T(8,128)(2,1)} %bitcast.62), custom_call_target="tpu_custom_call" | custom-call | tf_op jit(solution)/shard_map/pallas_call | solution.py:124
  52.2 63.0 %all-to-all-done = bf16[128,12,16,128]{3,2,1,0:T(8,128)(2,1)} async-done(((bf16[128,12,16,128]{3,2,1,0:T(8,128)(2,1)}), bf16[128,12,16,128]{3,2,1,0:T(8,128)(2,1)}, u32[]{:S(2)}, u32[]{:S(2)}) %all-to-all-start) | async-done | bytes 6291488 | tf_op jit(solution)/shard_map/all_to_all | solution.py:150
  115.2 5.8 %all-to-all-start.2 = ((bf16[128,12,16,128]{3,2,1,0:T(8,128)(2,1)}), bf16[128,12,16,128]{3,2,1,0:T(8,128)(2,1)}, u32[]{:S(2)}, u32[]{:S(2)}) async-start(bf16[128,12,16,128]{3,2,1,0:T(8,128)(2,1)} %bitcast.60), calls=%async_computation.2 | async-start | bytes 12582912 | tf_op jit(solution)/shard_map/all_to_all | solution.py:151
  121.0 0.0 copy-start.6
  121.0 9.0 %fusion.7 = f32[1536,768]{1,0:T(8,128)S(1)} fusion(bf16[192,8,16,128]{3,2,1,0:T(8,128)(2,1)} %bitcast.12, bf16[1,2048,768]{2,1,0:T(8,128)(2,1)} %param.15), kind=kOutput, calls=%fused_computation.12 | convolution fusion | flops 4831838208 | bytes 14155776 | tf_op jit(solution)/shard_map/dot_general | solution.py:12
  130.1 0.0 copy-done.6
  130.1 0.0 copy-start.8
  130.1 9.6 %fusion.5 = f32[1536,768]{1,0:T(8,128)S(1)} fusion(bf16[192,8,16,128]{3,2,1,0:T(8,128)(2,1)} %bitcast.12, bf16[1,2048,768]{2,1,0:T(8,128)(2,1)S(1)} %copy-done.6), kind=kOutput, calls=%fused_computation.10 | convolution fusion | flops 4831838208 | bytes 14155776 | tf_op jit(solution)/shard_map/dot_general | solution.py:13
  139.7 0.0 copy-done.8
  139.7 0.0 copy-start.9
  139.7 2.1 copy-done.9
  141.8 0.0 copy-done
  141.8 5.4 %fusion.21 = bf16[192,8,16,128]{3,1,2,0:T(8,128)(2,1)S(1)} fusion(bf16[1,768,2048]{2,1,0:T(8,128)(2,1)S(1)} %copy-done, f32[1536,768]{1,0:T(8,128)S(1)} %fusion.5, f32[1536,768]{1,0:T(8,128)S(1)} %fusion.7), kind=kOutput, calls=%fused_computation.28 | convolution fusion | flops 4842061824 | bytes 18874368 | tf_op jit(solution)/shard_map/dot_general | solution.py:20
  147.2 4.9 %copy.22 = bf16[192,8,16,128]{3,2,1,0:T(8,128)(2,1)} copy(bf16[192,8,16,128]{3,1,2,0:T(8,128)(2,1)S(1)} %fusion.21) | data formatting | bytes 12582912
  152.1 47.1 %all-to-all-done.2 = bf16[128,12,16,128]{3,2,1,0:T(8,128)(2,1)} async-done(((bf16[128,12,16,128]{3,2,1,0:T(8,128)(2,1)}), bf16[128,12,16,128]{3,2,1,0:T(8,128)(2,1)}, u32[]{:S(2)}, u32[]{:S(2)}) %all-to-all-start.2) | async-done | bytes 6291488 | tf_op jit(solution)/shard_map/all_to_all | solution.py:151
  199.2 5.8 %all-to-all-start.1 = ((bf16[128,12,16,128]{3,2,1,0:T(8,128)(2,1)}), bf16[128,12,16,128]{3,2,1,0:T(8,128)(2,1)}, u32[]{:S(2)}, u32[]{:S(2)}) async-start(bf16[128,12,16,128]{3,2,1,0:T(8,128)(2,1)} %bitcast.59), calls=%async_computation.1 | async-start | bytes 12582912 | tf_op jit(solution)/shard_map/all_to_all | solution.py:155
  205.0 0.0 copy-start.5
  205.0 8.1 %fusion.2 = f32[1536,768]{1,0:T(8,128)S(1)} fusion(bf16[192,8,16,128]{3,2,1,0:T(8,128)(2,1)} %bitcast.22, bf16[1,768,2048]{2,1,0:T(8,128)(2,1)S(1)} %copy-done), kind=kOutput, calls=%fused_computation.7 | convolution fusion | flops 4831838208 | bytes 14155776 | tf_op jit(solution)/shard_map/dot_general | solution.py:25
  213.2 0.0 copy-start.10
  213.2 2.2 copy-done.10
  215.3 0.0 copy-done.5
  215.3 14.7 %fusion.15 = f32[1536,2048]{1,0:T(8,128)} fusion(bf16[1,2048,768]{2,1,0:T(8,128)(2,1)S(1)} %copy-done.5, f32[1536,768]{1,0:T(8,128)} %copy-done.8, f32[1536,768]{1,0:T(8,128)S(1)} %fusion.2, f32[1536,768]{1,0:T(8,128)} %copy-done.9), kind=kOutput, calls=%fused_computation.24 | convolution fusion | flops 4843634688 | bytes 29884416 | tf_op jit(solution)/shard_map/dot_general | solution.py:30
  230.0 0.0 copy-done.7
  230.0 11.3 %fusion.18 = bf16[192,8,16,128]{3,1,2,0:T(8,128)(2,1)S(1)} fusion(f32[1536,2048]{1,0:T(8,128)} %fusion.15, bf16[1,2048,768]{2,1,0:T(8,128)(2,1)S(1)} %copy-done.7, f32[1536,768]{1,0:T(8,128)} %copy-done.10, f32[1536,768]{1,0:T(8,128)} %copy-done.8), kind=kOutput, calls=%fused_computation.27 | convolution fusion | flops 4845207552 | bytes 31457280 | tf_op jit(solution)/shard_map/dot_general | solution.py:33
  241.3 5.0 %copy.26 = bf16[192,8,16,128]{3,2,1,0:T(8,128)(2,1)} copy(bf16[192,8,16,128]{3,1,2,0:T(8,128)(2,1)S(1)} %fusion.18) | data formatting | bytes 12582912
  246.3 36.9 %all-to-all-done.1 = bf16[128,12,16,128]{3,2,1,0:T(8,128)(2,1)} async-done(((bf16[128,12,16,128]{3,2,1,0:T(8,128)(2,1)}), bf16[128,12,16,128]{3,2,1,0:T(8,128)(2,1)}, u32[]{:S(2)}, u32[]{:S(2)}) %all-to-all-start.1) | async-done | bytes 6291488 | tf_op jit(solution)/shard_map/all_to_all | solution.py:155
  283.2 5.7 %all-to-all-start.3 = ((bf16[128,12,16,128]{3,2,1,0:T(8,128)(2,1)}), bf16[128,12,16,128]{3,2,1,0:T(8,128)(2,1)}, u32[]{:S(2)}, u32[]{:S(2)}) async-start(bf16[128,12,16,128]{3,2,1,0:T(8,128)(2,1)} %bitcast.58), calls=%async_computation.3 | async-start | bytes 12582912 | tf_op jit(solution)/shard_map/all_to_all | solution.py:159
  288.9 0.0 copy-done.3
  288.9 0.0 copy-done.2
  289.0 0.1 bitcast_convert_fusion
  289.1 11.2 %gather_fusion = bf16[1024,16,128]{2,1,0:T(8,128)(2,1)} fusion(bf16[1536,16,128]{2,1,0:T(8,128)(2,1)} %bitcast.4, s32[1024]{0:T(1024)S(1)} %fusion.27), kind=kCustom, calls=%fused_computation | custom fusion | bytes 8392704 | tf_op jit(solution)/shard_map/gather | solution.py:163
  300.2 4.6 %fusion.1 = f32[128,8]{1,0:T(8,128)S(1)} fusion(bf16[128,8,16,128]{3,2,1,0:T(8,128)(2,1)} %bitcast.57, f32[128,16,128]{2,1,0:T(8,128)S(1)} %bitcast_convert_fusion), kind=kLoop, calls=%fused_computation.5 | loop fusion | flops 6290432 | bytes 5246976 | tf_op jit(solution)/shard_map/reduce_sum | solution.py:169
  304.8 0.7 copy.19
  305.5 4.3 %fusion = bf16[128,16,128]{2,1,0:T(8,128)(2,1)} fusion(f32[128,8]{1,0:T(8,128)S(1)} %copy.16, bf16[1024,16,128]{2,1,0:T(8,128)(2,1)} %gather_fusion), kind=kLoop, calls=%fused_computation.4 | loop fusion | flops 6029312 | bytes 4722688 | tf_op jit(solution)/shard_map/reduce_sum | solution.py:167
  309.8 57.4 %all-to-all-done.3 = bf16[128,12,16,128]{3,2,1,0:T(8,128)(2,1)} async-done(((bf16[128,12,16,128]{3,2,1,0:T(8,128)(2,1)}), bf16[128,12,16,128]{3,2,1,0:T(8,128)(2,1)}, u32[]{:S(2)}, u32[]{:S(2)}) %all-to-all-start.3) | async-done | bytes 6291488 | tf_op jit(solution)/shard_map/all_to_all | solution.py:159
  367.1 4.9 %shard_map.114 = bf16[128,16,128]{2,1,0:T(8,128)(2,1)} custom-call(s32[1024]{0:T(1024)} %get-tuple-element.6.place_ref, bf16[1536,16,128]{2,1,0:T(8,128)(2,1)} %bitcast.7.rows_ref), custom_call_target="tpu_custom_call" | custom-call | tf_op jit(solution)/shard_map/pallas_call | solution.py:50
  372.1 2.4 copy_bitcast_fusion
  (6 shorter events, 0.0 us)
Async XLA Ops:
  0.6 141.2 %copy-start = (bf16[1,768,2048]{2,1,0:T(8,128)(2,1)S(1)}, bf16[1,768,2048]{2,1,0:T(8,128)(2,1)}, u32[]{:S(2)}) copy-start(bf16[1,768,2048]{2,1,0:T(8,128)(2,1)} %param.17) | copy-start | bytes 9437188
  26.0 11.0 %copy-start.4 = (f32[128,8]{0,1:T(8,128)S(1)}, f32[128,8]{0,1:T(8,128)}, u32[]{:S(2)}) copy-start(f32[128,8]{0,1:T(8,128)} %param.11) | copy-start | bytes 12292
  26.0 89.2 %all-to-all-start = ((bf16[128,12,16,128]{3,2,1,0:T(8,128)(2,1)}), bf16[128,12,16,128]{3,2,1,0:T(8,128)(2,1)}, u32[]{:S(2)}, u32[]{:S(2)}) async-start(bf16[128,12,16,128]{3,2,1,0:T(8,128)(2,1)} %bitcast.61), calls=%async_computation | async-start | bytes 12582912 | tf_op jit(solution)/shard_map/all_to_all | solution.py:150
  115.2 84.0 %all-to-all-start.2 = ((bf16[128,12,16,128]{3,2,1,0:T(8,128)(2,1)}), bf16[128,12,16,128]{3,2,1,0:T(8,128)(2,1)}, u32[]{:S(2)}, u32[]{:S(2)}) async-start(bf16[128,12,16,128]{3,2,1,0:T(8,128)(2,1)} %bitcast.60), calls=%async_computation.2 | async-start | bytes 12582912 | tf_op jit(solution)/shard_map/all_to_all | solution.py:151
  121.0 9.1 %copy-start.6 = (bf16[1,2048,768]{2,1,0:T(8,128)(2,1)S(1)}, bf16[1,2048,768]{2,1,0:T(8,128)(2,1)}, u32[]{:S(2)}) copy-start(bf16[1,2048,768]{2,1,0:T(8,128)(2,1)} %param.16) | copy-start | bytes 9437188
  130.1 9.6 %copy-start.8 = (f32[1536,768]{1,0:T(8,128)}, f32[1536,768]{1,0:T(8,128)S(1)}, u32[]{:S(2)}) copy-start(f32[1536,768]{1,0:T(8,128)S(1)} %fusion.7) | copy-start | bytes 14155780
  139.7 2.1 copy-start.9
  199.2 84.0 %all-to-all-start.1 = ((bf16[128,12,16,128]{3,2,1,0:T(8,128)(2,1)}), bf16[128,12,16,128]{3,2,1,0:T(8,128)(2,1)}, u32[]{:S(2)}, u32[]{:S(2)}) async-start(bf16[128,12,16,128]{3,2,1,0:T(8,128)(2,1)} %bitcast.59), calls=%async_computation.1 | async-start | bytes 12582912 | tf_op jit(solution)/shard_map/all_to_all | solution.py:155
  205.0 10.3 %copy-start.5 = (bf16[1,2048,768]{2,1,0:T(8,128)(2,1)S(1)}, bf16[1,2048,768]{2,1,0:T(8,128)(2,1)}, u32[]{:S(2)}) copy-start(bf16[1,2048,768]{2,1,0:T(8,128)(2,1)} %param.15) | copy-start | bytes 9437188
  213.2 2.2 copy-start.10
  215.3 14.7 %copy-start.7 = (bf16[1,2048,768]{2,1,0:T(8,128)(2,1)S(1)}, bf16[1,2048,768]{2,1,0:T(8,128)(2,1)}, u32[]{:S(2)}) copy-start(bf16[1,2048,768]{2,1,0:T(8,128)(2,1)} %param.16) | copy-start | bytes 9437188
  283.2 5.7 %copy-start.3 = (s32[1024]{0:T(1024)S(1)}, s32[1024]{0:T(1024)}, u32[]{:S(2)}) copy-start(s32[1024]{0:T(1024)} %get-tuple-element.6.place_ref) | copy-start | bytes 12292
  283.2 5.7 %copy-start.2 = (bf16[16,8,16,128]{3,2,1,0:T(8,128)(2,1)S(1)}, bf16[16,8,16,128]{3,2,1,0:T(8,128)(2,1)}, u32[]{:S(2)}) copy-start(bf16[16,8,16,128]{3,2,1,0:T(8,128)(2,1)} %copy.24) | copy-start | bytes 1572868
  283.2 83.9 %all-to-all-start.3 = ((bf16[128,12,16,128]{3,2,1,0:T(8,128)(2,1)}), bf16[128,12,16,128]{3,2,1,0:T(8,128)(2,1)}, u32[]{:S(2)}, u32[]{:S(2)}) async-start(bf16[128,12,16,128]{3,2,1,0:T(8,128)(2,1)} %bitcast.58), calls=%async_computation.3 | async-start | bytes 12582912 | tf_op jit(solution)/shard_map/all_to_all | solution.py:159
  305.5 69.0 %copy-start.1 = (bf16[1,768,2048]{2,1,0:T(8,128)(2,1)S(1)}, bf16[1,768,2048]{2,1,0:T(8,128)(2,1)}, u32[]{:S(2)}) copy-start(bf16[1,768,2048]{2,1,0:T(8,128)(2,1)} %param.17) | copy-start | bytes 9437188

commit v4 on v2

--- a/solution.py
+++ b/solution.py
@@ -82,19 +82,16 @@
     running = jnp.cumsum(hot.astype(jnp.int32), axis=0)
     rank = jnp.sum(jnp.where(hot, running, 0), axis=1) - 1
     place = target * slots + rank
-    source = (
-        jnp.full((count * slots,), pairs, jnp.int32)
-        .at[place]
-        .set(jnp.arange(pairs, dtype=jnp.int32))
+    pair_row = jnp.arange(pairs, dtype=jnp.int32) // top_count
+    tok3 = tokens.reshape(tok_rows, sub, LANES)
+    cot3 = cotangent.reshape(tok_rows, sub, LANES)
+    empty = jnp.zeros((count * slots, sub, LANES), jnp.bfloat16)
+    send_x = empty.at[place].set(tok3[pair_row], unique_indices=True)
+    scaled = (cot3[pair_row].astype(jnp.float32) * gates.reshape(-1)[:, None, None]).astype(
+        jnp.bfloat16
     )
-    row_of = source // top_count
-    tok_pad = jnp.concatenate([tokens, jnp.zeros((1, width), jnp.bfloat16)], axis=0)
-    cot_pad = jnp.concatenate([cotangent, jnp.zeros((1, width), jnp.bfloat16)], axis=0)
-    gate_pad = jnp.concatenate([gates.reshape(-1), jnp.zeros((1,), jnp.float32)], axis=0)
-    tok3 = tok_pad.reshape(tok_rows + 1, sub, LANES)
-    cot3 = cot_pad.reshape(tok_rows + 1, sub, LANES)
-    send_x = tok3[row_of].reshape(count, slots, sub, LANES)
-    send_c = (cot3[row_of].astype(jnp.float32) * gate_pad[source][:, None, None]).astype(jnp.bfloat16)
+    send_c = empty.at[place].set(scaled, unique_indices=True)
+    send_x = send_x.reshape(count, slots, sub, LANES)
     send_c = send_c.reshape(count, slots, sub, LANES)
     recv_x = lax.all_to_all(send_x, "ep", split_axis=0, concat_axis=0, tiled=True)
     recv_c = lax.all_to_all(send_c, "ep", split_axis=0, concat_axis=0, tiled=True)
@@ -114,7 +111,7 @@
         .astype(jnp.float32)
     )
     mixed = jnp.sum(gates[:, :, None, None] * out_pairs, axis=1).astype(jnp.bfloat16)
-    cot_f = cotangent.reshape(tok_rows, 1, sub, LANES).astype(jnp.float32)
+    cot_f = cot3.reshape(tok_rows, 1, sub, LANES).astype(jnp.float32)
     gate_grad = jnp.sum(cot_f * out_pairs, axis=(2, 3))
     in_grad = combine_rows(place, grad_back.reshape(-1, sub, LANES), tok_rows, top_count)
     return (mixed.reshape(tok_rows, width), in_grad.reshape(tok_rows, width), gate_grad)

time: 370 us -> 533 us (1.44); the launches traced: 369 us -> 526 us
  local copies, waits for them, and re-layouts: 64.1 us -> 269 us
  waiting for transfers between devices: 194 us -> 141 us
    scatter x1 -> x2, local copies, waits for them, and re-layouts: 4.32 us -> 208 us  [the longest x1 104 us: body(): send_c = empty.at[place].set(scaled, unique_indices=True)]
    all_to_all x1, waiting for transfers between devices: 52.7 us -> 0.01 us  [body(): lax.all_to_all(send_x, 'ep', split_axis=0, concat_axis=0, tiled=True)]
    broadcast_in_dim x0 -> x2, local copies, waits for them, and re-layouts: none -> 6.43 us  [body(): empty = jnp.zeros((count * slots, sub, LANES), jnp.bfloat16)]
    gather x3 -> x2, local copies, waits for them, and re-layouts: 23.3 us -> 18.8 us  [the longest x1 9.42 us: body(): cot3[pair_row].astype(jnp.float32) * gates.reshape(-1)[:, None, None]]
    unnamed x34 -> x31, local copies, waits for them, and re-layouts: 19.9 us -> 20.5 us
  transfers between devices with their start and end apart: 4 -> 4, of which waited for: 4 -> 3; matrix products, arithmetic and copies ran while one was open for 31% -> 41% of each run, Pallas kernels for 0% -> 0%
where the time goes in v4:
time: 533 us; the launch traced here: 526 us
  local copies, waits for them, and re-layouts  269 us (50%)
  waiting for transfers between devices  141 us (26%)
  matrix products  58.1 us (11%)
  starting transfers between devices  32.6 us (6%)
  other arithmetic  18.4 us (3%)
    scatter x1, local copies, waits for them, and re-layouts, body(): send_c = empty.at[place].set(scaled, unique_indices=True)  104 us
    scatter x1, local copies, waits for them, and re-layouts, body(): send_x = empty.at[place].set(tok3[pair_row], unique_indices=True)  104 us
    all_to_all x1, waiting for transfers between devices, body(): lax.all_to_all(pair_grad.reshape(count, slots, sub, LANES), 'ep', split_a...  57.4 us
    all_to_all x1, waiting for transfers between devices, body(): lax.all_to_all(send_c, 'ep', split_axis=0, concat_axis=0, tiled=True)  47.1 us
    all_to_all x1, waiting for transfers between devices, body(): lax.all_to_all(out_rows.reshape(count, slots, sub, LANES), 'ep', split_ax...  36.9 us
    unnamed x31, local copies, waits for them, and re-layouts  20.5 us
    dot_general x1, matrix products, project_back(): lax.dot_general(grad_a, wg, (((1,), (1,)), ((), ())), preferred_element_t...  14.7 us
    dot_general x1, matrix products, project_back(): lax.dot_general(grad_b, wu, (((1,), (1,)), ((), ())), preferred_element_t...  11.3 us
  transfers between devices with their start and end apart: 4, of which 3 were waited for; matrix products, arithmetic and copies ran while one was open for 41% of the time, Pallas kernels for 0%

profile of v4, /device:TPU:27, one launch (start us, length us, event | category | flops | bytes accessed | tf_op | source)
XLA Modules:
  0.0 525.5 jit_solution(1330647813167119715)
XLA Ops:
  0.7 0.9 broadcast_in_dim.31
  1.6 0.1 reshape.176
  1.7 0.8 select_reduce_fusion.1
  2.5 0.7 add.71
  3.2 0.8 copy.25
  4.0 0.1 eq.53
  4.1 0.4 select_reduce_fusion
  4.5 0.1 copy.26
  4.6 0.2 fusion.28
  4.8 0.8 copy-done.3
  5.6 1.1 broadcast_add_fusion
  6.7 0.1 copy.27
  6.8 0.4 fusion.27
  7.2 2.0 copy.30
  9.1 9.4 %gather_fusion = bf16[1024,16,128]{2,1,0:T(8,128)(2,1)} fusion(bf16[128,16,128]{2,1,0:T(8,128)(2,1)} %bitcast.74, s32[1024]{0:T(1024)S(1)} %broadcast_clamp_fusion.1), kind=kCustom, calls=%fused_computation | custom fusion | bytes 8392704 | tf_op jit(solution)/shard_map/gather | solution.py:89
  18.6 3.2 broadcast_in_dim.30.clone
  21.7 104.2 %scatter_fusion = bf16[1536,16,128]{2,1,0:T(8,128)(2,1)} fusion(bf16[1536,16,128]{2,1,0:T(8,128)(2,1)} %broadcast_in_dim.30.clone, s32[1024]{0:T(1024)S(1)} %bitcast.82, bf16[1024,16,128]{2,1,0:T(8,128)(2,1)} %gather_fusion), kind=kCustom, calls=%fused_computation.3 | custom fusion | bytes 12587008 | tf_op jit(solution)/shard_map/scatter | solution.py:89
  126.0 11.0 %all-to-all-start = ((bf16[128,12,16,128]{3,2,1,0:T(8,128)(2,1)}), bf16[128,12,16,128]{3,2,1,0:T(8,128)(2,1)}, u32[]{:S(2)}, u32[]{:S(2)}) async-start(bf16[128,12,16,128]{3,2,1,0:T(8,128)(2,1)} %bitcast.73), calls=%async_computation | async-start | bytes 12582912 | tf_op jit(solution)/shard_map/all_to_all | solution.py:96
  137.0 0.1 copy.24
  137.1 0.1 mul.91
  137.2 2.0 copy.34
  139.1 9.4 %gather_fusion.2 = bf16[1024,16,128]{2,1,0:T(8,128)(2,1)} fusion(bf16[128,16,128]{2,1,0:T(8,128)(2,1)} %bitcast.71, s32[1024]{0:T(1024)S(1)} %broadcast_clamp_fusion.1), kind=kCustom, calls=%fused_computation.2 | custom fusion | bytes 8392704 | tf_op jit(solution)/shard_map/gather | solution.py:90
  148.6 5.9 %multiply_convert_fusion = bf16[1024,16,128]{2,1,0:T(8,128)(2,1)} fusion(bf16[1024,16,128]{2,1,0:T(8,128)(2,1)} %gather_fusion.2, f32[1024]{0:T(1024)S(1)} %mul.91), kind=kLoop, calls=%fused_computation.10 | loop fusion | flops 6291456 | bytes 8392704 | tf_op jit(solution)/shard_map/convert_element_type | solution.py:90
  154.4 3.3 broadcast_in_dim.30.clone.1
  157.7 104.3 %scatter_fusion.1 = bf16[1536,16,128]{2,1,0:T(8,128)(2,1)} fusion(bf16[1536,16,128]{2,1,0:T(8,128)(2,1)} %broadcast_in_dim.30.clone.1, s32[1024]{0:T(1024)S(1)} %bitcast.83, bf16[1024,16,128]{2,1,0:T(8,128)(2,1)} %multiply_convert_fusion), kind=kCustom, calls=%fused_computation.4 | custom fusion | bytes 12587008 | tf_op jit(solution)/shard_map/scatter | solution.py:93
  261.9 10.3 %all-to-all-start.2 = ((bf16[128,12,16,128]{3,2,1,0:T(8,128)(2,1)}), bf16[128,12,16,128]{3,2,1,0:T(8,128)(2,1)}, u32[]{:S(2)}, u32[]{:S(2)}) async-start(bf16[128,12,16,128]{3,2,1,0:T(8,128)(2,1)} %bitcast.72), calls=%async_computation.2 | async-start | bytes 12582912 | tf_op jit(solution)/shard_map/all_to_all | solution.py:97
  272.2 9.0 %fusion.7 = f32[1536,768]{1,0:T(8,128)S(1)} fusion(bf16[192,8,16,128]{3,2,1,0:T(8,128)(2,1)} %bitcast.20, bf16[1,2048,768]{2,1,0:T(8,128)(2,1)} %param.15), kind=kOutput, calls=%fused_computation.17 | convolution fusion | flops 4831838208 | bytes 14155776 | tf_op jit(solution)/shard_map/dot_general | solution.py:12
  281.3 9.6 %fusion.5 = f32[1536,768]{1,0:T(8,128)S(1)} fusion(bf16[192,8,16,128]{3,2,1,0:T(8,128)(2,1)} %bitcast.20, bf16[1,2048,768]{2,1,0:T(8,128)(2,1)S(1)} %copy-done.7), kind=kOutput, calls=%fused_computation.15 | convolution fusion | flops 4831838208 | bytes 14155776 | tf_op jit(solution)/shard_map/dot_general | solution.py:13
  290.9 2.1 copy-done.10
  293.0 5.4 %fusion.21 = bf16[192,8,16,128]{3,1,2,0:T(8,128)(2,1)S(1)} fusion(bf16[1,768,2048]{2,1,0:T(8,128)(2,1)S(1)} %copy-done, f32[1536,768]{1,0:T(8,128)S(1)} %fusion.5, f32[1536,768]{1,0:T(8,128)S(1)} %fusion.7), kind=kOutput, calls=%fused_computation.33 | convolution fusion | flops 4842061824 | bytes 18874368 | tf_op jit(solution)/shard_map/dot_general | solution.py:20
  298.4 4.9 copy.32
  303.3 47.1 %all-to-all-done.2 = bf16[128,12,16,128]{3,2,1,0:T(8,128)(2,1)} async-done(((bf16[128,12,16,128]{3,2,1,0:T(8,128)(2,1)}), bf16[128,12,16,128]{3,2,1,0:T(8,128)(2,1)}, u32[]{:S(2)}, u32[]{:S(2)}) %all-to-all-start.2) | async-done | bytes 6291488 | tf_op jit(solution)/shard_map/all_to_all | solution.py:97
  350.4 5.7 %all-to-all-start.1 = ((bf16[128,12,16,128]{3,2,1,0:T(8,128)(2,1)}), bf16[128,12,16,128]{3,2,1,0:T(8,128)(2,1)}, u32[]{:S(2)}, u32[]{:S(2)}) async-start(bf16[128,12,16,128]{3,2,1,0:T(8,128)(2,1)} %bitcast.77), calls=%async_computation.1 | async-start | bytes 12582912 | tf_op jit(solution)/shard_map/all_to_all | solution.py:101
  356.1 8.1 %fusion.2 = f32[1536,768]{1,0:T(8,128)S(1)} fusion(bf16[192,8,16,128]{3,2,1,0:T(8,128)(2,1)} %bitcast.30, bf16[1,768,2048]{2,1,0:T(8,128)(2,1)S(1)} %copy-done), kind=kOutput, calls=%fused_computation.12 | convolution fusion | flops 4831838208 | bytes 14155776 | tf_op jit(solution)/shard_map/dot_general | solution.py:25
  364.2 2.2 copy-done.11
  366.4 14.7 %fusion.15 = f32[1536,2048]{1,0:T(8,128)} fusion(bf16[1,2048,768]{2,1,0:T(8,128)(2,1)S(1)} %copy-done.6, f32[1536,768]{1,0:T(8,128)} %copy-done.9, f32[1536,768]{1,0:T(8,128)S(1)} %fusion.2, f32[1536,768]{1,0:T(8,128)} %copy-done.10), kind=kOutput, calls=%fused_computation.29 | convolution fusion | flops 4843634688 | bytes 29884416 | tf_op jit(solution)/shard_map/dot_general | solution.py:30
  381.1 11.3 %fusion.18 = bf16[192,8,16,128]{3,1,2,0:T(8,128)(2,1)S(1)} fusion(f32[1536,2048]{1,0:T(8,128)} %fusion.15, bf16[1,2048,768]{2,1,0:T(8,128)(2,1)S(1)} %copy-done.8, f32[1536,768]{1,0:T(8,128)} %copy-done.11, f32[1536,768]{1,0:T(8,128)} %copy-done.9), kind=kOutput, calls=%fused_computation.32 | convolution fusion | flops 4845207552 | bytes 31457280 | tf_op jit(solution)/shard_map/dot_general | solution.py:33
  392.4 5.0 copy.36
  397.4 36.9 %all-to-all-done.1 = bf16[128,12,16,128]{3,2,1,0:T(8,128)(2,1)} async-done(((bf16[128,12,16,128]{3,2,1,0:T(8,128)(2,1)}), bf16[128,12,16,128]{3,2,1,0:T(8,128)(2,1)}, u32[]{:S(2)}, u32[]{:S(2)}) %all-to-all-start.1) | async-done | bytes 6291488 | tf_op jit(solution)/shard_map/all_to_all | solution.py:101
  434.3 5.7 %all-to-all-start.3 = ((bf16[128,12,16,128]{3,2,1,0:T(8,128)(2,1)}), bf16[128,12,16,128]{3,2,1,0:T(8,128)(2,1)}, u32[]{:S(2)}, u32[]{:S(2)}) async-start(bf16[128,12,16,128]{3,2,1,0:T(8,128)(2,1)} %bitcast.76), calls=%async_computation.3 | async-start | bytes 12582912 | tf_op jit(solution)/shard_map/all_to_all | solution.py:105
  440.0 0.1 bitcast_convert_fusion
  440.1 11.2 %gather_fusion.1 = bf16[1024,16,128]{2,1,0:T(8,128)(2,1)} fusion(bf16[1536,16,128]{2,1,0:T(8,128)(2,1)} %bitcast.11, s32[1024]{0:T(1024)S(1)} %broadcast_clamp_fusion), kind=kCustom, calls=%fused_computation.1 | custom fusion | bytes 8392704 | tf_op jit(solution)/shard_map/gather | solution.py:109
  451.3 4.6 fusion.1
  455.9 0.7 copy.29
  456.5 4.3 fusion
  460.8 57.4 %all-to-all-done.3 = bf16[128,12,16,128]{3,2,1,0:T(8,128)(2,1)} async-done(((bf16[128,12,16,128]{3,2,1,0:T(8,128)(2,1)}), bf16[128,12,16,128]{3,2,1,0:T(8,128)(2,1)}, u32[]{:S(2)}, u32[]{:S(2)}) %all-to-all-start.3) | async-done | bytes 6291488 | tf_op jit(solution)/shard_map/all_to_all | solution.py:105
  518.2 4.9 shard_map.112
  523.1 2.4 copy_bitcast_fusion
  (31 shorter events, 0.1 us)
Async XLA Ops:
  0.6 292.4 %copy-start = (bf16[1,768,2048]{2,1,0:T(8,128)(2,1)S(1)}, bf16[1,768,2048]{2,1,0:T(8,128)(2,1)}, u32[]{:S(2)}) copy-start(bf16[1,768,2048]{2,1,0:T(8,128)(2,1)} %param.17) | copy-start | bytes 9437188
  4.8 0.8 copy-start.3
  7.2 11.4 %copy-start.4 = (s32[1024]{0:T(1024)}, s32[1024]{0:T(1024)S(1)}, u32[]{:S(2)}) copy-start(s32[1024]{0:T(1024)S(1)} %add_add_fusion.place_ref) | copy-start | bytes 12292
  126.0 11.0 %copy-start.5 = (f32[128,8]{0,1:T(8,128)S(1)}, f32[128,8]{0,1:T(8,128)}, u32[]{:S(2)}) copy-start(f32[128,8]{0,1:T(8,128)} %param.11) | copy-start | bytes 12292
  126.0 135.9 %all-to-all-start = ((bf16[128,12,16,128]{3,2,1,0:T(8,128)(2,1)}), bf16[128,12,16,128]{3,2,1,0:T(8,128)(2,1)}, u32[]{:S(2)}, u32[]{:S(2)}) async-start(bf16[128,12,16,128]{3,2,1,0:T(8,128)(2,1)} %bitcast.73), calls=%async_computation | async-start | bytes 12582912 | tf_op jit(solution)/shard_map/all_to_all | solution.py:96
  261.9 88.5 %all-to-all-start.2 = ((bf16[128,12,16,128]{3,2,1,0:T(8,128)(2,1)}), bf16[128,12,16,128]{3,2,1,0:T(8,128)(2,1)}, u32[]{:S(2)}, u32[]{:S(2)}) async-start(bf16[128,12,16,128]{3,2,1,0:T(8,128)(2,1)} %bitcast.72), calls=%async_computation.2 | async-start | bytes 12582912 | tf_op jit(solution)/shard_map/all_to_all | solution.py:97
  272.2 9.1 %copy-start.7 = (bf16[1,2048,768]{2,1,0:T(8,128)(2,1)S(1)}, bf16[1,2048,768]{2,1,0:T(8,128)(2,1)}, u32[]{:S(2)}) copy-start(bf16[1,2048,768]{2,1,0:T(8,128)(2,1)} %param.16) | copy-start | bytes 9437188
  281.3 9.6 %copy-start.9 = (f32[1536,768]{1,0:T(8,128)}, f32[1536,768]{1,0:T(8,128)S(1)}, u32[]{:S(2)}) copy-start(f32[1536,768]{1,0:T(8,128)S(1)} %fusion.7) | copy-start | bytes 14155780
  290.9 2.1 copy-start.10
  350.4 83.9 %all-to-all-start.1 = ((bf16[128,12,16,128]{3,2,1,0:T(8,128)(2,1)}), bf16[128,12,16,128]{3,2,1,0:T(8,128)(2,1)}, u32[]{:S(2)}, u32[]{:S(2)}) async-start(bf16[128,12,16,128]{3,2,1,0:T(8,128)(2,1)} %bitcast.77), calls=%async_computation.1 | async-start | bytes 12582912 | tf_op jit(solution)/shard_map/all_to_all | solution.py:101
  356.1 10.3 %copy-start.6 = (bf16[1,2048,768]{2,1,0:T(8,128)(2,1)S(1)}, bf16[1,2048,768]{2,1,0:T(8,128)(2,1)}, u32[]{:S(2)}) copy-start(bf16[1,2048,768]{2,1,0:T(8,128)(2,1)} %param.15) | copy-start | bytes 9437188
  364.2 2.2 copy-start.11
  366.4 14.7 %copy-start.8 = (bf16[1,2048,768]{2,1,0:T(8,128)(2,1)S(1)}, bf16[1,2048,768]{2,1,0:T(8,128)(2,1)}, u32[]{:S(2)}) copy-start(bf16[1,2048,768]{2,1,0:T(8,128)(2,1)} %param.16) | copy-start | bytes 9437188
  434.3 5.7 %copy-start.2 = (bf16[16,8,16,128]{3,2,1,0:T(8,128)(2,1)S(1)}, bf16[16,8,16,128]{3,2,1,0:T(8,128)(2,1)}, u32[]{:S(2)}) copy-start(bf16[16,8,16,128]{3,2,1,0:T(8,128)(2,1)} %copy.34) | copy-start | bytes 1572868
  434.3 83.9 %all-to-all-start.3 = ((bf16[128,12,16,128]{3,2,1,0:T(8,128)(2,1)}), bf16[128,12,16,128]{3,2,1,0:T(8,128)(2,1)}, u32[]{:S(2)}, u32[]{:S(2)}) async-start(bf16[128,12,16,128]{3,2,1,0:T(8,128)(2,1)} %bitcast.76), calls=%async_computation.3 | async-start | bytes 12582912 | tf_op jit(solution)/shard_map/all_to_all | solution.py:105
  456.5 69.0 %copy-start.1 = (bf16[1,768,2048]{2,1,0:T(8,128)(2,1)S(1)}, bf16[1,768,2048]{2,1,0:T(8,128)(2,1)}, u32[]{:S(2)}) copy-start(bf16[1,768,2048]{2,1,0:T(8,128)(2,1)} %param.17) | copy-start | bytes 9437188

commit v5 on v4

--- a/solution.py
+++ b/solution.py
@@ -58,6 +58,41 @@
     )(place, rows)
 
 
+def dispatch_tiles(place, gate_flat, src3, total, top_count):
+    pairs = place.shape[0]
+
+    def kernel(place_ref, *refs):
+        if gate_flat is None:
+            src_ref, out_ref = refs
+        else:
+            gate_ref, src_ref, out_ref = refs
+
+        def clear_row(i, carry):
+            out_ref[i] = jnp.zeros(out_ref.shape[1:], out_ref.dtype)
+            return carry
+
+        lax.fori_loop(0, total, clear_row, 0, unroll=8)
+
+        def one_pair(p, carry):
+            if gate_flat is None:
+                out_ref[place_ref[p]] = src_ref[p // top_count]
+            else:
+                row = src_ref[p // top_count].astype(jnp.float32) * gate_ref[p]
+                out_ref[place_ref[p]] = row.astype(out_ref.dtype)
+            return carry
+
+        lax.fori_loop(0, pairs, one_pair, 0, unroll=4)
+
+    smem = pl.BlockSpec(memory_space=pltpu.SMEM)
+    vmem = pl.BlockSpec(memory_space=pltpu.VMEM)
+    return pl.pallas_call(
+        kernel,
+        out_shape=jax.ShapeDtypeStruct((total,) + src3.shape[1:], src3.dtype),
+        in_specs=[smem, vmem] if gate_flat is None else [smem, smem, vmem],
+        out_specs=vmem,
+    )(*((place, src3) if gate_flat is None else (place, gate_flat, src3)))
+
+
 def body(tokens, cotangent, gates, experts, owner, swapped, w_gate, w_up, w_down):
     tok_rows, width = tokens.shape
     top_count = experts.shape[1]
@@ -82,15 +117,10 @@
     running = jnp.cumsum(hot.astype(jnp.int32), axis=0)
     rank = jnp.sum(jnp.where(hot, running, 0), axis=1) - 1
     place = target * slots + rank
-    pair_row = jnp.arange(pairs, dtype=jnp.int32) // top_count
     tok3 = tokens.reshape(tok_rows, sub, LANES)
     cot3 = cotangent.reshape(tok_rows, sub, LANES)
-    empty = jnp.zeros((count * slots, sub, LANES), jnp.bfloat16)
-    send_x = empty.at[place].set(tok3[pair_row], unique_indices=True)
-    scaled = (cot3[pair_row].astype(jnp.float32) * gates.reshape(-1)[:, None, None]).astype(
-        jnp.bfloat16
-    )
-    send_c = empty.at[place].set(scaled, unique_indices=True)
+    send_x = dispatch_tiles(place, None, tok3, count * slots, top_count)
+    send_c = dispatch_tiles(place, gates.reshape(-1), cot3, count * slots, top_count)
     send_x = send_x.reshape(count, slots, sub, LANES)
     send_c = send_c.reshape(count, slots, sub, LANES)
     recv_x = lax.all_to_all(send_x, "ep", split_axis=0, concat_axis=0, tiled=True)

time: 533 us -> 371 us (0.70); the launches traced: 526 us -> 370 us
  local copies, waits for them, and re-layouts: 269 us -> 36.1 us
  waiting for transfers between devices: 141 us -> 204 us
  Pallas kernels: 4.92 us -> 29.1 us
    scatter x2 -> x0, local copies, waits for them, and re-layouts: 208 us -> none  [the longest x1 104 us: body(): send_c = empty.at[place].set(scaled, unique_indices=True)]
    all_to_all x1, waiting for transfers between devices: 0.01 us -> 63 us  [body(): lax.all_to_all(send_x, 'ep', split_axis=0, concat_axis=0, tiled=True)]
    pallas_call x0 -> x2, Pallas kernels: none -> 24.2 us  [dispatch_tiles(): pl.pallas_call(kernel, out_shape=jax.ShapeDtypeStruct((total,) + src3.sha...]
    gather x2 -> x0, local copies, waits for them, and re-layouts: 18.8 us -> none  [the longest x1 9.42 us: body(): cot3[pair_row].astype(jnp.float32) * gates.reshape(-1)[:, None, None]]
    broadcast_in_dim x2 -> x0, local copies, waits for them, and re-layouts: 6.43 us -> none  [body(): empty = jnp.zeros((count * slots, sub, LANES), jnp.bfloat16)]
    convert_element_type x1 -> x0, other arithmetic: 5.86 us -> none  [body(): (cot3[pair_row].astype(jnp.float32) * gates.reshape(-1)[:, None, None]).a...]
  transfers between devices with their start and end apart: 4 -> 4, of which waited for: 3 -> 4; matrix products, arithmetic and copies ran while one was open for 41% -> 25% of each run, Pallas kernels for 0% -> 3%
where the time goes in v5:
time: 371 us; the launch traced here: 370 us
  waiting for transfers between devices  204 us (55%)
  matrix products  58.1 us (16%)
  local copies, waits for them, and re-layouts  36.1 us (10%)
  Pallas kernels  29.1 us (8%)
  starting transfers between devices  28.3 us (8%)
  other arithmetic  13.1 us (4%)
    all_to_all x1, waiting for transfers between devices, body(): lax.all_to_all(send_x, 'ep', split_axis=0, concat_axis=0, tiled=True)  63 us
    all_to_all x1, waiting for transfers between devices, body(): lax.all_to_all(pair_grad.reshape(count, slots, sub, LANES), 'ep', split_a...  57.4 us
    all_to_all x1, waiting for transfers between devices, body(): lax.all_to_all(send_c, 'ep', split_axis=0, concat_axis=0, tiled=True)  47.1 us
    all_to_all x1, waiting for transfers between devices, body(): lax.all_to_all(out_rows.reshape(count, slots, sub, LANES), 'ep', split_ax...  36.9 us
    pallas_call x2, Pallas kernels, dispatch_tiles(): pl.pallas_call(kernel, out_shape=jax.ShapeDtypeStruct((total,) + src3.sha...  24.2 us
    unnamed x31, local copies, waits for them, and re-layouts  20.5 us
    dot_general x1, matrix products, project_back(): lax.dot_general(grad_a, wg, (((1,), (1,)), ((), ())), preferred_element_t...  14.6 us
    dot_general x1, matrix products, project_back(): lax.dot_general(grad_b, wu, (((1,), (1,)), ((), ())), preferred_element_t...  11.3 us
  transfers between devices with their start and end apart: 4, of which 4 were waited for; matrix products, arithmetic and copies ran while one was open for 25% of the time, Pallas kernels for 3%

profile of v5, /device:TPU:27, one launch (start us, length us, event | category | flops | bytes accessed | tf_op | source)
XLA Modules:
  0.0 369.9 jit_solution(11617044508778482528)
XLA Ops:
  0.6 0.0 copy-start
  0.6 0.9 broadcast_in_dim.38
  1.5 0.1 reshape.135
  1.7 0.8 select_reduce_fusion.1
  2.5 0.7 add.51
  3.2 0.8 copy.25
  4.0 0.1 eq.53
  4.1 0.4 select_reduce_fusion
  4.4 0.1 copy.26
  4.5 0.2 fusion.28
  4.7 0.0 copy-start.3
  4.7 0.8 copy-done.3
  5.6 1.1 broadcast_add_fusion
  6.6 0.1 copy.27
  6.8 0.4 fusion.27
  7.1 0.6 add_add_fusion.place_ref
  7.7 1.9 copy.30
  9.7 11.7 %shard_map.112 = bf16[1536,16,128]{2,1,0:T(8,128)(2,1)} custom-call(s32[1024]{0:T(1024)} %add_add_fusion.place_ref, bf16[128,16,128]{2,1,0:T(8,128)(2,1)} %bitcast.74), custom_call_target="tpu_custom_call" | custom-call | tf_op jit(solution)/shard_map/pallas_call | solution.py:88
  21.4 10.9 %all-to-all-start = ((bf16[128,12,16,128]{3,2,1,0:T(8,128)(2,1)}), bf16[128,12,16,128]{3,2,1,0:T(8,128)(2,1)}, u32[]{:S(2)}, u32[]{:S(2)}) async-start(bf16[128,12,16,128]{3,2,1,0:T(8,128)(2,1)} %bitcast.72), calls=%async_computation | async-start | bytes 12582912 | tf_op jit(solution)/shard_map/all_to_all | solution.py:126
  32.3 0.1 copy.24
  32.4 0.7 reshape.142.refs_0_
  33.1 1.9 copy.34
  35.1 12.5 %shard_map.113 = bf16[1536,16,128]{2,1,0:T(8,128)(2,1)} custom-call(s32[1024]{0:T(1024)} %add_add_fusion.place_ref, f32[1024]{0:T(1024)} %reshape.142.refs_0_, bf16[128,16,128]{2,1,0:T(8,128)(2,1)} %bitcast.73), custom_call_target="tpu_custom_call" | custom-call | tf_op jit(solution)/shard_map/pallas_call | solution.py:88
  47.6 63.0 %all-to-all-done = bf16[128,12,16,128]{3,2,1,0:T(8,128)(2,1)} async-done(((bf16[128,12,16,128]{3,2,1,0:T(8,128)(2,1)}), bf16[128,12,16,128]{3,2,1,0:T(8,128)(2,1)}, u32[]{:S(2)}, u32[]{:S(2)}) %all-to-all-start) | async-done | bytes 6291488 | tf_op jit(solution)/shard_map/all_to_all | solution.py:126
  110.5 5.8 %all-to-all-start.2 = ((bf16[128,12,16,128]{3,2,1,0:T(8,128)(2,1)}), bf16[128,12,16,128]{3,2,1,0:T(8,128)(2,1)}, u32[]{:S(2)}, u32[]{:S(2)}) async-start(bf16[128,12,16,128]{3,2,1,0:T(8,128)(2,1)} %bitcast.71), calls=%async_computation.2 | async-start | bytes 12582912 | tf_op jit(solution)/shard_map/all_to_all | solution.py:127
  116.3 0.0 copy-start.7
  116.3 9.0 %fusion.7 = f32[1536,768]{1,0:T(8,128)S(1)} fusion(bf16[192,8,16,128]{3,2,1,0:T(8,128)(2,1)} %bitcast.19, bf16[1,2048,768]{2,1,0:T(8,128)(2,1)} %param.15), kind=kOutput, calls=%fused_computation.12 | convolution fusion | flops 4831838208 | bytes 14155776 | tf_op jit(solution)/shard_map/dot_general | solution.py:12
  125.4 9.6 %fusion.5 = f32[1536,768]{1,0:T(8,128)S(1)} fusion(bf16[192,8,16,128]{3,2,1,0:T(8,128)(2,1)} %bitcast.19, bf16[1,2048,768]{2,1,0:T(8,128)(2,1)S(1)} %copy-done.7), kind=kOutput, calls=%fused_computation.10 | convolution fusion | flops 4831838208 | bytes 14155776 | tf_op jit(solution)/shard_map/dot_general | solution.py:13
  135.0 2.1 copy-done.10
  137.1 5.4 %fusion.21 = bf16[192,8,16,128]{3,1,2,0:T(8,128)(2,1)S(1)} fusion(bf16[1,768,2048]{2,1,0:T(8,128)(2,1)S(1)} %copy-done, f32[1536,768]{1,0:T(8,128)S(1)} %fusion.5, f32[1536,768]{1,0:T(8,128)S(1)} %fusion.7), kind=kOutput, calls=%fused_computation.28 | convolution fusion | flops 4842061824 | bytes 18874368 | tf_op jit(solution)/shard_map/dot_general | solution.py:20
  142.5 4.9 %copy.32 = bf16[192,8,16,128]{3,2,1,0:T(8,128)(2,1)} copy(bf16[192,8,16,128]{3,1,2,0:T(8,128)(2,1)S(1)} %fusion.21) | data formatting | bytes 12582912
  147.5 47.1 %all-to-all-done.2 = bf16[128,12,16,128]{3,2,1,0:T(8,128)(2,1)} async-done(((bf16[128,12,16,128]{3,2,1,0:T(8,128)(2,1)}), bf16[128,12,16,128]{3,2,1,0:T(8,128)(2,1)}, u32[]{:S(2)}, u32[]{:S(2)}) %all-to-all-start.2) | async-done | bytes 6291488 | tf_op jit(solution)/shard_map/all_to_all | solution.py:127
  194.5 5.8 %all-to-all-start.1 = ((bf16[128,12,16,128]{3,2,1,0:T(8,128)(2,1)}), bf16[128,12,16,128]{3,2,1,0:T(8,128)(2,1)}, u32[]{:S(2)}, u32[]{:S(2)}) async-start(bf16[128,12,16,128]{3,2,1,0:T(8,128)(2,1)} %bitcast.70), calls=%async_computation.1 | async-start | bytes 12582912 | tf_op jit(solution)/shard_map/all_to_all | solution.py:131
  200.3 8.1 %fusion.2 = f32[1536,768]{1,0:T(8,128)S(1)} fusion(bf16[192,8,16,128]{3,2,1,0:T(8,128)(2,1)} %bitcast.29, bf16[1,768,2048]{2,1,0:T(8,128)(2,1)S(1)} %copy-done), kind=kOutput, calls=%fused_computation.7 | convolution fusion | flops 4831838208 | bytes 14155776 | tf_op jit(solution)/shard_map/dot_general | solution.py:25
  208.5 2.2 copy-done.11
  210.7 14.6 %fusion.15 = f32[1536,2048]{1,0:T(8,128)} fusion(bf16[1,2048,768]{2,1,0:T(8,128)(2,1)S(1)} %copy-done.6, f32[1536,768]{1,0:T(8,128)} %copy-done.9, f32[1536,768]{1,0:T(8,128)S(1)} %fusion.2, f32[1536,768]{1,0:T(8,128)} %copy-done.10), kind=kOutput, calls=%fused_computation.24 | convolution fusion | flops 4843634688 | bytes 29884416 | tf_op jit(solution)/shard_map/dot_general | solution.py:30
  225.3 11.3 %fusion.18 = bf16[192,8,16,128]{3,1,2,0:T(8,128)(2,1)S(1)} fusion(f32[1536,2048]{1,0:T(8,128)} %fusion.15, bf16[1,2048,768]{2,1,0:T(8,128)(2,1)S(1)} %copy-done.8, f32[1536,768]{1,0:T(8,128)} %copy-done.11, f32[1536,768]{1,0:T(8,128)} %copy-done.9), kind=kOutput, calls=%fused_computation.27 | convolution fusion | flops 4845207552 | bytes 31457280 | tf_op jit(solution)/shard_map/dot_general | solution.py:33
  236.6 5.0 %copy.36 = bf16[192,8,16,128]{3,2,1,0:T(8,128)(2,1)} copy(bf16[192,8,16,128]{3,1,2,0:T(8,128)(2,1)S(1)} %fusion.18) | data formatting | bytes 12582912
  241.6 36.9 %all-to-all-done.1 = bf16[128,12,16,128]{3,2,1,0:T(8,128)(2,1)} async-done(((bf16[128,12,16,128]{3,2,1,0:T(8,128)(2,1)}), bf16[128,12,16,128]{3,2,1,0:T(8,128)(2,1)}, u32[]{:S(2)}, u32[]{:S(2)}) %all-to-all-start.1) | async-done | bytes 6291488 | tf_op jit(solution)/shard_map/all_to_all | solution.py:131
  278.5 5.8 %all-to-all-start.3 = ((bf16[128,12,16,128]{3,2,1,0:T(8,128)(2,1)}), bf16[128,12,16,128]{3,2,1,0:T(8,128)(2,1)}, u32[]{:S(2)}, u32[]{:S(2)}) async-start(bf16[128,12,16,128]{3,2,1,0:T(8,128)(2,1)} %bitcast.69), calls=%async_computation.3 | async-start | bytes 12582912 | tf_op jit(solution)/shard_map/all_to_all | solution.py:135
  284.4 0.1 bitcast_convert_fusion
  284.5 11.2 %gather_fusion = bf16[1024,16,128]{2,1,0:T(8,128)(2,1)} fusion(bf16[1536,16,128]{2,1,0:T(8,128)(2,1)} %bitcast.8, s32[1024]{0:T(1024)S(1)} %broadcast_clamp_fusion), kind=kCustom, calls=%fused_computation | custom fusion | bytes 8392704 | tf_op jit(solution)/shard_map/gather | solution.py:139
  295.7 4.6 %fusion.1 = f32[128,8]{1,0:T(8,128)S(1)} fusion(bf16[128,8,16,128]{3,2,1,0:T(8,128)(2,1)} %bitcast.68, f32[128,16,128]{2,1,0:T(8,128)S(1)} %bitcast_convert_fusion), kind=kLoop, calls=%fused_computation.5 | loop fusion | flops 6290432 | bytes 5246976 | tf_op jit(solution)/shard_map/reduce_sum | solution.py:145
  300.2 0.7 copy.29
  300.9 4.3 %fusion = bf16[128,16,128]{2,1,0:T(8,128)(2,1)} fusion(f32[128,8]{1,0:T(8,128)S(1)} %copy.24, bf16[1024,16,128]{2,1,0:T(8,128)(2,1)} %gather_fusion), kind=kLoop, calls=%fused_computation.4 | loop fusion | flops 6029312 | bytes 4722688 | tf_op jit(solution)/shard_map/reduce_sum | solution.py:143
  305.2 57.4 %all-to-all-done.3 = bf16[128,12,16,128]{3,2,1,0:T(8,128)(2,1)} async-done(((bf16[128,12,16,128]{3,2,1,0:T(8,128)(2,1)}), bf16[128,12,16,128]{3,2,1,0:T(8,128)(2,1)}, u32[]{:S(2)}, u32[]{:S(2)}) %all-to-all-start.3) | async-done | bytes 6291488 | tf_op jit(solution)/shard_map/all_to_all | solution.py:135
  362.6 4.9 %shard_map.114 = bf16[128,16,128]{2,1,0:T(8,128)(2,1)} custom-call(s32[1024]{0:T(1024)} %add_add_fusion.place_ref, bf16[1536,16,128]{2,1,0:T(8,128)(2,1)} %bitcast.13.rows_ref), custom_call_target="tpu_custom_call" | custom-call | tf_op jit(solution)/shard_map/pallas_call | solution.py:50
  367.5 2.4 copy_bitcast_fusion
  (24 shorter events, 0.1 us)
Async XLA Ops:
  0.6 136.5 %copy-start = (bf16[1,768,2048]{2,1,0:T(8,128)(2,1)S(1)}, bf16[1,768,2048]{2,1,0:T(8,128)(2,1)}, u32[]{:S(2)}) copy-start(bf16[1,768,2048]{2,1,0:T(8,128)(2,1)} %param.17) | copy-start | bytes 9437188
  4.7 0.8 copy-start.3
  21.4 11.0 %copy-start.5 = (f32[128,8]{0,1:T(8,128)S(1)}, f32[128,8]{0,1:T(8,128)}, u32[]{:S(2)}) copy-start(f32[128,8]{0,1:T(8,128)} %param.11) | copy-start | bytes 12292
  21.4 89.2 %all-to-all-start = ((bf16[128,12,16,128]{3,2,1,0:T(8,128)(2,1)}), bf16[128,12,16,128]{3,2,1,0:T(8,128)(2,1)}, u32[]{:S(2)}, u32[]{:S(2)}) async-start(bf16[128,12,16,128]{3,2,1,0:T(8,128)(2,1)} %bitcast.72), calls=%async_computation | async-start | bytes 12582912 | tf_op jit(solution)/shard_map/all_to_all | solution.py:126
  110.5 84.0 %all-to-all-start.2 = ((bf16[128,12,16,128]{3,2,1,0:T(8,128)(2,1)}), bf16[128,12,16,128]{3,2,1,0:T(8,128)(2,1)}, u32[]{:S(2)}, u32[]{:S(2)}) async-start(bf16[128,12,16,128]{3,2,1,0:T(8,128)(2,1)} %bitcast.71), calls=%async_computation.2 | async-start | bytes 12582912 | tf_op jit(solution)/shard_map/all_to_all | solution.py:127
  116.3 9.1 %copy-start.7 = (bf16[1,2048,768]{2,1,0:T(8,128)(2,1)S(1)}, bf16[1,2048,768]{2,1,0:T(8,128)(2,1)}, u32[]{:S(2)}) copy-start(bf16[1,2048,768]{2,1,0:T(8,128)(2,1)} %param.16) | copy-start | bytes 9437188
  125.4 9.6 %copy-start.9 = (f32[1536,768]{1,0:T(8,128)}, f32[1536,768]{1,0:T(8,128)S(1)}, u32[]{:S(2)}) copy-start(f32[1536,768]{1,0:T(8,128)S(1)} %fusion.7) | copy-start | bytes 14155780
  135.0 2.1 copy-start.10
  194.5 84.0 %all-to-all-start.1 = ((bf16[128,12,16,128]{3,2,1,0:T(8,128)(2,1)}), bf16[128,12,16,128]{3,2,1,0:T(8,128)(2,1)}, u32[]{:S(2)}, u32[]{:S(2)}) async-start(bf16[128,12,16,128]{3,2,1,0:T(8,128)(2,1)} %bitcast.70), calls=%async_computation.1 | async-start | bytes 12582912 | tf_op jit(solution)/shard_map/all_to_all | solution.py:131
  200.3 10.3 %copy-start.6 = (bf16[1,2048,768]{2,1,0:T(8,128)(2,1)S(1)}, bf16[1,2048,768]{2,1,0:T(8,128)(2,1)}, u32[]{:S(2)}) copy-start(bf16[1,2048,768]{2,1,0:T(8,128)(2,1)} %param.15) | copy-start | bytes 9437188
  208.5 2.2 copy-start.11
  210.7 14.7 %copy-start.8 = (bf16[1,2048,768]{2,1,0:T(8,128)(2,1)S(1)}, bf16[1,2048,768]{2,1,0:T(8,128)(2,1)}, u32[]{:S(2)}) copy-start(bf16[1,2048,768]{2,1,0:T(8,128)(2,1)} %param.16) | copy-start | bytes 9437188
  278.5 5.8 %copy-start.4 = (s32[1024]{0:T(1024)S(1)}, s32[1024]{0:T(1024)}, u32[]{:S(2)}) copy-start(s32[1024]{0:T(1024)} %add_add_fusion.place_ref) | copy-start | bytes 12292
  278.5 5.8 %copy-start.2 = (bf16[16,8,16,128]{3,2,1,0:T(8,128)(2,1)S(1)}, bf16[16,8,16,128]{3,2,1,0:T(8,128)(2,1)}, u32[]{:S(2)}) copy-start(bf16[16,8,16,128]{3,2,1,0:T(8,128)(2,1)} %copy.34) | copy-start | bytes 1572868
  278.5 84.0 %all-to-all-start.3 = ((bf16[128,12,16,128]{3,2,1,0:T(8,128)(2,1)}), bf16[128,12,16,128]{3,2,1,0:T(8,128)(2,1)}, u32[]{:S(2)}, u32[]{:S(2)}) async-start(bf16[128,12,16,128]{3,2,1,0:T(8,128)(2,1)} %bitcast.69), calls=%async_computation.3 | async-start | bytes 12582912 | tf_op jit(solution)/shard_map/all_to_all | solution.py:135
  300.9 69.0 %copy-start.1 = (bf16[1,768,2048]{2,1,0:T(8,128)(2,1)S(1)}, bf16[1,768,2048]{2,1,0:T(8,128)(2,1)}, u32[]{:S(2)}) copy-start(bf16[1,768,2048]{2,1,0:T(8,128)(2,1)} %param.17) | copy-start | bytes 9437188

commit v6 on v2

--- a/solution.py
+++ b/solution.py
@@ -82,10 +82,10 @@
     running = jnp.cumsum(hot.astype(jnp.int32), axis=0)
     rank = jnp.sum(jnp.where(hot, running, 0), axis=1) - 1
     place = target * slots + rank
-    source = (
-        jnp.full((count * slots,), pairs, jnp.int32)
-        .at[place]
-        .set(jnp.arange(pairs, dtype=jnp.int32))
+    slot_ids = jnp.arange(count * slots, dtype=jnp.int32)
+    pair_ids = jnp.arange(pairs, dtype=jnp.int32)
+    source = jnp.min(
+        jnp.where(place[None, :] == slot_ids[:, None], pair_ids[None, :], pairs), axis=1
     )
     row_of = source // top_count
     tok_pad = jnp.concatenate([tokens, jnp.zeros((1, width), jnp.bfloat16)], axis=0)

time: 370 us -> 366 us (0.989)
  local copies, waits for them, and re-layouts: 64.1 us -> 59.7 us
    scatter x1 -> x0, local copies, waits for them, and re-layouts: 4.32 us -> none  [body(): source = jnp.full((count * slots,), pairs, jnp.int32).at[place].set(jnp.a...]
where the time goes in v6:
time: 366 us
  waiting for transfers between devices  194 us (53%)
  local copies, waits for them, and re-layouts  59.7 us (16%)
  matrix products  58.1 us (16%)
  starting transfers between devices  28.1 us (8%)
  other arithmetic  20 us (5%)
  Pallas kernels  4.92 us (1%)
    all_to_all x1, waiting for transfers between devices, body(): lax.all_to_all(pair_grad.reshape(count, slots, sub, LANES), 'ep', split_a...  57 us
    all_to_all x1, waiting for transfers between devices, body(): lax.all_to_all(send_x, 'ep', split_axis=0, concat_axis=0, tiled=True)  52.7 us
    all_to_all x1, waiting for transfers between devices, body(): lax.all_to_all(send_c, 'ep', split_axis=0, concat_axis=0, tiled=True)  47.1 us
    all_to_all x1, waiting for transfers between devices, body(): lax.all_to_all(out_rows.reshape(count, slots, sub, LANES), 'ep', split_ax...  36.9 us
    unnamed x34, local copies, waits for them, and re-layouts  19.9 us
    dot_general x1, matrix products, project_back(): lax.dot_general(grad_a, wg, (((1,), (1,)), ((), ())), preferred_element_t...  14.7 us
    dot_general x1, matrix products, project_back(): lax.dot_general(grad_b, wu, (((1,), (1,)), ((), ())), preferred_element_t...  11.3 us
    gather x1, local copies, waits for them, and re-layouts, body(): back.reshape(-1, sub, LANES)[place].reshape(tok_rows, top_count, sub, LANES)  11.2 us
  transfers between devices with their start and end apart: 4, of which 4 were waited for; matrix products, arithmetic and copies ran while one was open for 31% of the time, Pallas kernels for 0%

profile of v6, /device:TPU:27, one launch (start us, length us, event | category | flops | bytes accessed | tf_op | source)
XLA Modules:
  0.0 365.5 jit_solution(4092495887535272928)
XLA Ops:
  0.6 0.9 broadcast_in_dim.40
  1.5 0.1 reshape.218
  1.7 0.8 select_reduce_fusion.2
  2.5 0.7 add.91
  3.2 0.8 copy.25
  4.1 0.4 select_reduce_fusion.1
  4.5 0.2 fusion.29
  4.7 0.8 copy-done.2
  5.6 1.1 broadcast_add_fusion
  6.6 0.1 copy.27
  6.8 0.4 fusion.28
  7.1 0.9 select_reduce_fusion
  8.1 1.1 concatenate.9
  9.2 0.1 copy.30
  9.4 0.8 slice.18
  10.2 7.5 %gather_fusion = bf16[1536,16,128]{2,1,0:T(8,128)(2,1)} fusion(bf16[129,16,128]{2,1,0:T(8,128)(2,1)} %slice.18, s32[2048]{0:T(1024)S(1)} %get-tuple-element.12), kind=kCustom, calls=%fused_computation | custom fusion | bytes 12589056 | tf_op jit(solution)/shard_map/gather | solution.py:96
  17.7 10.9 %all-to-all-start = ((bf16[128,12,16,128]{3,2,1,0:T(8,128)(2,1)}), bf16[128,12,16,128]{3,2,1,0:T(8,128)(2,1)}, u32[]{:S(2)}, u32[]{:S(2)}) async-start(bf16[128,12,16,128]{3,2,1,0:T(8,128)(2,1)} %bitcast.78), calls=%async_computation | async-start | bytes 12582912 | tf_op jit(solution)/shard_map/all_to_all | solution.py:99
  28.8 8.4 %gather_fusion.3 = f32[1536]{0:T(1024)S(1)} fusion(f32[1025]{0:T(1024)S(1)} %pad_maximum_fusion, s32[2048]{0:T(1024)S(1)} %get-tuple-element.11), kind=kCustom, calls=%fused_computation.3 | custom fusion | bytes 18432 | tf_op jit(solution)/shard_map/gather | solution.py:97
  37.3 1.1 concatenate.10
  38.4 0.1 copy.34
  38.6 0.9 slice.19
  39.4 7.4 %gather_fusion.2 = bf16[1536,16,128]{2,1,0:T(8,128)(2,1)} fusion(bf16[129,16,128]{2,1,0:T(8,128)(2,1)} %slice.19, s32[2048]{0:T(1024)S(1)} %get-tuple-element.12), kind=kCustom, calls=%fused_computation.2 | custom fusion | bytes 12589056 | tf_op jit(solution)/shard_map/gather | solution.py:97
  46.8 7.3 %fusion = bf16[128,12,16,128]{3,2,1,0:T(8,128)(2,1)} fusion(bf16[128,12,16,128]{3,2,1,0:T(8,128)(2,1)} %bitcast.79, f32[128,12]{1,0:T(8,128)S(1)} %mul.96), kind=kLoop, calls=%fused_computation.5 | loop fusion | flops 9437184 | bytes 12589056 | tf_op jit(solution)/shard_map/convert_element_type | solution.py:97
  54.2 52.7 %all-to-all-done = bf16[128,12,16,128]{3,2,1,0:T(8,128)(2,1)} async-done(((bf16[128,12,16,128]{3,2,1,0:T(8,128)(2,1)}), bf16[128,12,16,128]{3,2,1,0:T(8,128)(2,1)}, u32[]{:S(2)}, u32[]{:S(2)}) %all-to-all-start) | async-done | bytes 6291488 | tf_op jit(solution)/shard_map/all_to_all | solution.py:99
  106.8 5.8 %all-to-all-start.2 = ((bf16[128,12,16,128]{3,2,1,0:T(8,128)(2,1)}), bf16[128,12,16,128]{3,2,1,0:T(8,128)(2,1)}, u32[]{:S(2)}, u32[]{:S(2)}) async-start(bf16[128,12,16,128]{3,2,1,0:T(8,128)(2,1)} %fusion), calls=%async_computation.2 | async-start | bytes 12582912 | tf_op jit(solution)/shard_map/all_to_all | solution.py:100
  112.6 9.0 %fusion.8 = f32[1536,768]{1,0:T(8,128)S(1)} fusion(bf16[192,8,16,128]{3,2,1,0:T(8,128)(2,1)} %bitcast.21, bf16[1,2048,768]{2,1,0:T(8,128)(2,1)} %param.15), kind=kOutput, calls=%fused_computation.17 | convolution fusion | flops 4831838208 | bytes 14155776 | tf_op jit(solution)/shard_map/dot_general | solution.py:12
  121.7 9.6 %fusion.6 = f32[1536,768]{1,0:T(8,128)S(1)} fusion(bf16[192,8,16,128]{3,2,1,0:T(8,128)(2,1)} %bitcast.21, bf16[1,2048,768]{2,1,0:T(8,128)(2,1)S(1)} %copy-done.7), kind=kOutput, calls=%fused_computation.15 | convolution fusion | flops 4831838208 | bytes 14155776 | tf_op jit(solution)/shard_map/dot_general | solution.py:13
  131.3 2.1 copy-done.10
  133.4 5.4 %fusion.22 = bf16[192,8,16,128]{3,1,2,0:T(8,128)(2,1)S(1)} fusion(bf16[1,768,2048]{2,1,0:T(8,128)(2,1)S(1)} %copy-done, f32[1536,768]{1,0:T(8,128)S(1)} %fusion.6, f32[1536,768]{1,0:T(8,128)S(1)} %fusion.8), kind=kOutput, calls=%fused_computation.35 | convolution fusion | flops 4842061824 | bytes 18874368 | tf_op jit(solution)/shard_map/dot_general | solution.py:20
  138.8 4.9 %copy.32 = bf16[192,8,16,128]{3,2,1,0:T(8,128)(2,1)} copy(bf16[192,8,16,128]{3,1,2,0:T(8,128)(2,1)S(1)} %fusion.22) | data formatting | bytes 12582912
  143.8 47.1 %all-to-all-done.2 = bf16[128,12,16,128]{3,2,1,0:T(8,128)(2,1)} async-done(((bf16[128,12,16,128]{3,2,1,0:T(8,128)(2,1)}), bf16[128,12,16,128]{3,2,1,0:T(8,128)(2,1)}, u32[]{:S(2)}, u32[]{:S(2)}) %all-to-all-start.2) | async-done | bytes 6291488 | tf_op jit(solution)/shard_map/all_to_all | solution.py:100
  190.8 5.7 %all-to-all-start.1 = ((bf16[128,12,16,128]{3,2,1,0:T(8,128)(2,1)}), bf16[128,12,16,128]{3,2,1,0:T(8,128)(2,1)}, u32[]{:S(2)}, u32[]{:S(2)}) async-start(bf16[128,12,16,128]{3,2,1,0:T(8,128)(2,1)} %bitcast.77), calls=%async_computation.1 | async-start | bytes 12582912 | tf_op jit(solution)/shard_map/all_to_all | solution.py:104
  196.5 8.1 %fusion.3 = f32[1536,768]{1,0:T(8,128)S(1)} fusion(bf16[192,8,16,128]{3,2,1,0:T(8,128)(2,1)} %bitcast.32, bf16[1,768,2048]{2,1,0:T(8,128)(2,1)S(1)} %copy-done), kind=kOutput, calls=%fused_computation.12 | convolution fusion | flops 4831838208 | bytes 14155776 | tf_op jit(solution)/shard_map/dot_general | solution.py:25
  204.7 2.2 copy-done.11
  206.9 14.7 %fusion.16 = f32[1536,2048]{1,0:T(8,128)} fusion(bf16[1,2048,768]{2,1,0:T(8,128)(2,1)S(1)} %copy-done.6, f32[1536,768]{1,0:T(8,128)} %copy-done.9, f32[1536,768]{1,0:T(8,128)S(1)} %fusion.3, f32[1536,768]{1,0:T(8,128)} %copy-done.10), kind=kOutput, calls=%fused_computation.31 | convolution fusion | flops 4843634688 | bytes 29884416 | tf_op jit(solution)/shard_map/dot_general | solution.py:30
  221.6 11.3 %fusion.19 = bf16[192,8,16,128]{3,1,2,0:T(8,128)(2,1)S(1)} fusion(f32[1536,2048]{1,0:T(8,128)} %fusion.16, bf16[1,2048,768]{2,1,0:T(8,128)(2,1)S(1)} %copy-done.8, f32[1536,768]{1,0:T(8,128)} %copy-done.11, f32[1536,768]{1,0:T(8,128)} %copy-done.9), kind=kOutput, calls=%fused_computation.34 | convolution fusion | flops 4845207552 | bytes 31457280 | tf_op jit(solution)/shard_map/dot_general | solution.py:33
  232.8 5.0 %copy.36 = bf16[192,8,16,128]{3,2,1,0:T(8,128)(2,1)} copy(bf16[192,8,16,128]{3,1,2,0:T(8,128)(2,1)S(1)} %fusion.19) | data formatting | bytes 12582912
  237.8 36.9 %all-to-all-done.1 = bf16[128,12,16,128]{3,2,1,0:T(8,128)(2,1)} async-done(((bf16[128,12,16,128]{3,2,1,0:T(8,128)(2,1)}), bf16[128,12,16,128]{3,2,1,0:T(8,128)(2,1)}, u32[]{:S(2)}, u32[]{:S(2)}) %all-to-all-start.1) | async-done | bytes 6291488 | tf_op jit(solution)/shard_map/all_to_all | solution.py:104
  274.8 5.7 %all-to-all-start.3 = ((bf16[128,12,16,128]{3,2,1,0:T(8,128)(2,1)}), bf16[128,12,16,128]{3,2,1,0:T(8,128)(2,1)}, u32[]{:S(2)}, u32[]{:S(2)}) async-start(bf16[128,12,16,128]{3,2,1,0:T(8,128)(2,1)} %bitcast.76), calls=%async_computation.3 | async-start | bytes 12582912 | tf_op jit(solution)/shard_map/all_to_all | solution.py:108
  280.5 0.2 copy.38
  280.8 11.2 %gather_fusion.1 = bf16[1024,16,128]{2,1,0:T(8,128)(2,1)} fusion(bf16[1536,16,128]{2,1,0:T(8,128)(2,1)} %bitcast.8, s32[1024]{0:T(1024)S(1)} %broadcast_clamp_fusion), kind=kCustom, calls=%fused_computation.1 | custom fusion | bytes 8392704 | tf_op jit(solution)/shard_map/gather | solution.py:112
  291.9 4.6 %fusion.2 = f32[128,8]{1,0:T(8,128)S(1)} fusion(bf16[128,8,16,128]{3,2,1,0:T(8,128)(2,1)} %bitcast.75, f32[128,16,128]{2,1,0:T(8,128)S(1)} %bitcast.80), kind=kLoop, calls=%fused_computation.10 | loop fusion | flops 6290432 | bytes 5246976 | tf_op jit(solution)/shard_map/reduce_sum | solution.py:118
  296.5 0.7 copy.29
  297.2 3.5 fusion.1
  300.7 0.9 copy.54
  301.6 57.0 %all-to-all-done.3 = bf16[128,12,16,128]{3,2,1,0:T(8,128)(2,1)} async-done(((bf16[128,12,16,128]{3,2,1,0:T(8,128)(2,1)}), bf16[128,12,16,128]{3,2,1,0:T(8,128)(2,1)}, u32[]{:S(2)}, u32[]{:S(2)}) %all-to-all-start.3) | async-done | bytes 6291488 | tf_op jit(solution)/shard_map/all_to_all | solution.py:108
  358.6 4.9 %shard_map.112 = bf16[128,16,128]{2,1,0:T(8,128)(2,1)} custom-call(s32[1024]{0:T(1024)} %copy-done.4, bf16[1536,16,128]{2,1,0:T(8,128)(2,1)} %bitcast.13.rows_ref), custom_call_target="tpu_custom_call" | custom-call | tf_op jit(solution)/shard_map/pallas_call | solution.py:50
  363.6 2.0 copy.53
  (37 shorter events, 0.8 us)
Async XLA Ops:
  0.6 132.8 %copy-start = (bf16[1,768,2048]{2,1,0:T(8,128)(2,1)S(1)}, bf16[1,768,2048]{2,1,0:T(8,128)(2,1)}, u32[]{:S(2)}) copy-start(bf16[1,768,2048]{2,1,0:T(8,128)(2,1)} %param.17) | copy-start | bytes 9437188
  4.7 0.8 copy-start.2
  7.1 273.6 %copy-start.4 = (s32[1024]{0:T(1024)}, s32[1024]{0:T(1024)S(1)}, u32[]{:S(2)}) copy-start(s32[1024]{0:T(1024)S(1)} %add_add_fusion.place_ref) | copy-start | bytes 12292
  17.7 11.0 %copy-start.5 = (f32[128,8]{0,1:T(8,128)S(1)}, f32[128,8]{0,1:T(8,128)}, u32[]{:S(2)}) copy-start(f32[128,8]{0,1:T(8,128)} %param.11) | copy-start | bytes 12292
  17.7 89.2 %all-to-all-start = ((bf16[128,12,16,128]{3,2,1,0:T(8,128)(2,1)}), bf16[128,12,16,128]{3,2,1,0:T(8,128)(2,1)}, u32[]{:S(2)}, u32[]{:S(2)}) async-start(bf16[128,12,16,128]{3,2,1,0:T(8,128)(2,1)} %bitcast.78), calls=%async_computation | async-start | bytes 12582912 | tf_op jit(solution)/shard_map/all_to_all | solution.py:99
  106.8 84.0 %all-to-all-start.2 = ((bf16[128,12,16,128]{3,2,1,0:T(8,128)(2,1)}), bf16[128,12,16,128]{3,2,1,0:T(8,128)(2,1)}, u32[]{:S(2)}, u32[]{:S(2)}) async-start(bf16[128,12,16,128]{3,2,1,0:T(8,128)(2,1)} %fusion), calls=%async_computation.2 | async-start | bytes 12582912 | tf_op jit(solution)/shard_map/all_to_all | solution.py:100
  112.6 9.1 %copy-start.7 = (bf16[1,2048,768]{2,1,0:T(8,128)(2,1)S(1)}, bf16[1,2048,768]{2,1,0:T(8,128)(2,1)}, u32[]{:S(2)}) copy-start(bf16[1,2048,768]{2,1,0:T(8,128)(2,1)} %param.16) | copy-start | bytes 9437188
  121.7 9.6 %copy-start.9 = (f32[1536,768]{1,0:T(8,128)}, f32[1536,768]{1,0:T(8,128)S(1)}, u32[]{:S(2)}) copy-start(f32[1536,768]{1,0:T(8,128)S(1)} %fusion.8) | copy-start | bytes 14155780
  131.3 2.1 copy-start.10
  190.8 83.9 %all-to-all-start.1 = ((bf16[128,12,16,128]{3,2,1,0:T(8,128)(2,1)}), bf16[128,12,16,128]{3,2,1,0:T(8,128)(2,1)}, u32[]{:S(2)}, u32[]{:S(2)}) async-start(bf16[128,12,16,128]{3,2,1,0:T(8,128)(2,1)} %bitcast.77), calls=%async_computation.1 | async-start | bytes 12582912 | tf_op jit(solution)/shard_map/all_to_all | solution.py:104
  196.5 10.3 %copy-start.6 = (bf16[1,2048,768]{2,1,0:T(8,128)(2,1)S(1)}, bf16[1,2048,768]{2,1,0:T(8,128)(2,1)}, u32[]{:S(2)}) copy-start(bf16[1,2048,768]{2,1,0:T(8,128)(2,1)} %param.15) | copy-start | bytes 9437188
  204.7 2.2 copy-start.11
  206.9 14.7 %copy-start.8 = (bf16[1,2048,768]{2,1,0:T(8,128)(2,1)S(1)}, bf16[1,2048,768]{2,1,0:T(8,128)(2,1)}, u32[]{:S(2)}) copy-start(bf16[1,2048,768]{2,1,0:T(8,128)(2,1)} %param.16) | copy-start | bytes 9437188
  274.8 5.7 %copy-start.3 = (bf16[128,2048]{1,0:T(8,128)(2,1)S(1)}, bf16[128,2048]{1,0:T(8,128)(2,1)}, u32[]{:S(2)}) copy-start(bf16[128,2048]{1,0:T(8,128)(2,1)} %param.10) | copy-start | bytes 1572868
  274.8 83.9 %all-to-all-start.3 = ((bf16[128,12,16,128]{3,2,1,0:T(8,128)(2,1)}), bf16[128,12,16,128]{3,2,1,0:T(8,128)(2,1)}, u32[]{:S(2)}, u32[]{:S(2)}) async-start(bf16[128,12,16,128]{3,2,1,0:T(8,128)(2,1)} %bitcast.76), calls=%async_computation.3 | async-start | bytes 12582912 | tf_op jit(solution)/shard_map/all_to_all | solution.py:108
  297.2 68.4 %copy-start.1 = (bf16[1,768,2048]{2,1,0:T(8,128)(2,1)S(1)}, bf16[1,768,2048]{2,1,0:T(8,128)(2,1)}, u32[]{:S(2)}) copy-start(bf16[1,768,2048]{2,1,0:T(8,128)(2,1)} %param.17) | copy-start | bytes 9437188

commit v7 on v6

--- a/solution.py
+++ b/solution.py
@@ -66,24 +66,22 @@
     slots = tok_rows * top_count * 3 // (2 * expert_total)
     pairs = tok_rows * top_count
     sub = width // LANES
-    devices = jnp.arange(count, dtype=jnp.int32)
-    dev_flag = jnp.repeat(swapped, 2)
-    step_dev = dev_flag * (1 - 2 * (devices % 2))
-    holder = owner + jnp.sum(
-        jnp.where(owner[:, None] == devices[None, :], step_dev[None, :], 0), axis=1
+    pair_slots = jnp.arange(swapped.shape[0], dtype=jnp.int32)
+    flag = jnp.sum(
+        jnp.where((owner // 2)[:, None] == pair_slots[None, :], swapped[None, :], 0), axis=1
     )
+    holder = owner + flag * (1 - 2 * (owner % 2))
     wg = w_gate[0]
     wu = w_up[0]
     wd = w_down[0]
     flat_e = experts.reshape(-1)
     chosen = flat_e[:, None] == jnp.arange(expert_total, dtype=jnp.int32)[None, :]
     target = jnp.sum(jnp.where(chosen, holder[None, :], 0), axis=1)
-    hot = target[:, None] == devices[None, :]
-    running = jnp.cumsum(hot.astype(jnp.int32), axis=0)
-    rank = jnp.sum(jnp.where(hot, running, 0), axis=1) - 1
+    pair_ids = jnp.arange(pairs, dtype=jnp.int32)
+    earlier = (target[None, :] == target[:, None]) & (pair_ids[None, :] < pair_ids[:, None])
+    rank = jnp.sum(earlier.astype(jnp.int32), axis=1)
     place = target * slots + rank
     slot_ids = jnp.arange(count * slots, dtype=jnp.int32)
-    pair_ids = jnp.arange(pairs, dtype=jnp.int32)
     source = jnp.min(
         jnp.where(place[None, :] == slot_ids[:, None], pair_ids[None, :], pairs), axis=1
     )

time: 366 us -> 364 us (level)
    unnamed x34 -> x32, local copies, waits for them, and re-layouts: 19.9 us -> 19.1 us
  transfers between devices with their start and end apart: 4 -> 4, of which waited for: 4 -> 4; matrix products, arithmetic and copies ran while one was open for 31% -> 32% of each run, Pallas kernels for 0% -> 0%
where the time goes in v7:
time: 364 us; the launch traced here: 363 us
  waiting for transfers between devices  194 us (53%)
  matrix products  58.1 us (16%)
  local copies, waits for them, and re-layouts  57.7 us (16%)
  starting transfers between devices  28.1 us (8%)
  other arithmetic  19.8 us (5%)
  Pallas kernels  4.92 us (1%)
    all_to_all x1, waiting for transfers between devices, body(): lax.all_to_all(pair_grad.reshape(count, slots, sub, LANES), 'ep', split_a...  57 us
    all_to_all x1, waiting for transfers between devices, body(): lax.all_to_all(send_x, 'ep', split_axis=0, concat_axis=0, tiled=True)  52.7 us
    all_to_all x1, waiting for transfers between devices, body(): lax.all_to_all(send_c, 'ep', split_axis=0, concat_axis=0, tiled=True)  47.1 us
    all_to_all x1, waiting for transfers between devices, body(): lax.all_to_all(out_rows.reshape(count, slots, sub, LANES), 'ep', split_ax...  36.9 us
    unnamed x32, local copies, waits for them, and re-layouts  19.1 us
    dot_general x1, matrix products, project_back(): lax.dot_general(grad_a, wg, (((1,), (1,)), ((), ())), preferred_element_t...  14.7 us
    dot_general x1, matrix products, project_back(): lax.dot_general(grad_b, wu, (((1,), (1,)), ((), ())), preferred_element_t...  11.3 us
    gather x1, local copies, waits for them, and re-layouts, body(): back.reshape(-1, sub, LANES)[place].reshape(tok_rows, top_count, sub, LANES)  11.2 us
  transfers between devices with their start and end apart: 4, of which 4 were waited for; matrix products, arithmetic and copies ran while one was open for 32% of the time, Pallas kernels for 0%

profile of v7, /device:TPU:27, one launch (start us, length us, event | category | flops | bytes accessed | tf_op | source)
XLA Modules:
  0.0 363.2 jit_solution(17832872147222515738)
XLA Ops:
  0.6 0.8 and_select_fusion.2
  1.5 0.9 select_reduce_fusion.2
  2.3 0.7 fusion.34
  3.0 0.8 copy.21
  3.8 0.1 eq.28
  3.9 0.4 select_reduce_fusion.1
  4.3 0.5 convert_reduce_fusion
  4.8 0.9 select_reduce_fusion
  5.8 1.1 concatenate.9
  6.9 0.1 copy.24
  7.0 0.8 slice.8
  7.8 7.5 %gather_fusion = bf16[1536,16,128]{2,1,0:T(8,128)(2,1)} fusion(bf16[129,16,128]{2,1,0:T(8,128)(2,1)} %slice.8, s32[2048]{0:T(1024)S(1)} %get-tuple-element.12), kind=kCustom, calls=%fused_computation | custom fusion | bytes 12589056 | tf_op jit(solution)/shard_map/gather | solution.py:94
  15.3 10.9 %all-to-all-start = ((bf16[128,12,16,128]{3,2,1,0:T(8,128)(2,1)}), bf16[128,12,16,128]{3,2,1,0:T(8,128)(2,1)}, u32[]{:S(2)}, u32[]{:S(2)}) async-start(bf16[128,12,16,128]{3,2,1,0:T(8,128)(2,1)} %bitcast.69), calls=%async_computation | async-start | bytes 12582912 | tf_op jit(solution)/shard_map/all_to_all | solution.py:97
  26.3 0.1 copy.20
  26.4 0.1 reshape.185
  26.5 8.4 %gather_fusion.3 = f32[1536]{0:T(1024)S(1)} fusion(f32[1025]{0:T(1024)S(1)} %pad_maximum_fusion, s32[2048]{0:T(1024)S(1)} %get-tuple-element.11), kind=kCustom, calls=%fused_computation.3 | custom fusion | bytes 18432 | tf_op jit(solution)/shard_map/gather | solution.py:95
  34.9 0.1 mul.88
  35.0 1.1 concatenate.10
  36.1 0.1 copy.28
  36.2 0.9 slice.9
  37.1 7.4 %gather_fusion.2 = bf16[1536,16,128]{2,1,0:T(8,128)(2,1)} fusion(bf16[129,16,128]{2,1,0:T(8,128)(2,1)} %slice.9, s32[2048]{0:T(1024)S(1)} %get-tuple-element.12), kind=kCustom, calls=%fused_computation.2 | custom fusion | bytes 12589056 | tf_op jit(solution)/shard_map/gather | solution.py:95
  44.5 7.3 %fusion = bf16[128,12,16,128]{3,2,1,0:T(8,128)(2,1)} fusion(bf16[128,12,16,128]{3,2,1,0:T(8,128)(2,1)} %bitcast.70, f32[128,12]{1,0:T(8,128)S(1)} %mul.88), kind=kLoop, calls=%fused_computation.5 | loop fusion | flops 9437184 | bytes 12589056 | tf_op jit(solution)/shard_map/convert_element_type | solution.py:95
  51.8 52.7 %all-to-all-done = bf16[128,12,16,128]{3,2,1,0:T(8,128)(2,1)} async-done(((bf16[128,12,16,128]{3,2,1,0:T(8,128)(2,1)}), bf16[128,12,16,128]{3,2,1,0:T(8,128)(2,1)}, u32[]{:S(2)}, u32[]{:S(2)}) %all-to-all-start) | async-done | bytes 6291488 | tf_op jit(solution)/shard_map/all_to_all | solution.py:97
  104.5 5.8 %all-to-all-start.2 = ((bf16[128,12,16,128]{3,2,1,0:T(8,128)(2,1)}), bf16[128,12,16,128]{3,2,1,0:T(8,128)(2,1)}, u32[]{:S(2)}, u32[]{:S(2)}) async-start(bf16[128,12,16,128]{3,2,1,0:T(8,128)(2,1)} %fusion), calls=%async_computation.2 | async-start | bytes 12582912 | tf_op jit(solution)/shard_map/all_to_all | solution.py:98
  110.3 9.0 %fusion.8 = f32[1536,768]{1,0:T(8,128)S(1)} fusion(bf16[192,8,16,128]{3,2,1,0:T(8,128)(2,1)} %bitcast.16, bf16[1,2048,768]{2,1,0:T(8,128)(2,1)} %param.15), kind=kOutput, calls=%fused_computation.17 | convolution fusion | flops 4831838208 | bytes 14155776 | tf_op jit(solution)/shard_map/dot_general | solution.py:12
  119.4 9.6 %fusion.6 = f32[1536,768]{1,0:T(8,128)S(1)} fusion(bf16[192,8,16,128]{3,2,1,0:T(8,128)(2,1)} %bitcast.16, bf16[1,2048,768]{2,1,0:T(8,128)(2,1)S(1)} %copy-done.6), kind=kOutput, calls=%fused_computation.15 | convolution fusion | flops 4831838208 | bytes 14155776 | tf_op jit(solution)/shard_map/dot_general | solution.py:13
  129.0 2.1 copy-done.9
  131.1 5.4 %fusion.23 = bf16[192,8,16,128]{3,1,2,0:T(8,128)(2,1)S(1)} fusion(bf16[1,768,2048]{2,1,0:T(8,128)(2,1)S(1)} %copy-done, f32[1536,768]{1,0:T(8,128)S(1)} %fusion.6, f32[1536,768]{1,0:T(8,128)S(1)} %fusion.8), kind=kOutput, calls=%fused_computation.38 | convolution fusion | flops 4842061824 | bytes 18874368 | tf_op jit(solution)/shard_map/dot_general | solution.py:20
  136.5 4.9 %copy.26 = bf16[192,8,16,128]{3,2,1,0:T(8,128)(2,1)} copy(bf16[192,8,16,128]{3,1,2,0:T(8,128)(2,1)S(1)} %fusion.23) | data formatting | bytes 12582912
  141.4 47.1 %all-to-all-done.2 = bf16[128,12,16,128]{3,2,1,0:T(8,128)(2,1)} async-done(((bf16[128,12,16,128]{3,2,1,0:T(8,128)(2,1)}), bf16[128,12,16,128]{3,2,1,0:T(8,128)(2,1)}, u32[]{:S(2)}, u32[]{:S(2)}) %all-to-all-start.2) | async-done | bytes 6291488 | tf_op jit(solution)/shard_map/all_to_all | solution.py:98
  188.5 5.7 %all-to-all-start.1 = ((bf16[128,12,16,128]{3,2,1,0:T(8,128)(2,1)}), bf16[128,12,16,128]{3,2,1,0:T(8,128)(2,1)}, u32[]{:S(2)}, u32[]{:S(2)}) async-start(bf16[128,12,16,128]{3,2,1,0:T(8,128)(2,1)} %bitcast.68), calls=%async_computation.1 | async-start | bytes 12582912 | tf_op jit(solution)/shard_map/all_to_all | solution.py:102
  194.2 8.1 %fusion.3 = f32[1536,768]{1,0:T(8,128)S(1)} fusion(bf16[192,8,16,128]{3,2,1,0:T(8,128)(2,1)} %bitcast.27, bf16[1,768,2048]{2,1,0:T(8,128)(2,1)S(1)} %copy-done), kind=kOutput, calls=%fused_computation.12 | convolution fusion | flops 4831838208 | bytes 14155776 | tf_op jit(solution)/shard_map/dot_general | solution.py:25
  202.3 2.2 copy-done.10
  204.5 14.7 %fusion.17 = f32[1536,2048]{1,0:T(8,128)} fusion(bf16[1,2048,768]{2,1,0:T(8,128)(2,1)S(1)} %copy-done.5, f32[1536,768]{1,0:T(8,128)} %copy-done.8, f32[1536,768]{1,0:T(8,128)S(1)} %fusion.3, f32[1536,768]{1,0:T(8,128)} %copy-done.9), kind=kOutput, calls=%fused_computation.34 | convolution fusion | flops 4843634688 | bytes 29884416 | tf_op jit(solution)/shard_map/dot_general | solution.py:30
  219.2 11.3 %fusion.20 = bf16[192,8,16,128]{3,1,2,0:T(8,128)(2,1)S(1)} fusion(f32[1536,2048]{1,0:T(8,128)} %fusion.17, bf16[1,2048,768]{2,1,0:T(8,128)(2,1)S(1)} %copy-done.7, f32[1536,768]{1,0:T(8,128)} %copy-done.10, f32[1536,768]{1,0:T(8,128)} %copy-done.8), kind=kOutput, calls=%fused_computation.37 | convolution fusion | flops 4845207552 | bytes 31457280 | tf_op jit(solution)/shard_map/dot_general | solution.py:33
  230.5 5.0 %copy.30 = bf16[192,8,16,128]{3,2,1,0:T(8,128)(2,1)} copy(bf16[192,8,16,128]{3,1,2,0:T(8,128)(2,1)S(1)} %fusion.20) | data formatting | bytes 12582912
  235.5 36.9 %all-to-all-done.1 = bf16[128,12,16,128]{3,2,1,0:T(8,128)(2,1)} async-done(((bf16[128,12,16,128]{3,2,1,0:T(8,128)(2,1)}), bf16[128,12,16,128]{3,2,1,0:T(8,128)(2,1)}, u32[]{:S(2)}, u32[]{:S(2)}) %all-to-all-start.1) | async-done | bytes 6291488 | tf_op jit(solution)/shard_map/all_to_all | solution.py:102
  272.4 5.7 %all-to-all-start.3 = ((bf16[128,12,16,128]{3,2,1,0:T(8,128)(2,1)}), bf16[128,12,16,128]{3,2,1,0:T(8,128)(2,1)}, u32[]{:S(2)}, u32[]{:S(2)}) async-start(bf16[128,12,16,128]{3,2,1,0:T(8,128)(2,1)} %bitcast.67), calls=%async_computation.3 | async-start | bytes 12582912 | tf_op jit(solution)/shard_map/all_to_all | solution.py:106
  278.1 0.1 convert_bitcast_fusion
  278.2 0.2 copy.32
  278.4 11.2 %gather_fusion.1 = bf16[1024,16,128]{2,1,0:T(8,128)(2,1)} fusion(bf16[1536,16,128]{2,1,0:T(8,128)(2,1)} %bitcast.4, s32[1024]{0:T(1024)S(1)} %broadcast_clamp_fusion), kind=kCustom, calls=%fused_computation.1 | custom fusion | bytes 8392704 | tf_op jit(solution)/shard_map/gather | solution.py:110
  289.6 4.6 %fusion.2 = f32[128,8]{1,0:T(8,128)S(1)} fusion(bf16[128,8,16,128]{3,2,1,0:T(8,128)(2,1)} %bitcast.66, f32[128,16,128]{2,1,0:T(8,128)S(1)} %bitcast.71), kind=kLoop, calls=%fused_computation.10 | loop fusion | flops 6290432 | bytes 5246976 | tf_op jit(solution)/shard_map/reduce_sum | solution.py:116
  294.2 0.7 copy.23
  294.8 3.5 fusion.1
  298.3 0.9 copy.48
  299.3 57.0 %all-to-all-done.3 = bf16[128,12,16,128]{3,2,1,0:T(8,128)(2,1)} async-done(((bf16[128,12,16,128]{3,2,1,0:T(8,128)(2,1)}), bf16[128,12,16,128]{3,2,1,0:T(8,128)(2,1)}, u32[]{:S(2)}, u32[]{:S(2)}) %all-to-all-start.3) | async-done | bytes 6291488 | tf_op jit(solution)/shard_map/all_to_all | solution.py:106
  356.3 4.9 %shard_map.112 = bf16[128,16,128]{2,1,0:T(8,128)(2,1)} custom-call(s32[1024]{0:T(1024)} %copy-done.3, bf16[1536,16,128]{2,1,0:T(8,128)(2,1)} %bitcast.9.rows_ref), custom_call_target="tpu_custom_call" | custom-call | tf_op jit(solution)/shard_map/pallas_call | solution.py:50
  361.2 2.0 copy.47
  (26 shorter events, 0.2 us)
Async XLA Ops:
  0.6 130.5 %copy-start = (bf16[1,768,2048]{2,1,0:T(8,128)(2,1)S(1)}, bf16[1,768,2048]{2,1,0:T(8,128)(2,1)}, u32[]{:S(2)}) copy-start(bf16[1,768,2048]{2,1,0:T(8,128)(2,1)} %param.17) | copy-start | bytes 9437188
  4.8 273.6 %copy-start.3 = (s32[1024]{0:T(1024)}, s32[1024]{0:T(1024)S(1)}, u32[]{:S(2)}) copy-start(s32[1024]{0:T(1024)S(1)} %multiply_add_fusion.place_ref) | copy-start | bytes 12292
  15.3 11.0 %copy-start.4 = (f32[128,8]{0,1:T(8,128)S(1)}, f32[128,8]{0,1:T(8,128)}, u32[]{:S(2)}) copy-start(f32[128,8]{0,1:T(8,128)} %param.11) | copy-start | bytes 12292
  15.3 89.2 %all-to-all-start = ((bf16[128,12,16,128]{3,2,1,0:T(8,128)(2,1)}), bf16[128,12,16,128]{3,2,1,0:T(8,128)(2,1)}, u32[]{:S(2)}, u32[]{:S(2)}) async-start(bf16[128,12,16,128]{3,2,1,0:T(8,128)(2,1)} %bitcast.69), calls=%async_computation | async-start | bytes 12582912 | tf_op jit(solution)/shard_map/all_to_all | solution.py:97
  104.5 84.0 %all-to-all-start.2 = ((bf16[128,12,16,128]{3,2,1,0:T(8,128)(2,1)}), bf16[128,12,16,128]{3,2,1,0:T(8,128)(2,1)}, u32[]{:S(2)}, u32[]{:S(2)}) async-start(bf16[128,12,16,128]{3,2,1,0:T(8,128)(2,1)} %fusion), calls=%async_computation.2 | async-start | bytes 12582912 | tf_op jit(solution)/shard_map/all_to_all | solution.py:98
  110.3 9.1 %copy-start.6 = (bf16[1,2048,768]{2,1,0:T(8,128)(2,1)S(1)}, bf16[1,2048,768]{2,1,0:T(8,128)(2,1)}, u32[]{:S(2)}) copy-start(bf16[1,2048,768]{2,1,0:T(8,128)(2,1)} %param.16) | copy-start | bytes 9437188
  119.4 9.6 %copy-start.8 = (f32[1536,768]{1,0:T(8,128)}, f32[1536,768]{1,0:T(8,128)S(1)}, u32[]{:S(2)}) copy-start(f32[1536,768]{1,0:T(8,128)S(1)} %fusion.8) | copy-start | bytes 14155780
  129.0 2.1 copy-start.9
  188.5 83.9 %all-to-all-start.1 = ((bf16[128,12,16,128]{3,2,1,0:T(8,128)(2,1)}), bf16[128,12,16,128]{3,2,1,0:T(8,128)(2,1)}, u32[]{:S(2)}, u32[]{:S(2)}) async-start(bf16[128,12,16,128]{3,2,1,0:T(8,128)(2,1)} %bitcast.68), calls=%async_computation.1 | async-start | bytes 12582912 | tf_op jit(solution)/shard_map/all_to_all | solution.py:102
  194.2 10.3 %copy-start.5 = (bf16[1,2048,768]{2,1,0:T(8,128)(2,1)S(1)}, bf16[1,2048,768]{2,1,0:T(8,128)(2,1)}, u32[]{:S(2)}) copy-start(bf16[1,2048,768]{2,1,0:T(8,128)(2,1)} %param.15) | copy-start | bytes 9437188
  202.3 2.2 copy-start.10
  204.5 14.7 %copy-start.7 = (bf16[1,2048,768]{2,1,0:T(8,128)(2,1)S(1)}, bf16[1,2048,768]{2,1,0:T(8,128)(2,1)}, u32[]{:S(2)}) copy-start(bf16[1,2048,768]{2,1,0:T(8,128)(2,1)} %param.16) | copy-start | bytes 9437188
  272.4 5.7 %copy-start.2 = (bf16[128,2048]{1,0:T(8,128)(2,1)S(1)}, bf16[128,2048]{1,0:T(8,128)(2,1)}, u32[]{:S(2)}) copy-start(bf16[128,2048]{1,0:T(8,128)(2,1)} %param.10) | copy-start | bytes 1572868
  272.4 83.9 %all-to-all-start.3 = ((bf16[128,12,16,128]{3,2,1,0:T(8,128)(2,1)}), bf16[128,12,16,128]{3,2,1,0:T(8,128)(2,1)}, u32[]{:S(2)}, u32[]{:S(2)}) async-start(bf16[128,12,16,128]{3,2,1,0:T(8,128)(2,1)} %bitcast.67), calls=%async_computation.3 | async-start | bytes 12582912 | tf_op jit(solution)/shard_map/all_to_all | solution.py:106
  294.8 68.4 %copy-start.1 = (bf16[1,768,2048]{2,1,0:T(8,128)(2,1)S(1)}, bf16[1,768,2048]{2,1,0:T(8,128)(2,1)}, u32[]{:S(2)}) copy-start(bf16[1,768,2048]{2,1,0:T(8,128)(2,1)} %param.17) | copy-start | bytes 9437188

commit v8 on v7

--- a/solution.py
+++ b/solution.py
@@ -58,6 +58,30 @@
     )(place, rows)
 
 
+def gather_tiles(row_of, src3, block):
+    total = row_of.shape[0]
+
+    def kernel(row_ref, src_ref, out_ref):
+        base = pl.program_id(0) * block
+
+        def one_slot(i, carry):
+            out_ref[i] = src_ref[row_ref[base + i]]
+            return carry
+
+        lax.fori_loop(0, block, one_slot, 0, unroll=8)
+
+    return pl.pallas_call(
+        kernel,
+        out_shape=jax.ShapeDtypeStruct((total,) + src3.shape[1:], src3.dtype),
+        grid_spec=pltpu.PrefetchScalarGridSpec(
+            num_scalar_prefetch=1,
+            grid=(total // block,),
+            in_specs=[pl.BlockSpec(src3.shape, lambda g, rows: (0, 0, 0))],
+            out_specs=pl.BlockSpec((block,) + src3.shape[1:], lambda g, rows: (g, 0, 0)),
+        ),
+    )(row_of, src3)
+
+
 def body(tokens, cotangent, gates, experts, owner, swapped, w_gate, w_up, w_down):
     tok_rows, width = tokens.shape
     top_count = experts.shape[1]
@@ -91,7 +115,9 @@
     gate_pad = jnp.concatenate([gates.reshape(-1), jnp.zeros((1,), jnp.float32)], axis=0)
     tok3 = tok_pad.reshape(tok_rows + 1, sub, LANES)
     cot3 = cot_pad.reshape(tok_rows + 1, sub, LANES)
-    send_x = tok3[row_of].reshape(count, slots, sub, LANES)
+    send_x = gather_tiles(
+        jnp.minimum(row_of, tok_rows - 1), tokens.reshape(tok_rows, sub, LANES), 256
+    ).reshape(count, slots, sub, LANES)
     send_c = (cot3[row_of].astype(jnp.float32) * gate_pad[source][:, None, None]).astype(jnp.bfloat16)
     send_c = send_c.reshape(count, slots, sub, LANES)
     recv_x = lax.all_to_all(send_x, "ep", split_axis=0, concat_axis=0, tiled=True)

time: 364 us -> 364 us (level)
  local copies, waits for them, and re-layouts: 57.7 us -> 50.2 us
  Pallas kernels: 4.92 us -> 11.7 us
    gather x1 -> x0, local copies, waits for them, and re-layouts: 7.46 us -> none  [body(): send_x = tok3[row_of].reshape(count, slots, sub, LANES)]
    pallas_call x0 -> x1, Pallas kernels: none -> 6.78 us  [gather_tiles(): pl.pallas_call(kernel, out_shape=jax.ShapeDtypeStruct((total,) + src3.sha...]
where the time goes in v8:
time: 364 us; the launch traced here: 363 us
  waiting for transfers between devices  194 us (53%)
  matrix products  58.1 us (16%)
  local copies, waits for them, and re-layouts  50.2 us (14%)
  starting transfers between devices  28.1 us (8%)
  other arithmetic  20.4 us (6%)
  Pallas kernels  11.7 us (3%)
    all_to_all x1, waiting for transfers between devices, body(): lax.all_to_all(pair_grad.reshape(count, slots, sub, LANES), 'ep', split_a...  57 us
    all_to_all x1, waiting for transfers between devices, body(): lax.all_to_all(send_x, 'ep', split_axis=0, concat_axis=0, tiled=True)  52.5 us
    all_to_all x1, waiting for transfers between devices, body(): lax.all_to_all(send_c, 'ep', split_axis=0, concat_axis=0, tiled=True)  47 us
    all_to_all x1, waiting for transfers between devices, body(): lax.all_to_all(out_rows.reshape(count, slots, sub, LANES), 'ep', split_ax...  37 us
    unnamed x32, local copies, waits for them, and re-layouts  21 us
    dot_general x1, matrix products, project_back(): lax.dot_general(grad_a, wg, (((1,), (1,)), ((), ())), preferred_element_t...  14.7 us
    dot_general x1, matrix products, project_back(): lax.dot_general(grad_b, wu, (((1,), (1,)), ((), ())), preferred_element_t...  11.3 us
    gather x1, local copies, waits for them, and re-layouts, body(): back.reshape(-1, sub, LANES)[place].reshape(tok_rows, top_count, sub, LANES)  11.2 us
  transfers between devices with their start and end apart: 4, of which 4 were waited for; matrix products, arithmetic and copies ran while one was open for 32% of the time, Pallas kernels for 0%

profile of v8, /device:TPU:27, one launch (start us, length us, event | category | flops | bytes accessed | tf_op | source)
XLA Modules:
  0.0 362.9 jit_solution(15057006249046750762)
XLA Ops:
  0.6 0.8 and_select_fusion.2
  1.5 0.9 select_reduce_fusion.2
  2.3 0.7 fusion.37
  3.0 0.8 copy.21
  3.8 0.1 eq.28
  3.9 0.4 select_reduce_fusion.1
  4.3 0.5 convert_reduce_fusion
  4.8 0.9 select_reduce_fusion
  5.7 0.6 fusion.30.row_ref
  6.3 1.9 copy.24
  8.3 6.8 %shard_map.112 = bf16[1536,16,128]{2,1,0:T(8,128)(2,1)} custom-call(s32[1536]{0:T(1024)} %fusion.30.row_ref, bf16[128,16,128]{2,1,0:T(8,128)(2,1)} %bitcast.75), custom_call_target="tpu_custom_call" | custom-call | tf_op jit(solution)/shard_map/pallas_call | solution.py:73
  15.1 10.9 %all-to-all-start = ((bf16[128,12,16,128]{3,2,1,0:T(8,128)(2,1)}), bf16[128,12,16,128]{3,2,1,0:T(8,128)(2,1)}, u32[]{:S(2)}, u32[]{:S(2)}) async-start(bf16[128,12,16,128]{3,2,1,0:T(8,128)(2,1)} %bitcast.66), calls=%async_computation | async-start | bytes 12582912 | tf_op jit(solution)/shard_map/all_to_all | solution.py:123
  26.0 0.1 copy.20
  26.1 0.1 reshape.185
  26.2 0.1 fusion.32
  26.3 8.4 %gather_fusion.2 = f32[1536]{0:T(1024)S(1)} fusion(f32[1025]{0:T(1024)S(1)} %pad_maximum_fusion, s32[2048]{0:T(1024)S(1)} %get-tuple-element.11), kind=kCustom, calls=%fused_computation.2 | custom fusion | bytes 18432 | tf_op jit(solution)/shard_map/gather | solution.py:121
  34.7 0.1 mul.88
  34.8 1.1 concatenate.6
  35.9 0.1 copy.28
  36.0 0.9 slice.6
  36.9 7.4 %gather_fusion.1 = bf16[1536,16,128]{2,1,0:T(8,128)(2,1)} fusion(bf16[129,16,128]{2,1,0:T(8,128)(2,1)} %slice.6, s32[2048]{0:T(1024)S(1)} %get-tuple-element.12), kind=kCustom, calls=%fused_computation.1 | custom fusion | bytes 12589056 | tf_op jit(solution)/shard_map/gather | solution.py:121
  44.4 7.4 %fusion = bf16[128,12,16,128]{3,2,1,0:T(8,128)(2,1)} fusion(bf16[128,12,16,128]{3,2,1,0:T(8,128)(2,1)} %bitcast.69, f32[128,12]{1,0:T(8,128)S(1)} %mul.88), kind=kLoop, calls=%fused_computation.4 | loop fusion | flops 9437184 | bytes 12589056 | tf_op jit(solution)/shard_map/convert_element_type | solution.py:121
  51.7 52.5 %all-to-all-done = bf16[128,12,16,128]{3,2,1,0:T(8,128)(2,1)} async-done(((bf16[128,12,16,128]{3,2,1,0:T(8,128)(2,1)}), bf16[128,12,16,128]{3,2,1,0:T(8,128)(2,1)}, u32[]{:S(2)}, u32[]{:S(2)}) %all-to-all-start) | async-done | bytes 6291488 | tf_op jit(solution)/shard_map/all_to_all | solution.py:123
  104.2 5.8 %all-to-all-start.2 = ((bf16[128,12,16,128]{3,2,1,0:T(8,128)(2,1)}), bf16[128,12,16,128]{3,2,1,0:T(8,128)(2,1)}, u32[]{:S(2)}, u32[]{:S(2)}) async-start(bf16[128,12,16,128]{3,2,1,0:T(8,128)(2,1)} %fusion), calls=%async_computation.2 | async-start | bytes 12582912 | tf_op jit(solution)/shard_map/all_to_all | solution.py:124
  110.0 9.0 %fusion.8 = f32[1536,768]{1,0:T(8,128)S(1)} fusion(bf16[192,8,16,128]{3,2,1,0:T(8,128)(2,1)} %bitcast.15, bf16[1,2048,768]{2,1,0:T(8,128)(2,1)} %param.15), kind=kOutput, calls=%fused_computation.16 | convolution fusion | flops 4831838208 | bytes 14155776 | tf_op jit(solution)/shard_map/dot_general | solution.py:12
  119.1 9.6 %fusion.6 = f32[1536,768]{1,0:T(8,128)S(1)} fusion(bf16[192,8,16,128]{3,2,1,0:T(8,128)(2,1)} %bitcast.15, bf16[1,2048,768]{2,1,0:T(8,128)(2,1)S(1)} %copy-done.6), kind=kOutput, calls=%fused_computation.14 | convolution fusion | flops 4831838208 | bytes 14155776 | tf_op jit(solution)/shard_map/dot_general | solution.py:13
  128.7 2.1 copy-done.9
  130.8 5.4 %fusion.23 = bf16[192,8,16,128]{3,1,2,0:T(8,128)(2,1)S(1)} fusion(bf16[1,768,2048]{2,1,0:T(8,128)(2,1)S(1)} %copy-done, f32[1536,768]{1,0:T(8,128)S(1)} %fusion.6, f32[1536,768]{1,0:T(8,128)S(1)} %fusion.8), kind=kOutput, calls=%fused_computation.37 | convolution fusion | flops 4842061824 | bytes 18874368 | tf_op jit(solution)/shard_map/dot_general | solution.py:20
  136.2 5.0 %copy.26 = bf16[192,8,16,128]{3,2,1,0:T(8,128)(2,1)} copy(bf16[192,8,16,128]{3,1,2,0:T(8,128)(2,1)S(1)} %fusion.23) | data formatting | bytes 12582912
  141.2 47.0 %all-to-all-done.2 = bf16[128,12,16,128]{3,2,1,0:T(8,128)(2,1)} async-done(((bf16[128,12,16,128]{3,2,1,0:T(8,128)(2,1)}), bf16[128,12,16,128]{3,2,1,0:T(8,128)(2,1)}, u32[]{:S(2)}, u32[]{:S(2)}) %all-to-all-start.2) | async-done | bytes 6291488 | tf_op jit(solution)/shard_map/all_to_all | solution.py:124
  188.2 5.7 %all-to-all-start.1 = ((bf16[128,12,16,128]{3,2,1,0:T(8,128)(2,1)}), bf16[128,12,16,128]{3,2,1,0:T(8,128)(2,1)}, u32[]{:S(2)}, u32[]{:S(2)}) async-start(bf16[128,12,16,128]{3,2,1,0:T(8,128)(2,1)} %bitcast.68), calls=%async_computation.1 | async-start | bytes 12582912 | tf_op jit(solution)/shard_map/all_to_all | solution.py:128
  193.9 8.1 %fusion.3 = f32[1536,768]{1,0:T(8,128)S(1)} fusion(bf16[192,8,16,128]{3,2,1,0:T(8,128)(2,1)} %bitcast.26, bf16[1,768,2048]{2,1,0:T(8,128)(2,1)S(1)} %copy-done), kind=kOutput, calls=%fused_computation.11 | convolution fusion | flops 4831838208 | bytes 14155776 | tf_op jit(solution)/shard_map/dot_general | solution.py:25
  202.1 2.2 copy-done.10
  204.3 14.7 %fusion.17 = f32[1536,2048]{1,0:T(8,128)} fusion(bf16[1,2048,768]{2,1,0:T(8,128)(2,1)S(1)} %copy-done.5, f32[1536,768]{1,0:T(8,128)} %copy-done.8, f32[1536,768]{1,0:T(8,128)S(1)} %fusion.3, f32[1536,768]{1,0:T(8,128)} %copy-done.9), kind=kOutput, calls=%fused_computation.33 | convolution fusion | flops 4843634688 | bytes 29884416 | tf_op jit(solution)/shard_map/dot_general | solution.py:30
  218.9 11.3 %fusion.20 = bf16[192,8,16,128]{3,1,2,0:T(8,128)(2,1)S(1)} fusion(f32[1536,2048]{1,0:T(8,128)} %fusion.17, bf16[1,2048,768]{2,1,0:T(8,128)(2,1)S(1)} %copy-done.7, f32[1536,768]{1,0:T(8,128)} %copy-done.10, f32[1536,768]{1,0:T(8,128)} %copy-done.8), kind=kOutput, calls=%fused_computation.36 | convolution fusion | flops 4845207552 | bytes 31457280 | tf_op jit(solution)/shard_map/dot_general | solution.py:33
  230.2 5.0 %copy.30 = bf16[192,8,16,128]{3,2,1,0:T(8,128)(2,1)} copy(bf16[192,8,16,128]{3,1,2,0:T(8,128)(2,1)S(1)} %fusion.20) | data formatting | bytes 12582912
  235.2 37.0 %all-to-all-done.1 = bf16[128,12,16,128]{3,2,1,0:T(8,128)(2,1)} async-done(((bf16[128,12,16,128]{3,2,1,0:T(8,128)(2,1)}), bf16[128,12,16,128]{3,2,1,0:T(8,128)(2,1)}, u32[]{:S(2)}, u32[]{:S(2)}) %all-to-all-start.1) | async-done | bytes 6291488 | tf_op jit(solution)/shard_map/all_to_all | solution.py:128
  272.1 5.7 %all-to-all-start.3 = ((bf16[128,12,16,128]{3,2,1,0:T(8,128)(2,1)}), bf16[128,12,16,128]{3,2,1,0:T(8,128)(2,1)}, u32[]{:S(2)}, u32[]{:S(2)}) async-start(bf16[128,12,16,128]{3,2,1,0:T(8,128)(2,1)} %bitcast.67), calls=%async_computation.3 | async-start | bytes 12582912 | tf_op jit(solution)/shard_map/all_to_all | solution.py:132
  277.8 0.1 convert_bitcast_fusion
  277.9 0.2 copy.32
  278.2 11.2 %gather_fusion = bf16[1024,16,128]{2,1,0:T(8,128)(2,1)} fusion(bf16[1536,16,128]{2,1,0:T(8,128)(2,1)} %bitcast.4, s32[1024]{0:T(1024)S(1)} %broadcast_clamp_fusion), kind=kCustom, calls=%fused_computation | custom fusion | bytes 8392704 | tf_op jit(solution)/shard_map/gather | solution.py:136
  289.3 4.6 %fusion.2 = f32[128,8]{1,0:T(8,128)S(1)} fusion(bf16[128,8,16,128]{3,2,1,0:T(8,128)(2,1)} %bitcast.65, f32[128,16,128]{2,1,0:T(8,128)S(1)} %bitcast.70), kind=kLoop, calls=%fused_computation.9 | loop fusion | flops 6290432 | bytes 5246976 | tf_op jit(solution)/shard_map/reduce_sum | solution.py:142
  293.9 0.7 copy.23
  294.6 3.5 fusion.1
  298.1 0.9 copy.48
  299.0 57.0 %all-to-all-done.3 = bf16[128,12,16,128]{3,2,1,0:T(8,128)(2,1)} async-done(((bf16[128,12,16,128]{3,2,1,0:T(8,128)(2,1)}), bf16[128,12,16,128]{3,2,1,0:T(8,128)(2,1)}, u32[]{:S(2)}, u32[]{:S(2)}) %all-to-all-start.3) | async-done | bytes 6291488 | tf_op jit(solution)/shard_map/all_to_all | solution.py:132
  356.0 4.9 %shard_map.113 = bf16[128,16,128]{2,1,0:T(8,128)(2,1)} custom-call(s32[1024]{0:T(1024)} %copy-done.3, bf16[1536,16,128]{2,1,0:T(8,128)(2,1)} %bitcast.9.rows_ref), custom_call_target="tpu_custom_call" | custom-call | tf_op jit(solution)/shard_map/pallas_call | solution.py:50
  360.9 2.0 copy.47
  (25 shorter events, 0.1 us)
Async XLA Ops:
  0.6 130.2 %copy-start = (bf16[1,768,2048]{2,1,0:T(8,128)(2,1)S(1)}, bf16[1,768,2048]{2,1,0:T(8,128)(2,1)}, u32[]{:S(2)}) copy-start(bf16[1,768,2048]{2,1,0:T(8,128)(2,1)} %param.17) | copy-start | bytes 9437188
  4.8 273.3 %copy-start.3 = (s32[1024]{0:T(1024)}, s32[1024]{0:T(1024)S(1)}, u32[]{:S(2)}) copy-start(s32[1024]{0:T(1024)S(1)} %multiply_add_fusion.place_ref) | copy-start | bytes 12292
  15.0 11.0 %copy-start.4 = (f32[128,8]{0,1:T(8,128)S(1)}, f32[128,8]{0,1:T(8,128)}, u32[]{:S(2)}) copy-start(f32[128,8]{0,1:T(8,128)} %param.11) | copy-start | bytes 12292
  15.1 89.2 %all-to-all-start = ((bf16[128,12,16,128]{3,2,1,0:T(8,128)(2,1)}), bf16[128,12,16,128]{3,2,1,0:T(8,128)(2,1)}, u32[]{:S(2)}, u32[]{:S(2)}) async-start(bf16[128,12,16,128]{3,2,1,0:T(8,128)(2,1)} %bitcast.66), calls=%async_computation | async-start | bytes 12582912 | tf_op jit(solution)/shard_map/all_to_all | solution.py:123
  104.2 84.0 %all-to-all-start.2 = ((bf16[128,12,16,128]{3,2,1,0:T(8,128)(2,1)}), bf16[128,12,16,128]{3,2,1,0:T(8,128)(2,1)}, u32[]{:S(2)}, u32[]{:S(2)}) async-start(bf16[128,12,16,128]{3,2,1,0:T(8,128)(2,1)} %fusion), calls=%async_computation.2 | async-start | bytes 12582912 | tf_op jit(solution)/shard_map/all_to_all | solution.py:124
  110.0 9.1 %copy-start.6 = (bf16[1,2048,768]{2,1,0:T(8,128)(2,1)S(1)}, bf16[1,2048,768]{2,1,0:T(8,128)(2,1)}, u32[]{:S(2)}) copy-start(bf16[1,2048,768]{2,1,0:T(8,128)(2,1)} %param.16) | copy-start | bytes 9437188
  119.1 9.6 %copy-start.8 = (f32[1536,768]{1,0:T(8,128)}, f32[1536,768]{1,0:T(8,128)S(1)}, u32[]{:S(2)}) copy-start(f32[1536,768]{1,0:T(8,128)S(1)} %fusion.8) | copy-start | bytes 14155780
  128.7 2.1 copy-start.9
  188.2 83.9 %all-to-all-start.1 = ((bf16[128,12,16,128]{3,2,1,0:T(8,128)(2,1)}), bf16[128,12,16,128]{3,2,1,0:T(8,128)(2,1)}, u32[]{:S(2)}, u32[]{:S(2)}) async-start(bf16[128,12,16,128]{3,2,1,0:T(8,128)(2,1)} %bitcast.68), calls=%async_computation.1 | async-start | bytes 12582912 | tf_op jit(solution)/shard_map/all_to_all | solution.py:128
  193.9 10.3 %copy-start.5 = (bf16[1,2048,768]{2,1,0:T(8,128)(2,1)S(1)}, bf16[1,2048,768]{2,1,0:T(8,128)(2,1)}, u32[]{:S(2)}) copy-start(bf16[1,2048,768]{2,1,0:T(8,128)(2,1)} %param.15) | copy-start | bytes 9437188
  202.1 2.2 copy-start.10
  204.3 14.7 %copy-start.7 = (bf16[1,2048,768]{2,1,0:T(8,128)(2,1)S(1)}, bf16[1,2048,768]{2,1,0:T(8,128)(2,1)}, u32[]{:S(2)}) copy-start(bf16[1,2048,768]{2,1,0:T(8,128)(2,1)} %param.16) | copy-start | bytes 9437188
  272.1 5.7 %copy-start.2 = (bf16[128,2048]{1,0:T(8,128)(2,1)S(1)}, bf16[128,2048]{1,0:T(8,128)(2,1)}, u32[]{:S(2)}) copy-start(bf16[128,2048]{1,0:T(8,128)(2,1)} %param.10) | copy-start | bytes 1572868
  272.1 83.9 %all-to-all-start.3 = ((bf16[128,12,16,128]{3,2,1,0:T(8,128)(2,1)}), bf16[128,12,16,128]{3,2,1,0:T(8,128)(2,1)}, u32[]{:S(2)}, u32[]{:S(2)}) async-start(bf16[128,12,16,128]{3,2,1,0:T(8,128)(2,1)} %bitcast.67), calls=%async_computation.3 | async-start | bytes 12582912 | tf_op jit(solution)/shard_map/all_to_all | solution.py:132
  294.6 68.4 %copy-start.1 = (bf16[1,768,2048]{2,1,0:T(8,128)(2,1)S(1)}, bf16[1,768,2048]{2,1,0:T(8,128)(2,1)}, u32[]{:S(2)}) copy-start(bf16[1,768,2048]{2,1,0:T(8,128)(2,1)} %param.17) | copy-start | bytes 9437188

commit v9 on v8

--- a/solution.py
+++ b/solution.py
@@ -58,28 +58,39 @@
     )(place, rows)
 
 
-def gather_tiles(row_of, src3, block):
+def gather_tiles(row_of, src3, block, scale=None):
     total = row_of.shape[0]
 
-    def kernel(row_ref, src_ref, out_ref):
+    def kernel(row_ref, *refs):
+        if scale is None:
+            src_ref, out_ref = refs
+        else:
+            scale_ref, src_ref, out_ref = refs
         base = pl.program_id(0) * block
 
         def one_slot(i, carry):
-            out_ref[i] = src_ref[row_ref[base + i]]
+            if scale is None:
+                out_ref[i] = src_ref[row_ref[base + i]]
+            else:
+                row = src_ref[row_ref[base + i]].astype(jnp.float32) * scale_ref[base + i]
+                out_ref[i] = row.astype(out_ref.dtype)
             return carry
 
         lax.fori_loop(0, block, one_slot, 0, unroll=8)
 
+    src_spec = pl.BlockSpec(src3.shape, lambda g, rows: (0, 0, 0))
+    in_specs = [src_spec] if scale is None else [pl.BlockSpec(memory_space=pltpu.SMEM), src_spec]
+    operands = (row_of, src3) if scale is None else (row_of, scale, src3)
     return pl.pallas_call(
         kernel,
         out_shape=jax.ShapeDtypeStruct((total,) + src3.shape[1:], src3.dtype),
         grid_spec=pltpu.PrefetchScalarGridSpec(
             num_scalar_prefetch=1,
             grid=(total // block,),
-            in_specs=[pl.BlockSpec(src3.shape, lambda g, rows: (0, 0, 0))],
+            in_specs=in_specs,
             out_specs=pl.BlockSpec((block,) + src3.shape[1:], lambda g, rows: (g, 0, 0)),
         ),
-    )(row_of, src3)
+    )(*operands)
 
 
 def body(tokens, cotangent, gates, experts, owner, swapped, w_gate, w_up, w_down):
@@ -106,20 +117,17 @@
     rank = jnp.sum(earlier.astype(jnp.int32), axis=1)
     place = target * slots + rank
     slot_ids = jnp.arange(count * slots, dtype=jnp.int32)
-    source = jnp.min(
-        jnp.where(place[None, :] == slot_ids[:, None], pair_ids[None, :], pairs), axis=1
-    )
+    match = place[None, :] == slot_ids[:, None]
+    source = jnp.min(jnp.where(match, pair_ids[None, :], pairs), axis=1)
+    gate_slot = jnp.sum(jnp.where(match, gates.reshape(-1)[None, :], 0.0), axis=1)
     row_of = source // top_count
-    tok_pad = jnp.concatenate([tokens, jnp.zeros((1, width), jnp.bfloat16)], axis=0)
-    cot_pad = jnp.concatenate([cotangent, jnp.zeros((1, width), jnp.bfloat16)], axis=0)
-    gate_pad = jnp.concatenate([gates.reshape(-1), jnp.zeros((1,), jnp.float32)], axis=0)
-    tok3 = tok_pad.reshape(tok_rows + 1, sub, LANES)
-    cot3 = cot_pad.reshape(tok_rows + 1, sub, LANES)
+    row_clamped = jnp.minimum(row_of, tok_rows - 1)
     send_x = gather_tiles(
-        jnp.minimum(row_of, tok_rows - 1), tokens.reshape(tok_rows, sub, LANES), 256
+        row_clamped, tokens.reshape(tok_rows, sub, LANES), 256
     ).reshape(count, slots, sub, LANES)
-    send_c = (cot3[row_of].astype(jnp.float32) * gate_pad[source][:, None, None]).astype(jnp.bfloat16)
-    send_c = send_c.reshape(count, slots, sub, LANES)
+    send_c = gather_tiles(
+        row_clamped, cotangent.reshape(tok_rows, sub, LANES), 256, gate_slot
+    ).reshape(count, slots, sub, LANES)
     recv_x = lax.all_to_all(send_x, "ep", split_axis=0, concat_axis=0, tiled=True)
     recv_c = lax.all_to_all(send_c, "ep", split_axis=0, concat_axis=0, tiled=True)
     flat = recv_x.reshape(-1, width)

time: 364 us -> 364 us (level)
  local copies, waits for them, and re-layouts: 50.2 us -> 33.5 us
  waiting for transfers between devices: 194 us -> 209 us
  Pallas kernels: 11.7 us -> 19.2 us
  other arithmetic: 20.4 us -> 15 us
    gather x2 -> x0, local copies, waits for them, and re-layouts: 15.8 us -> none  [the longest x1 8.39 us: body(): gate_pad[source][:, None, None]]
    all_to_all x1, waiting for transfers between devices: 52.5 us -> 67.3 us  [body(): lax.all_to_all(send_x, 'ep', split_axis=0, concat_axis=0, tiled=True)]
    pallas_call x1 -> x2, Pallas kernels: 6.78 us -> 14.3 us  [gather_tiles(): pl.pallas_call(kernel, out_shape=jax.ShapeDtypeStruct((total,) + src3.sha...]
    convert_element_type x1, other arithmetic: 7.37 us -> 0.11 us  [body(): cot_f = cotangent.reshape(tok_rows, 1, sub, LANES).astype(jnp.float32)]
    unnamed x32 -> x29, local copies, waits for them, and re-layouts: 21 us -> 19.7 us
  transfers between devices with their start and end apart: 4 -> 4, of which waited for: 4 -> 4; matrix products, arithmetic and copies ran while one was open for 32% -> 25% of each run, Pallas kernels for 0% -> 2%
where the time goes in v9:
time: 364 us; the launch traced here: 363 us
  waiting for transfers between devices  209 us (57%)
  matrix products  58.1 us (16%)
  local copies, waits for them, and re-layouts  33.5 us (9%)
  starting transfers between devices  28.1 us (8%)
  Pallas kernels  19.2 us (5%)
  other arithmetic  15 us (4%)
    all_to_all x1, waiting for transfers between devices, body(): lax.all_to_all(send_x, 'ep', split_axis=0, concat_axis=0, tiled=True)  67.3 us
    all_to_all x1, waiting for transfers between devices, body(): lax.all_to_all(pair_grad.reshape(count, slots, sub, LANES), 'ep', split_a...  57.4 us
    all_to_all x1, waiting for transfers between devices, body(): lax.all_to_all(send_c, 'ep', split_axis=0, concat_axis=0, tiled=True)  47.1 us
    all_to_all x1, waiting for transfers between devices, body(): lax.all_to_all(out_rows.reshape(count, slots, sub, LANES), 'ep', split_ax...  36.9 us
    unnamed x29, local copies, waits for them, and re-layouts  19.7 us
    dot_general x1, matrix products, project_back(): lax.dot_general(grad_a, wg, (((1,), (1,)), ((), ())), preferred_element_t...  14.7 us
    pallas_call x2, Pallas kernels, gather_tiles(): pl.pallas_call(kernel, out_shape=jax.ShapeDtypeStruct((total,) + src3.sha...  14.3 us
    dot_general x1, matrix products, project_back(): lax.dot_general(grad_b, wu, (((1,), (1,)), ((), ())), preferred_element_t...  11.3 us
  transfers between devices with their start and end apart: 4, of which 4 were waited for; matrix products, arithmetic and copies ran while one was open for 25% of the time, Pallas kernels for 2%

profile of v9, /device:TPU:27, one launch (start us, length us, event | category | flops | bytes accessed | tf_op | source)
XLA Modules:
  0.0 363.4 jit_solution(14603706622642135669)
XLA Ops:
  0.6 0.0 copy-start
  0.6 0.8 and_select_fusion.1
  1.5 0.9 select_reduce_fusion.3
  2.3 0.7 fusion.34
  3.0 0.8 copy.21
  3.8 0.1 eq.28
  3.9 0.4 select_reduce_fusion.2
  4.3 0.5 convert_reduce_fusion
  4.8 0.9 select_reduce_fusion.1
  5.7 0.6 fusion.29.row_ref
  6.3 1.9 copy.24
  8.3 6.8 %shard_map.112 = bf16[1536,16,128]{2,1,0:T(8,128)(2,1)} custom-call(s32[1536]{0:T(1024)} %fusion.29.row_ref, bf16[128,16,128]{2,1,0:T(8,128)(2,1)} %bitcast.67), custom_call_target="tpu_custom_call" | custom-call | tf_op jit(solution)/shard_map/pallas_call | solution.py:84
  15.1 10.9 %all-to-all-start = ((bf16[128,12,16,128]{3,2,1,0:T(8,128)(2,1)}), bf16[128,12,16,128]{3,2,1,0:T(8,128)(2,1)}, u32[]{:S(2)}, u32[]{:S(2)}) async-start(bf16[128,12,16,128]{3,2,1,0:T(8,128)(2,1)} %bitcast.63), calls=%async_computation | async-start | bytes 12582912 | tf_op jit(solution)/shard_map/all_to_all | solution.py:131
  26.0 0.0 copy-done.4
  26.1 0.1 copy.20
  26.2 0.1 broadcast_in_dim.70
  26.3 2.0 copy.28
  28.2 1.3 select_reduce_fusion.refs_0_
  29.5 7.5 %shard_map.113 = bf16[1536,16,128]{2,1,0:T(8,128)(2,1)} custom-call(s32[1536]{0:T(1024)} %fusion.29.row_ref, f32[1536]{0:T(1024)} %select_reduce_fusion.refs_0_, bf16[128,16,128]{2,1,0:T(8,128)(2,1)} %bitcast.64), custom_call_target="tpu_custom_call" | custom-call | tf_op jit(solution)/shard_map/pallas_call | solution.py:84
  37.0 67.3 %all-to-all-done = bf16[128,12,16,128]{3,2,1,0:T(8,128)(2,1)} async-done(((bf16[128,12,16,128]{3,2,1,0:T(8,128)(2,1)}), bf16[128,12,16,128]{3,2,1,0:T(8,128)(2,1)}, u32[]{:S(2)}, u32[]{:S(2)}) %all-to-all-start) | async-done | bytes 6291488 | tf_op jit(solution)/shard_map/all_to_all | solution.py:131
  104.3 5.8 %all-to-all-start.2 = ((bf16[128,12,16,128]{3,2,1,0:T(8,128)(2,1)}), bf16[128,12,16,128]{3,2,1,0:T(8,128)(2,1)}, u32[]{:S(2)}, u32[]{:S(2)}) async-start(bf16[128,12,16,128]{3,2,1,0:T(8,128)(2,1)} %bitcast.62), calls=%async_computation.2 | async-start | bytes 12582912 | tf_op jit(solution)/shard_map/all_to_all | solution.py:132
  110.1 0.0 copy-start.6
  110.1 9.0 %fusion.7 = f32[1536,768]{1,0:T(8,128)S(1)} fusion(bf16[192,8,16,128]{3,2,1,0:T(8,128)(2,1)} %bitcast.14, bf16[1,2048,768]{2,1,0:T(8,128)(2,1)} %param.15), kind=kOutput, calls=%fused_computation.12 | convolution fusion | flops 4831838208 | bytes 14155776 | tf_op jit(solution)/shard_map/dot_general | solution.py:12
  119.1 9.6 %fusion.5 = f32[1536,768]{1,0:T(8,128)S(1)} fusion(bf16[192,8,16,128]{3,2,1,0:T(8,128)(2,1)} %bitcast.14, bf16[1,2048,768]{2,1,0:T(8,128)(2,1)S(1)} %copy-done.6), kind=kOutput, calls=%fused_computation.10 | convolution fusion | flops 4831838208 | bytes 14155776 | tf_op jit(solution)/shard_map/dot_general | solution.py:13
  128.8 2.1 copy-done.9
  130.9 0.0 copy-done
  130.9 5.4 %fusion.22 = bf16[192,8,16,128]{3,1,2,0:T(8,128)(2,1)S(1)} fusion(bf16[1,768,2048]{2,1,0:T(8,128)(2,1)S(1)} %copy-done, f32[1536,768]{1,0:T(8,128)S(1)} %fusion.5, f32[1536,768]{1,0:T(8,128)S(1)} %fusion.7), kind=kOutput, calls=%fused_computation.34 | convolution fusion | flops 4842061824 | bytes 18874368 | tf_op jit(solution)/shard_map/dot_general | solution.py:20
  136.3 4.9 %copy.26 = bf16[192,8,16,128]{3,2,1,0:T(8,128)(2,1)} copy(bf16[192,8,16,128]{3,1,2,0:T(8,128)(2,1)S(1)} %fusion.22) | data formatting | bytes 12582912
  141.2 47.1 %all-to-all-done.2 = bf16[128,12,16,128]{3,2,1,0:T(8,128)(2,1)} async-done(((bf16[128,12,16,128]{3,2,1,0:T(8,128)(2,1)}), bf16[128,12,16,128]{3,2,1,0:T(8,128)(2,1)}, u32[]{:S(2)}, u32[]{:S(2)}) %all-to-all-start.2) | async-done | bytes 6291488 | tf_op jit(solution)/shard_map/all_to_all | solution.py:132
  188.3 5.7 %all-to-all-start.1 = ((bf16[128,12,16,128]{3,2,1,0:T(8,128)(2,1)}), bf16[128,12,16,128]{3,2,1,0:T(8,128)(2,1)}, u32[]{:S(2)}, u32[]{:S(2)}) async-start(bf16[128,12,16,128]{3,2,1,0:T(8,128)(2,1)} %bitcast.61), calls=%async_computation.1 | async-start | bytes 12582912 | tf_op jit(solution)/shard_map/all_to_all | solution.py:136
  194.0 0.0 copy-start.5
  194.0 8.1 %fusion.2 = f32[1536,768]{1,0:T(8,128)S(1)} fusion(bf16[192,8,16,128]{3,2,1,0:T(8,128)(2,1)} %bitcast.24, bf16[1,768,2048]{2,1,0:T(8,128)(2,1)S(1)} %copy-done), kind=kOutput, calls=%fused_computation.7 | convolution fusion | flops 4831838208 | bytes 14155776 | tf_op jit(solution)/shard_map/dot_general | solution.py:25
  202.1 0.0 copy-start.10
  202.1 2.1 copy-done.10
  204.3 14.7 %fusion.16 = f32[1536,2048]{1,0:T(8,128)} fusion(bf16[1,2048,768]{2,1,0:T(8,128)(2,1)S(1)} %copy-done.5, f32[1536,768]{1,0:T(8,128)} %copy-done.8, f32[1536,768]{1,0:T(8,128)S(1)} %fusion.2, f32[1536,768]{1,0:T(8,128)} %copy-done.9), kind=kOutput, calls=%fused_computation.30 | convolution fusion | flops 4843634688 | bytes 29884416 | tf_op jit(solution)/shard_map/dot_general | solution.py:30
  219.0 11.3 %fusion.19 = bf16[192,8,16,128]{3,1,2,0:T(8,128)(2,1)S(1)} fusion(f32[1536,2048]{1,0:T(8,128)} %fusion.16, bf16[1,2048,768]{2,1,0:T(8,128)(2,1)S(1)} %copy-done.7, f32[1536,768]{1,0:T(8,128)} %copy-done.10, f32[1536,768]{1,0:T(8,128)} %copy-done.8), kind=kOutput, calls=%fused_computation.33 | convolution fusion | flops 4845207552 | bytes 31457280 | tf_op jit(solution)/shard_map/dot_general | solution.py:33
  230.2 5.0 %copy.30 = bf16[192,8,16,128]{3,2,1,0:T(8,128)(2,1)} copy(bf16[192,8,16,128]{3,1,2,0:T(8,128)(2,1)S(1)} %fusion.19) | data formatting | bytes 12582912
  235.2 36.9 %all-to-all-done.1 = bf16[128,12,16,128]{3,2,1,0:T(8,128)(2,1)} async-done(((bf16[128,12,16,128]{3,2,1,0:T(8,128)(2,1)}), bf16[128,12,16,128]{3,2,1,0:T(8,128)(2,1)}, u32[]{:S(2)}, u32[]{:S(2)}) %all-to-all-start.1) | async-done | bytes 6291488 | tf_op jit(solution)/shard_map/all_to_all | solution.py:136
  272.2 5.7 %all-to-all-start.3 = ((bf16[128,12,16,128]{3,2,1,0:T(8,128)(2,1)}), bf16[128,12,16,128]{3,2,1,0:T(8,128)(2,1)}, u32[]{:S(2)}, u32[]{:S(2)}) async-start(bf16[128,12,16,128]{3,2,1,0:T(8,128)(2,1)} %bitcast.60), calls=%async_computation.3 | async-start | bytes 12582912 | tf_op jit(solution)/shard_map/all_to_all | solution.py:140
  277.9 0.0 copy-done.2
  277.9 0.1 bitcast_convert_fusion
  278.0 11.2 %gather_fusion = bf16[1024,16,128]{2,1,0:T(8,128)(2,1)} fusion(bf16[1536,16,128]{2,1,0:T(8,128)(2,1)} %bitcast.4, s32[1024]{0:T(1024)S(1)} %broadcast_clamp_fusion), kind=kCustom, calls=%fused_computation | custom fusion | bytes 8392704 | tf_op jit(solution)/shard_map/gather | solution.py:144
  289.2 4.6 %fusion.1 = f32[128,8]{1,0:T(8,128)S(1)} fusion(bf16[128,8,16,128]{3,2,1,0:T(8,128)(2,1)} %bitcast.59, f32[128,16,128]{2,1,0:T(8,128)S(1)} %bitcast_convert_fusion), kind=kLoop, calls=%fused_computation.5 | loop fusion | flops 6290432 | bytes 5246976 | tf_op jit(solution)/shard_map/reduce_sum | solution.py:150
  293.7 0.7 copy.23
  294.4 4.3 %fusion = bf16[128,16,128]{2,1,0:T(8,128)(2,1)} fusion(f32[128,8]{1,0:T(8,128)S(1)} %copy.20, bf16[1024,16,128]{2,1,0:T(8,128)(2,1)} %gather_fusion), kind=kLoop, calls=%fused_computation.4 | loop fusion | flops 6029312 | bytes 4722688 | tf_op jit(solution)/shard_map/reduce_sum | solution.py:148
  298.7 57.4 %all-to-all-done.3 = bf16[128,12,16,128]{3,2,1,0:T(8,128)(2,1)} async-done(((bf16[128,12,16,128]{3,2,1,0:T(8,128)(2,1)}), bf16[128,12,16,128]{3,2,1,0:T(8,128)(2,1)}, u32[]{:S(2)}, u32[]{:S(2)}) %all-to-all-start.3) | async-done | bytes 6291488 | tf_op jit(solution)/shard_map/all_to_all | solution.py:140
  356.1 4.9 %shard_map.114 = bf16[128,16,128]{2,1,0:T(8,128)(2,1)} custom-call(s32[1024]{0:T(1024)} %copy-done.3, bf16[1536,16,128]{2,1,0:T(8,128)(2,1)} %bitcast.9.rows_ref), custom_call_target="tpu_custom_call" | custom-call | tf_op jit(solution)/shard_map/pallas_call | solution.py:50
  361.0 2.4 copy_bitcast_fusion
  (16 shorter events, 0.0 us)
Async XLA Ops:
  0.6 130.3 %copy-start = (bf16[1,768,2048]{2,1,0:T(8,128)(2,1)S(1)}, bf16[1,768,2048]{2,1,0:T(8,128)(2,1)}, u32[]{:S(2)}) copy-start(bf16[1,768,2048]{2,1,0:T(8,128)(2,1)} %param.17) | copy-start | bytes 9437188
  4.8 273.1 %copy-start.3 = (s32[1024]{0:T(1024)}, s32[1024]{0:T(1024)S(1)}, u32[]{:S(2)}) copy-start(s32[1024]{0:T(1024)S(1)} %multiply_add_fusion.place_ref) | copy-start | bytes 12292
  15.1 11.0 %copy-start.4 = (f32[128,8]{0,1:T(8,128)S(1)}, f32[128,8]{0,1:T(8,128)}, u32[]{:S(2)}) copy-start(f32[128,8]{0,1:T(8,128)} %param.11) | copy-start | bytes 12292
  15.1 89.2 %all-to-all-start = ((bf16[128,12,16,128]{3,2,1,0:T(8,128)(2,1)}), bf16[128,12,16,128]{3,2,1,0:T(8,128)(2,1)}, u32[]{:S(2)}, u32[]{:S(2)}) async-start(bf16[128,12,16,128]{3,2,1,0:T(8,128)(2,1)} %bitcast.63), calls=%async_computation | async-start | bytes 12582912 | tf_op jit(solution)/shard_map/all_to_all | solution.py:131
  104.3 84.0 %all-to-all-start.2 = ((bf16[128,12,16,128]{3,2,1,0:T(8,128)(2,1)}), bf16[128,12,16,128]{3,2,1,0:T(8,128)(2,1)}, u32[]{:S(2)}, u32[]{:S(2)}) async-start(bf16[128,12,16,128]{3,2,1,0:T(8,128)(2,1)} %bitcast.62), calls=%async_computation.2 | async-start | bytes 12582912 | tf_op jit(solution)/shard_map/all_to_all | solution.py:132
  110.1 9.1 %copy-start.6 = (bf16[1,2048,768]{2,1,0:T(8,128)(2,1)S(1)}, bf16[1,2048,768]{2,1,0:T(8,128)(2,1)}, u32[]{:S(2)}) copy-start(bf16[1,2048,768]{2,1,0:T(8,128)(2,1)} %param.16) | copy-start | bytes 9437188
  119.1 9.6 %copy-start.8 = (f32[1536,768]{1,0:T(8,128)}, f32[1536,768]{1,0:T(8,128)S(1)}, u32[]{:S(2)}) copy-start(f32[1536,768]{1,0:T(8,128)S(1)} %fusion.7) | copy-start | bytes 14155780
  128.8 2.1 copy-start.9
  188.3 83.9 %all-to-all-start.1 = ((bf16[128,12,16,128]{3,2,1,0:T(8,128)(2,1)}), bf16[128,12,16,128]{3,2,1,0:T(8,128)(2,1)}, u32[]{:S(2)}, u32[]{:S(2)}) async-start(bf16[128,12,16,128]{3,2,1,0:T(8,128)(2,1)} %bitcast.61), calls=%async_computation.1 | async-start | bytes 12582912 | tf_op jit(solution)/shard_map/all_to_all | solution.py:136
  194.0 10.3 %copy-start.5 = (bf16[1,2048,768]{2,1,0:T(8,128)(2,1)S(1)}, bf16[1,2048,768]{2,1,0:T(8,128)(2,1)}, u32[]{:S(2)}) copy-start(bf16[1,2048,768]{2,1,0:T(8,128)(2,1)} %param.15) | copy-start | bytes 9437188
  202.1 2.1 copy-start.10
  204.3 14.7 %copy-start.7 = (bf16[1,2048,768]{2,1,0:T(8,128)(2,1)S(1)}, bf16[1,2048,768]{2,1,0:T(8,128)(2,1)}, u32[]{:S(2)}) copy-start(bf16[1,2048,768]{2,1,0:T(8,128)(2,1)} %param.16) | copy-start | bytes 9437188
  272.2 5.7 %copy-start.2 = (bf16[16,8,16,128]{3,2,1,0:T(8,128)(2,1)S(1)}, bf16[16,8,16,128]{3,2,1,0:T(8,128)(2,1)}, u32[]{:S(2)}) copy-start(bf16[16,8,16,128]{3,2,1,0:T(8,128)(2,1)} %copy.28) | copy-start | bytes 1572868
  272.2 83.9 %all-to-all-start.3 = ((bf16[128,12,16,128]{3,2,1,0:T(8,128)(2,1)}), bf16[128,12,16,128]{3,2,1,0:T(8,128)(2,1)}, u32[]{:S(2)}, u32[]{:S(2)}) async-start(bf16[128,12,16,128]{3,2,1,0:T(8,128)(2,1)} %bitcast.60), calls=%async_computation.3 | async-start | bytes 12582912 | tf_op jit(solution)/shard_map/all_to_all | solution.py:140
  294.4 69.0 %copy-start.1 = (bf16[1,768,2048]{2,1,0:T(8,128)(2,1)S(1)}, bf16[1,768,2048]{2,1,0:T(8,128)(2,1)}, u32[]{:S(2)}) copy-start(bf16[1,768,2048]{2,1,0:T(8,128)(2,1)} %param.17) | copy-start | bytes 9437188

commit v10 on v9

--- a/solution.py
+++ b/solution.py
@@ -45,7 +45,7 @@
             out_ref[t] = acc.astype(out_ref.dtype)
             return carry
 
-        lax.fori_loop(0, tok_rows, one_token, 0, unroll=4)
+        lax.fori_loop(0, tok_rows, one_token, 0, unroll=8)
 
     return pl.pallas_call(
         kernel,
@@ -76,7 +76,7 @@
                 out_ref[i] = row.astype(out_ref.dtype)
             return carry
 
-        lax.fori_loop(0, block, one_slot, 0, unroll=8)
+        lax.fori_loop(0, block, one_slot, 0, unroll=16)
 
     src_spec = pl.BlockSpec(src3.shape, lambda g, rows: (0, 0, 0))
     in_specs = [src_spec] if scale is None else [pl.BlockSpec(memory_space=pltpu.SMEM), src_spec]

time: 364 us -> 364 us (level)
  no operation moved by 1% of the time
where the time goes in v10:
time: 364 us; the launch traced here: 363 us
  waiting for transfers between devices  209 us (57%)
  matrix products  58.1 us (16%)
  local copies, waits for them, and re-layouts  33.5 us (9%)
  starting transfers between devices  28.1 us (8%)
  Pallas kernels  18.3 us (5%)
  other arithmetic  15 us (4%)
    all_to_all x1, waiting for transfers between devices, body(): lax.all_to_all(send_x, 'ep', split_axis=0, concat_axis=0, tiled=True)  67.8 us
    all_to_all x1, waiting for transfers between devices, body(): lax.all_to_all(pair_grad.reshape(count, slots, sub, LANES), 'ep', split_a...  57.4 us
    all_to_all x1, waiting for transfers between devices, body(): lax.all_to_all(send_c, 'ep', split_axis=0, concat_axis=0, tiled=True)  47.1 us
    all_to_all x1, waiting for transfers between devices, body(): lax.all_to_all(out_rows.reshape(count, slots, sub, LANES), 'ep', split_ax...  37 us
    unnamed x29, local copies, waits for them, and re-layouts  19.7 us
    dot_general x1, matrix products, project_back(): lax.dot_general(grad_a, wg, (((1,), (1,)), ((), ())), preferred_element_t...  14.7 us
    pallas_call x2, Pallas kernels, gather_tiles(): pl.pallas_call(kernel, out_shape=jax.ShapeDtypeStruct((total,) + src3.sha...  13.5 us
    dot_general x1, matrix products, project_back(): lax.dot_general(grad_b, wu, (((1,), (1,)), ((), ())), preferred_element_t...  11.3 us
  transfers between devices with their start and end apart: 4, of which 4 were waited for; matrix products, arithmetic and copies ran while one was open for 25% of the time, Pallas kernels for 2%

profile of v10, /device:TPU:27, one launch (start us, length us, event | category | flops | bytes accessed | tf_op | source)
XLA Modules:
  0.0 363.0 jit_solution(13965931314412755280)
XLA Ops:
  0.6 0.0 copy-start
  0.6 0.8 and_select_fusion.1
  1.5 0.9 select_reduce_fusion.3
  2.3 0.7 fusion.34
  3.0 0.8 copy.21
  3.8 0.1 eq.28
  3.9 0.4 select_reduce_fusion.2
  4.3 0.5 convert_reduce_fusion
  4.8 0.9 select_reduce_fusion.1
  5.7 0.6 fusion.29.row_ref
  6.3 1.9 copy.24
  8.3 6.5 %shard_map.112 = bf16[1536,16,128]{2,1,0:T(8,128)(2,1)} custom-call(s32[1536]{0:T(1024)} %fusion.29.row_ref, bf16[128,16,128]{2,1,0:T(8,128)(2,1)} %bitcast.67), custom_call_target="tpu_custom_call" | custom-call | tf_op jit(solution)/shard_map/pallas_call | solution.py:84
  14.8 10.9 %all-to-all-start = ((bf16[128,12,16,128]{3,2,1,0:T(8,128)(2,1)}), bf16[128,12,16,128]{3,2,1,0:T(8,128)(2,1)}, u32[]{:S(2)}, u32[]{:S(2)}) async-start(bf16[128,12,16,128]{3,2,1,0:T(8,128)(2,1)} %bitcast.63), calls=%async_computation | async-start | bytes 12582912 | tf_op jit(solution)/shard_map/all_to_all | solution.py:131
  25.8 0.1 copy.20
  25.9 0.1 broadcast_in_dim.70
  26.0 2.0 copy.28
  27.9 1.3 select_reduce_fusion.refs_0_
  29.2 7.0 %shard_map.113 = bf16[1536,16,128]{2,1,0:T(8,128)(2,1)} custom-call(s32[1536]{0:T(1024)} %fusion.29.row_ref, f32[1536]{0:T(1024)} %select_reduce_fusion.refs_0_, bf16[128,16,128]{2,1,0:T(8,128)(2,1)} %bitcast.64), custom_call_target="tpu_custom_call" | custom-call | tf_op jit(solution)/shard_map/pallas_call | solution.py:84
  36.2 67.8 %all-to-all-done = bf16[128,12,16,128]{3,2,1,0:T(8,128)(2,1)} async-done(((bf16[128,12,16,128]{3,2,1,0:T(8,128)(2,1)}), bf16[128,12,16,128]{3,2,1,0:T(8,128)(2,1)}, u32[]{:S(2)}, u32[]{:S(2)}) %all-to-all-start) | async-done | bytes 6291488 | tf_op jit(solution)/shard_map/all_to_all | solution.py:131
  104.0 5.8 %all-to-all-start.2 = ((bf16[128,12,16,128]{3,2,1,0:T(8,128)(2,1)}), bf16[128,12,16,128]{3,2,1,0:T(8,128)(2,1)}, u32[]{:S(2)}, u32[]{:S(2)}) async-start(bf16[128,12,16,128]{3,2,1,0:T(8,128)(2,1)} %bitcast.62), calls=%async_computation.2 | async-start | bytes 12582912 | tf_op jit(solution)/shard_map/all_to_all | solution.py:132
  109.8 0.0 copy-start.6
  109.8 9.0 %fusion.7 = f32[1536,768]{1,0:T(8,128)S(1)} fusion(bf16[192,8,16,128]{3,2,1,0:T(8,128)(2,1)} %bitcast.14, bf16[1,2048,768]{2,1,0:T(8,128)(2,1)} %param.15), kind=kOutput, calls=%fused_computation.12 | convolution fusion | flops 4831838208 | bytes 14155776 | tf_op jit(solution)/shard_map/dot_general | solution.py:12
  118.9 9.6 %fusion.5 = f32[1536,768]{1,0:T(8,128)S(1)} fusion(bf16[192,8,16,128]{3,2,1,0:T(8,128)(2,1)} %bitcast.14, bf16[1,2048,768]{2,1,0:T(8,128)(2,1)S(1)} %copy-done.6), kind=kOutput, calls=%fused_computation.10 | convolution fusion | flops 4831838208 | bytes 14155776 | tf_op jit(solution)/shard_map/dot_general | solution.py:13
  128.5 0.0 copy-done.8
  128.5 0.0 copy-start.9
  128.5 2.1 copy-done.9
  130.6 5.4 %fusion.22 = bf16[192,8,16,128]{3,1,2,0:T(8,128)(2,1)S(1)} fusion(bf16[1,768,2048]{2,1,0:T(8,128)(2,1)S(1)} %copy-done, f32[1536,768]{1,0:T(8,128)S(1)} %fusion.5, f32[1536,768]{1,0:T(8,128)S(1)} %fusion.7), kind=kOutput, calls=%fused_computation.34 | convolution fusion | flops 4842061824 | bytes 18874368 | tf_op jit(solution)/shard_map/dot_general | solution.py:20
  136.0 4.9 %copy.26 = bf16[192,8,16,128]{3,2,1,0:T(8,128)(2,1)} copy(bf16[192,8,16,128]{3,1,2,0:T(8,128)(2,1)S(1)} %fusion.22) | data formatting | bytes 12582912
  140.9 47.1 %all-to-all-done.2 = bf16[128,12,16,128]{3,2,1,0:T(8,128)(2,1)} async-done(((bf16[128,12,16,128]{3,2,1,0:T(8,128)(2,1)}), bf16[128,12,16,128]{3,2,1,0:T(8,128)(2,1)}, u32[]{:S(2)}, u32[]{:S(2)}) %all-to-all-start.2) | async-done | bytes 6291488 | tf_op jit(solution)/shard_map/all_to_all | solution.py:132
  188.0 5.7 %all-to-all-start.1 = ((bf16[128,12,16,128]{3,2,1,0:T(8,128)(2,1)}), bf16[128,12,16,128]{3,2,1,0:T(8,128)(2,1)}, u32[]{:S(2)}, u32[]{:S(2)}) async-start(bf16[128,12,16,128]{3,2,1,0:T(8,128)(2,1)} %bitcast.61), calls=%async_computation.1 | async-start | bytes 12582912 | tf_op jit(solution)/shard_map/all_to_all | solution.py:136
  193.7 0.0 copy-start.5
  193.7 8.1 %fusion.2 = f32[1536,768]{1,0:T(8,128)S(1)} fusion(bf16[192,8,16,128]{3,2,1,0:T(8,128)(2,1)} %bitcast.24, bf16[1,768,2048]{2,1,0:T(8,128)(2,1)S(1)} %copy-done), kind=kOutput, calls=%fused_computation.7 | convolution fusion | flops 4831838208 | bytes 14155776 | tf_op jit(solution)/shard_map/dot_general | solution.py:25
  201.8 2.1 copy-done.10
  204.0 0.0 copy-done.5
  204.0 14.7 %fusion.16 = f32[1536,2048]{1,0:T(8,128)} fusion(bf16[1,2048,768]{2,1,0:T(8,128)(2,1)S(1)} %copy-done.5, f32[1536,768]{1,0:T(8,128)} %copy-done.8, f32[1536,768]{1,0:T(8,128)S(1)} %fusion.2, f32[1536,768]{1,0:T(8,128)} %copy-done.9), kind=kOutput, calls=%fused_computation.30 | convolution fusion | flops 4843634688 | bytes 29884416 | tf_op jit(solution)/shard_map/dot_general | solution.py:30
  218.7 11.3 %fusion.19 = bf16[192,8,16,128]{3,1,2,0:T(8,128)(2,1)S(1)} fusion(f32[1536,2048]{1,0:T(8,128)} %fusion.16, bf16[1,2048,768]{2,1,0:T(8,128)(2,1)S(1)} %copy-done.7, f32[1536,768]{1,0:T(8,128)} %copy-done.10, f32[1536,768]{1,0:T(8,128)} %copy-done.8), kind=kOutput, calls=%fused_computation.33 | convolution fusion | flops 4845207552 | bytes 31457280 | tf_op jit(solution)/shard_map/dot_general | solution.py:33
  229.9 5.0 %copy.30 = bf16[192,8,16,128]{3,2,1,0:T(8,128)(2,1)} copy(bf16[192,8,16,128]{3,1,2,0:T(8,128)(2,1)S(1)} %fusion.19) | data formatting | bytes 12582912
  234.9 37.0 %all-to-all-done.1 = bf16[128,12,16,128]{3,2,1,0:T(8,128)(2,1)} async-done(((bf16[128,12,16,128]{3,2,1,0:T(8,128)(2,1)}), bf16[128,12,16,128]{3,2,1,0:T(8,128)(2,1)}, u32[]{:S(2)}, u32[]{:S(2)}) %all-to-all-start.1) | async-done | bytes 6291488 | tf_op jit(solution)/shard_map/all_to_all | solution.py:136
  271.9 5.7 %all-to-all-start.3 = ((bf16[128,12,16,128]{3,2,1,0:T(8,128)(2,1)}), bf16[128,12,16,128]{3,2,1,0:T(8,128)(2,1)}, u32[]{:S(2)}, u32[]{:S(2)}) async-start(bf16[128,12,16,128]{3,2,1,0:T(8,128)(2,1)} %bitcast.60), calls=%async_computation.3 | async-start | bytes 12582912 | tf_op jit(solution)/shard_map/all_to_all | solution.py:140
  277.6 0.0 copy-done.3
  277.6 0.1 bitcast_convert_fusion
  277.7 11.2 %gather_fusion = bf16[1024,16,128]{2,1,0:T(8,128)(2,1)} fusion(bf16[1536,16,128]{2,1,0:T(8,128)(2,1)} %bitcast.4, s32[1024]{0:T(1024)S(1)} %broadcast_clamp_fusion), kind=kCustom, calls=%fused_computation | custom fusion | bytes 8392704 | tf_op jit(solution)/shard_map/gather | solution.py:144
  288.9 4.6 %fusion.1 = f32[128,8]{1,0:T(8,128)S(1)} fusion(bf16[128,8,16,128]{3,2,1,0:T(8,128)(2,1)} %bitcast.59, f32[128,16,128]{2,1,0:T(8,128)S(1)} %bitcast_convert_fusion), kind=kLoop, calls=%fused_computation.5 | loop fusion | flops 6290432 | bytes 5246976 | tf_op jit(solution)/shard_map/reduce_sum | solution.py:150
  293.5 0.7 copy.23
  294.1 4.3 %fusion = bf16[128,16,128]{2,1,0:T(8,128)(2,1)} fusion(f32[128,8]{1,0:T(8,128)S(1)} %copy.20, bf16[1024,16,128]{2,1,0:T(8,128)(2,1)} %gather_fusion), kind=kLoop, calls=%fused_computation.4 | loop fusion | flops 6029312 | bytes 4722688 | tf_op jit(solution)/shard_map/reduce_sum | solution.py:148
  298.4 57.4 %all-to-all-done.3 = bf16[128,12,16,128]{3,2,1,0:T(8,128)(2,1)} async-done(((bf16[128,12,16,128]{3,2,1,0:T(8,128)(2,1)}), bf16[128,12,16,128]{3,2,1,0:T(8,128)(2,1)}, u32[]{:S(2)}, u32[]{:S(2)}) %all-to-all-start.3) | async-done | bytes 6291488 | tf_op jit(solution)/shard_map/all_to_all | solution.py:140
  355.8 4.8 %shard_map.114 = bf16[128,16,128]{2,1,0:T(8,128)(2,1)} custom-call(s32[1024]{0:T(1024)} %copy-done.3, bf16[1536,16,128]{2,1,0:T(8,128)(2,1)} %bitcast.9.rows_ref), custom_call_target="tpu_custom_call" | custom-call | tf_op jit(solution)/shard_map/pallas_call | solution.py:50
  360.6 2.4 copy_bitcast_fusion
  (16 shorter events, 0.0 us)
Async XLA Ops:
  0.6 130.0 %copy-start = (bf16[1,768,2048]{2,1,0:T(8,128)(2,1)S(1)}, bf16[1,768,2048]{2,1,0:T(8,128)(2,1)}, u32[]{:S(2)}) copy-start(bf16[1,768,2048]{2,1,0:T(8,128)(2,1)} %param.17) | copy-start | bytes 9437188
  4.8 272.8 %copy-start.3 = (s32[1024]{0:T(1024)}, s32[1024]{0:T(1024)S(1)}, u32[]{:S(2)}) copy-start(s32[1024]{0:T(1024)S(1)} %multiply_add_fusion.place_ref) | copy-start | bytes 12292
  14.8 11.0 %copy-start.4 = (f32[128,8]{0,1:T(8,128)S(1)}, f32[128,8]{0,1:T(8,128)}, u32[]{:S(2)}) copy-start(f32[128,8]{0,1:T(8,128)} %param.11) | copy-start | bytes 12292
  14.8 89.2 %all-to-all-start = ((bf16[128,12,16,128]{3,2,1,0:T(8,128)(2,1)}), bf16[128,12,16,128]{3,2,1,0:T(8,128)(2,1)}, u32[]{:S(2)}, u32[]{:S(2)}) async-start(bf16[128,12,16,128]{3,2,1,0:T(8,128)(2,1)} %bitcast.63), calls=%async_computation | async-start | bytes 12582912 | tf_op jit(solution)/shard_map/all_to_all | solution.py:131
  104.0 84.0 %all-to-all-start.2 = ((bf16[128,12,16,128]{3,2,1,0:T(8,128)(2,1)}), bf16[128,12,16,128]{3,2,1,0:T(8,128)(2,1)}, u32[]{:S(2)}, u32[]{:S(2)}) async-start(bf16[128,12,16,128]{3,2,1,0:T(8,128)(2,1)} %bitcast.62), calls=%async_computation.2 | async-start | bytes 12582912 | tf_op jit(solution)/shard_map/all_to_all | solution.py:132
  109.8 9.1 %copy-start.6 = (bf16[1,2048,768]{2,1,0:T(8,128)(2,1)S(1)}, bf16[1,2048,768]{2,1,0:T(8,128)(2,1)}, u32[]{:S(2)}) copy-start(bf16[1,2048,768]{2,1,0:T(8,128)(2,1)} %param.16) | copy-start | bytes 9437188
  118.8 9.6 %copy-start.8 = (f32[1536,768]{1,0:T(8,128)}, f32[1536,768]{1,0:T(8,128)S(1)}, u32[]{:S(2)}) copy-start(f32[1536,768]{1,0:T(8,128)S(1)} %fusion.7) | copy-start | bytes 14155780
  128.5 2.1 copy-start.9
  188.0 83.9 %all-to-all-start.1 = ((bf16[128,12,16,128]{3,2,1,0:T(8,128)(2,1)}), bf16[128,12,16,128]{3,2,1,0:T(8,128)(2,1)}, u32[]{:S(2)}, u32[]{:S(2)}) async-start(bf16[128,12,16,128]{3,2,1,0:T(8,128)(2,1)} %bitcast.61), calls=%async_computation.1 | async-start | bytes 12582912 | tf_op jit(solution)/shard_map/all_to_all | solution.py:136
  193.7 10.3 %copy-start.5 = (bf16[1,2048,768]{2,1,0:T(8,128)(2,1)S(1)}, bf16[1,2048,768]{2,1,0:T(8,128)(2,1)}, u32[]{:S(2)}) copy-start(bf16[1,2048,768]{2,1,0:T(8,128)(2,1)} %param.15) | copy-start | bytes 9437188
  201.8 2.1 copy-start.10
  204.0 14.7 %copy-start.7 = (bf16[1,2048,768]{2,1,0:T(8,128)(2,1)S(1)}, bf16[1,2048,768]{2,1,0:T(8,128)(2,1)}, u32[]{:S(2)}) copy-start(bf16[1,2048,768]{2,1,0:T(8,128)(2,1)} %param.16) | copy-start | bytes 9437188
  271.9 5.7 %copy-start.2 = (bf16[16,8,16,128]{3,2,1,0:T(8,128)(2,1)S(1)}, bf16[16,8,16,128]{3,2,1,0:T(8,128)(2,1)}, u32[]{:S(2)}) copy-start(bf16[16,8,16,128]{3,2,1,0:T(8,128)(2,1)} %copy.28) | copy-start | bytes 1572868
  271.9 83.9 %all-to-all-start.3 = ((bf16[128,12,16,128]{3,2,1,0:T(8,128)(2,1)}), bf16[128,12,16,128]{3,2,1,0:T(8,128)(2,1)}, u32[]{:S(2)}, u32[]{:S(2)}) async-start(bf16[128,12,16,128]{3,2,1,0:T(8,128)(2,1)} %bitcast.60), calls=%async_computation.3 | async-start | bytes 12582912 | tf_op jit(solution)/shard_map/all_to_all | solution.py:140
  294.1 68.9 %copy-start.1 = (bf16[1,768,2048]{2,1,0:T(8,128)(2,1)S(1)}, bf16[1,768,2048]{2,1,0:T(8,128)(2,1)}, u32[]{:S(2)}) copy-start(bf16[1,768,2048]{2,1,0:T(8,128)(2,1)} %param.17) | copy-start | bytes 9437188

commit v11 on v10

--- a/solution.py
+++ b/solution.py
@@ -39,9 +39,9 @@
 def combine_rows(place, rows, tok_rows, top_count):
     def kernel(place_ref, rows_ref, out_ref):
         def one_token(t, carry):
-            acc = rows_ref[place_ref[t * top_count]].astype(jnp.float32)
+            acc = rows_ref[place_ref[t]].astype(jnp.float32)
             for k in range(1, top_count):
-                acc = acc + rows_ref[place_ref[t * top_count + k]].astype(jnp.float32)
+                acc = acc + rows_ref[place_ref[k * tok_rows + t]].astype(jnp.float32)
             out_ref[t] = acc.astype(out_ref.dtype)
             return carry
 
@@ -109,7 +109,7 @@
     wg = w_gate[0]
     wu = w_up[0]
     wd = w_down[0]
-    flat_e = experts.reshape(-1)
+    flat_e = experts.T.reshape(-1)
     chosen = flat_e[:, None] == jnp.arange(expert_total, dtype=jnp.int32)[None, :]
     target = jnp.sum(jnp.where(chosen, holder[None, :], 0), axis=1)
     pair_ids = jnp.arange(pairs, dtype=jnp.int32)
@@ -119,8 +119,8 @@
     slot_ids = jnp.arange(count * slots, dtype=jnp.int32)
     match = place[None, :] == slot_ids[:, None]
     source = jnp.min(jnp.where(match, pair_ids[None, :], pairs), axis=1)
-    gate_slot = jnp.sum(jnp.where(match, gates.reshape(-1)[None, :], 0.0), axis=1)
-    row_of = source // top_count
+    gate_slot = jnp.sum(jnp.where(match, gates.T.reshape(-1)[None, :], 0.0), axis=1)
+    row_of = source % tok_rows
     row_clamped = jnp.minimum(row_of, tok_rows - 1)
     send_x = gather_tiles(
         row_clamped, tokens.reshape(tok_rows, sub, LANES), 256
@@ -142,12 +142,12 @@
     )
     out_pairs = (
         back.reshape(-1, sub, LANES)[place]
-        .reshape(tok_rows, top_count, sub, LANES)
+        .reshape(top_count, tok_rows, sub, LANES)
         .astype(jnp.float32)
     )
-    mixed = jnp.sum(gates[:, :, None, None] * out_pairs, axis=1).astype(jnp.bfloat16)
-    cot_f = cotangent.reshape(tok_rows, 1, sub, LANES).astype(jnp.float32)
-    gate_grad = jnp.sum(cot_f * out_pairs, axis=(2, 3))
+    mixed = jnp.sum(gates.T[:, :, None, None] * out_pairs, axis=0).astype(jnp.bfloat16)
+    cot_f = cotangent.reshape(1, tok_rows, sub, LANES).astype(jnp.float32)
+    gate_grad = jnp.sum(cot_f * out_pairs, axis=(2, 3)).T
     in_grad = combine_rows(place, grad_back.reshape(-1, sub, LANES), tok_rows, top_count)
     return (mixed.reshape(tok_rows, width), in_grad.reshape(tok_rows, width), gate_grad)
 

time: 364 us -> 420 us (1.15)
  waiting for transfers between devices: 209 us -> 263 us
  local copies, waits for them, and re-layouts: 33.5 us -> 26.6 us
  matrix products: 58.1 us -> 63.3 us
    all_to_all x1, waiting for transfers between devices: 37 us -> 72.3 us  [body(): lax.all_to_all(out_rows.reshape(count, slots, sub, LANES), 'ep', split_ax...]
    all_to_all x1, waiting for transfers between devices: 47.1 us -> 59.4 us  [body(): lax.all_to_all(send_c, 'ep', split_axis=0, concat_axis=0, tiled=True)]
    all_to_all x1, waiting for transfers between devices: 57.4 us -> 63.7 us  [body(): lax.all_to_all(pair_grad.reshape(count, slots, sub, LANES), 'ep', split_a...]
    unnamed x29 -> x26, local copies, waits for them, and re-layouts: 19.7 us -> 14 us
    reduce_sum x3 -> x2, other arithmetic: 10.1 us -> 11.8 us  [the longest x1 10.5 us: body(): gate_grad = jnp.sum(cot_f * out_pairs, axis=(2, 3)).T]
  transfers between devices with their start and end apart: 4 -> 4, of which waited for: 4 -> 4; matrix products, arithmetic and copies ran while one was open for 25% -> 9% of each run, Pallas kernels for 2% -> 3%
where the time goes in v11:
time: 420 us; the launch traced here: 419 us
  waiting for transfers between devices  263 us (63%)
  matrix products  63.3 us (15%)
  starting transfers between devices  28.2 us (7%)
  local copies, waits for them, and re-layouts  26.6 us (6%)
  other arithmetic  18.4 us (4%)
  Pallas kernels  18.2 us (4%)
    all_to_all x1, waiting for transfers between devices, body(): lax.all_to_all(out_rows.reshape(count, slots, sub, LANES), 'ep', split_ax...  72.3 us
    all_to_all x1, waiting for transfers between devices, body(): lax.all_to_all(send_x, 'ep', split_axis=0, concat_axis=0, tiled=True)  68 us
    all_to_all x1, waiting for transfers between devices, body(): lax.all_to_all(pair_grad.reshape(count, slots, sub, LANES), 'ep', split_a...  63.7 us
    all_to_all x1, waiting for transfers between devices, body(): lax.all_to_all(send_c, 'ep', split_axis=0, concat_axis=0, tiled=True)  59.4 us
    unnamed x26, local copies, waits for them, and re-layouts  14 us
    pallas_call x2, Pallas kernels, gather_tiles(): pl.pallas_call(kernel, out_shape=jax.ShapeDtypeStruct((total,) + src3.sha...  13.4 us
    dot_general x1, matrix products, project_back(): lax.dot_general(grad_a, wg, (((1,), (1,)), ((), ())), preferred_element_t...  13.3 us
    gather x1, local copies, waits for them, and re-layouts, body(): back.reshape(-1, sub, LANES)[place].reshape(top_count, tok_rows, sub, LANES)  11.4 us
  transfers between devices with their start and end apart: 4, of which 4 were waited for; matrix products, arithmetic and copies ran while one was open for 9% of the time, Pallas kernels for 3%

profile of v11, /device:TPU:27, one launch (start us, length us, event | category | flops | bytes accessed | tf_op | source)
XLA Modules:
  0.0 419.0 jit_solution(10841074981885873435)
XLA Ops:
  0.6 0.0 copy-start
  0.6 0.8 and_select_fusion.1
  1.5 0.9 select_reduce_fusion.3
  2.3 0.7 fusion.33
  3.0 1.0 select_reduce_fusion.2
  4.1 0.5 convert_reduce_fusion
  4.6 0.0 copy-start.4
  4.6 0.9 select_reduce_fusion.1
  5.5 0.6 fusion.29.row_ref
  6.1 1.9 copy.12
  8.1 6.5 %shard_map.112 = bf16[1536,16,128]{2,1,0:T(8,128)(2,1)} custom-call(s32[1536]{0:T(1024)} %fusion.29.row_ref, bf16[128,16,128]{2,1,0:T(8,128)(2,1)} %bitcast.72), custom_call_target="tpu_custom_call" | custom-call | tf_op jit(solution)/shard_map/pallas_call | solution.py:84
  14.5 0.0 copy-start.5
  14.5 10.9 %all-to-all-start = ((bf16[128,12,16,128]{3,2,1,0:T(8,128)(2,1)}), bf16[128,12,16,128]{3,2,1,0:T(8,128)(2,1)}, u32[]{:S(2)}, u32[]{:S(2)}) async-start(bf16[128,12,16,128]{3,2,1,0:T(8,128)(2,1)} %bitcast.67), calls=%async_computation | async-start | bytes 12582912 | tf_op jit(solution)/shard_map/all_to_all | solution.py:131
  25.5 2.0 copy.16
  27.5 0.0 copy-done.5
  27.5 1.3 select_reduce_fusion.refs_0_
  28.8 7.0 %shard_map.113 = bf16[1536,16,128]{2,1,0:T(8,128)(2,1)} custom-call(s32[1536]{0:T(1024)} %fusion.29.row_ref, f32[1536]{0:T(1024)} %select_reduce_fusion.refs_0_, bf16[128,16,128]{2,1,0:T(8,128)(2,1)} %bitcast.70), custom_call_target="tpu_custom_call" | custom-call | tf_op jit(solution)/shard_map/pallas_call | solution.py:84
  35.7 68.0 %all-to-all-done = bf16[128,12,16,128]{3,2,1,0:T(8,128)(2,1)} async-done(((bf16[128,12,16,128]{3,2,1,0:T(8,128)(2,1)}), bf16[128,12,16,128]{3,2,1,0:T(8,128)(2,1)}, u32[]{:S(2)}, u32[]{:S(2)}) %all-to-all-start) | async-done | bytes 6291488 | tf_op jit(solution)/shard_map/all_to_all | solution.py:131
  103.7 5.8 %all-to-all-start.2 = ((bf16[128,12,16,128]{3,2,1,0:T(8,128)(2,1)}), bf16[128,12,16,128]{3,2,1,0:T(8,128)(2,1)}, u32[]{:S(2)}, u32[]{:S(2)}) async-start(bf16[128,12,16,128]{3,2,1,0:T(8,128)(2,1)} %bitcast.66), calls=%async_computation.2 | async-start | bytes 12582912 | tf_op jit(solution)/shard_map/all_to_all | solution.py:132
  109.5 0.0 copy-done
  109.5 0.0 copy-start.6
  109.5 9.4 %fusion.7 = f32[1536,768]{1,0:T(8,128)} fusion(bf16[192,8,16,128]{3,2,1,0:T(8,128)(2,1)} %bitcast.21, bf16[1,2048,768]{2,1,0:T(8,128)(2,1)S(1)} %copy-done), kind=kOutput, calls=%fused_computation.12 | convolution fusion | flops 4831838208 | bytes 14155776 | tf_op jit(solution)/shard_map/dot_general | solution.py:12
  119.0 0.0 copy-done.6
  119.0 9.3 %fusion.5 = f32[1536,768]{1,0:T(8,128)} fusion(bf16[192,8,16,128]{3,2,1,0:T(8,128)(2,1)} %bitcast.21, bf16[1,2048,768]{2,1,0:T(8,128)(2,1)S(1)} %copy-done.6), kind=kOutput, calls=%fused_computation.10 | convolution fusion | flops 4831838208 | bytes 14155776 | tf_op jit(solution)/shard_map/dot_general | solution.py:13
  128.3 59.4 %all-to-all-done.2 = bf16[128,12,16,128]{3,2,1,0:T(8,128)(2,1)} async-done(((bf16[128,12,16,128]{3,2,1,0:T(8,128)(2,1)}), bf16[128,12,16,128]{3,2,1,0:T(8,128)(2,1)}, u32[]{:S(2)}, u32[]{:S(2)}) %all-to-all-start.2) | async-done | bytes 6291488 | tf_op jit(solution)/shard_map/all_to_all | solution.py:132
  187.7 10.6 %fusion.2 = f32[1536,768]{1,0:T(8,128)} fusion(bf16[192,8,16,128]{3,2,1,0:T(8,128)(2,1)} %bitcast.31, bf16[1,768,2048]{2,1,0:T(8,128)(2,1)} %param.17), kind=kOutput, calls=%fused_computation.7 | convolution fusion | flops 4831838208 | bytes 14155776 | tf_op jit(solution)/shard_map/dot_general | solution.py:25
  198.3 0.0 copy-done.9
  198.3 0.0 copy-done.10
  198.3 13.3 %fusion.16 = f32[1536,2048]{1,0:T(8,128)} fusion(bf16[1,2048,768]{2,1,0:T(8,128)(2,1)S(1)} %copy-done, f32[1536,768]{1,0:T(8,128)S(1)} %copy-done.9, f32[1536,768]{1,0:T(8,128)} %fusion.2, f32[1536,768]{1,0:T(8,128)S(1)} %copy-done.10), kind=kOutput, calls=%fused_computation.30 | convolution fusion | flops 4843634688 | bytes 29884416 | tf_op jit(solution)/shard_map/dot_general | solution.py:30
  211.6 0.0 copy-done.7
  211.6 11.3 %fusion.19 = bf16[192,8,16,128]{3,1,2,0:T(8,128)(2,1)S(1)} fusion(f32[1536,2048]{1,0:T(8,128)} %fusion.16, bf16[1,2048,768]{2,1,0:T(8,128)(2,1)S(1)} %copy-done.7, f32[1536,768]{1,0:T(8,128)} %fusion.2, f32[1536,768]{1,0:T(8,128)} %fusion.7), kind=kOutput, calls=%fused_computation.33 | convolution fusion | flops 4845207552 | bytes 31457280 | tf_op jit(solution)/shard_map/dot_general | solution.py:33
  222.9 5.0 %copy.18 = bf16[192,8,16,128]{3,2,1,0:T(8,128)(2,1)} copy(bf16[192,8,16,128]{3,1,2,0:T(8,128)(2,1)S(1)} %fusion.19) | data formatting | bytes 12582912
  227.9 5.7 %all-to-all-start.3 = ((bf16[128,12,16,128]{3,2,1,0:T(8,128)(2,1)}), bf16[128,12,16,128]{3,2,1,0:T(8,128)(2,1)}, u32[]{:S(2)}, u32[]{:S(2)}) async-start(bf16[128,12,16,128]{3,2,1,0:T(8,128)(2,1)} %bitcast.68), calls=%async_computation.3 | async-start | bytes 12582912 | tf_op jit(solution)/shard_map/all_to_all | solution.py:140
  233.6 0.0 copy-done.8
  233.6 9.4 %fusion.22 = bf16[192,8,16,128]{3,1,2,0:T(8,128)(2,1)S(1)} fusion(bf16[1,768,2048]{2,1,0:T(8,128)(2,1)S(1)} %copy-done.8, f32[1536,768]{1,0:T(8,128)} %fusion.5, f32[1536,768]{1,0:T(8,128)} %fusion.7), kind=kOutput, calls=%fused_computation.34 | convolution fusion | flops 4842061824 | bytes 18874368 | tf_op jit(solution)/shard_map/dot_general | solution.py:20
  243.0 5.1 %copy.14 = bf16[192,8,16,128]{3,2,1,0:T(8,128)(2,1)} copy(bf16[192,8,16,128]{3,1,2,0:T(8,128)(2,1)S(1)} %fusion.22) | data formatting | bytes 12582912
  248.0 63.7 %all-to-all-done.3 = bf16[128,12,16,128]{3,2,1,0:T(8,128)(2,1)} async-done(((bf16[128,12,16,128]{3,2,1,0:T(8,128)(2,1)}), bf16[128,12,16,128]{3,2,1,0:T(8,128)(2,1)}, u32[]{:S(2)}, u32[]{:S(2)}) %all-to-all-start.3) | async-done | bytes 6291488 | tf_op jit(solution)/shard_map/all_to_all | solution.py:140
  311.8 5.8 %all-to-all-start.1 = ((bf16[128,12,16,128]{3,2,1,0:T(8,128)(2,1)}), bf16[128,12,16,128]{3,2,1,0:T(8,128)(2,1)}, u32[]{:S(2)}, u32[]{:S(2)}) async-start(bf16[128,12,16,128]{3,2,1,0:T(8,128)(2,1)} %bitcast.65), calls=%async_computation.1 | async-start | bytes 12582912 | tf_op jit(solution)/shard_map/all_to_all | solution.py:136
  317.6 0.0 copy-done.4
  317.6 0.0 copy-done.2
  317.6 1.1 bitcast_convert_fusion
  318.7 4.8 %shard_map.114 = bf16[128,16,128]{2,1,0:T(8,128)(2,1)} custom-call(s32[1024]{0:T(1024)} %copy-done.4, bf16[1536,16,128]{2,1,0:T(8,128)(2,1)} %bitcast.13.rows_ref), custom_call_target="tpu_custom_call" | custom-call | tf_op jit(solution)/shard_map/pallas_call | solution.py:50
  323.5 72.3 %all-to-all-done.1 = bf16[128,12,16,128]{3,2,1,0:T(8,128)(2,1)} async-done(((bf16[128,12,16,128]{3,2,1,0:T(8,128)(2,1)}), bf16[128,12,16,128]{3,2,1,0:T(8,128)(2,1)}, u32[]{:S(2)}, u32[]{:S(2)}) %all-to-all-start.1) | async-done | bytes 6291488 | tf_op jit(solution)/shard_map/all_to_all | solution.py:136
  395.8 11.4 %gather_fusion = bf16[1024,16,128]{2,1,0:T(8,128)(2,1)} fusion(bf16[1536,16,128]{2,1,0:T(8,128)(2,1)} %bitcast.7, s32[1024]{0:T(1024)S(1)} %broadcast_clamp_fusion), kind=kCustom, calls=%fused_computation | custom fusion | bytes 8392704 | tf_op jit(solution)/shard_map/gather | solution.py:144
  407.2 10.5 %fusion.1 = (f32[8,128]{1,0:T(8,128)}, bf16[128,16,128]{2,1,0:T(8,128)(2,1)S(1)}) fusion(bf16[8,128,16,128]{3,2,1,0:T(8,128)(2,1)} %bitcast.69, f32[128,16,128]{2,1,0:T(8,128)} %bitcast_convert_fusion, f32[8,128]{1,0:T(8,128)S(1)} %bitcast.80), kind=kLoop, calls=%fused_computation.5 | loop fusion | flops 10222592 | bytes 5775360 | tf_op jit(solution)/shard_map/reduce_sum | solution.py:150
  417.8 0.0 copy-done.3
  417.8 1.2 copy_bitcast_fusion
  419.0 0.0 copy-done.1
  (10 shorter events, 0.0 us)
Async XLA Ops:
  0.6 108.9 %copy-start = (bf16[1,2048,768]{2,1,0:T(8,128)(2,1)S(1)}, bf16[1,2048,768]{2,1,0:T(8,128)(2,1)}, u32[]{:S(2)}) copy-start(bf16[1,2048,768]{2,1,0:T(8,128)(2,1)} %param.15) | copy-start | bytes 9437188
  4.6 313.0 %copy-start.4 = (s32[1024]{0:T(1024)}, s32[1024]{0:T(1024)S(1)}, u32[]{:S(2)}) copy-start(s32[1024]{0:T(1024)S(1)} %multiply_add_fusion.place_ref) | copy-start | bytes 12292
  14.5 12.9 %copy-start.5 = (f32[128,8]{0,1:T(8,128)S(1)}, f32[128,8]{0,1:T(8,128)}, u32[]{:S(2)}) copy-start(f32[128,8]{0,1:T(8,128)} %param.11) | copy-start | bytes 12292
  14.5 89.2 %all-to-all-start = ((bf16[128,12,16,128]{3,2,1,0:T(8,128)(2,1)}), bf16[128,12,16,128]{3,2,1,0:T(8,128)(2,1)}, u32[]{:S(2)}, u32[]{:S(2)}) async-start(bf16[128,12,16,128]{3,2,1,0:T(8,128)(2,1)} %bitcast.67), calls=%async_computation | async-start | bytes 12582912 | tf_op jit(solution)/shard_map/all_to_all | solution.py:131
  103.7 84.0 %all-to-all-start.2 = ((bf16[128,12,16,128]{3,2,1,0:T(8,128)(2,1)}), bf16[128,12,16,128]{3,2,1,0:T(8,128)(2,1)}, u32[]{:S(2)}, u32[]{:S(2)}) async-start(bf16[128,12,16,128]{3,2,1,0:T(8,128)(2,1)} %bitcast.66), calls=%async_computation.2 | async-start | bytes 12582912 | tf_op jit(solution)/shard_map/all_to_all | solution.py:132
  109.5 9.4 %copy-start.6 = (bf16[1,2048,768]{2,1,0:T(8,128)(2,1)S(1)}, bf16[1,2048,768]{2,1,0:T(8,128)(2,1)}, u32[]{:S(2)}) copy-start(bf16[1,2048,768]{2,1,0:T(8,128)(2,1)} %param.16) | copy-start | bytes 9437188
  187.7 10.6 %copy-start.9 = (f32[1536,768]{1,0:T(8,128)S(1)}, f32[1536,768]{1,0:T(8,128)}, u32[]{:S(2)}) copy-start(f32[1536,768]{1,0:T(8,128)} %fusion.7) | copy-start | bytes 14155780
  187.7 10.6 %copy-start.10 = (f32[1536,768]{1,0:T(8,128)S(1)}, f32[1536,768]{1,0:T(8,128)}, u32[]{:S(2)}) copy-start(f32[1536,768]{1,0:T(8,128)} %fusion.5) | copy-start | bytes 14155780
  198.3 13.3 %copy-start.7 = (bf16[1,2048,768]{2,1,0:T(8,128)(2,1)S(1)}, bf16[1,2048,768]{2,1,0:T(8,128)(2,1)}, u32[]{:S(2)}) copy-start(bf16[1,2048,768]{2,1,0:T(8,128)(2,1)} %param.16) | copy-start | bytes 9437188
  227.9 5.7 %copy-start.8 = (bf16[1,768,2048]{2,1,0:T(8,128)(2,1)S(1)}, bf16[1,768,2048]{2,1,0:T(8,128)(2,1)}, u32[]{:S(2)}) copy-start(bf16[1,768,2048]{2,1,0:T(8,128)(2,1)} %param.17) | copy-start | bytes 9437188
  227.9 83.9 %all-to-all-start.3 = ((bf16[128,12,16,128]{3,2,1,0:T(8,128)(2,1)}), bf16[128,12,16,128]{3,2,1,0:T(8,128)(2,1)}, u32[]{:S(2)}, u32[]{:S(2)}) async-start(bf16[128,12,16,128]{3,2,1,0:T(8,128)(2,1)} %bitcast.68), calls=%async_computation.3 | async-start | bytes 12582912 | tf_op jit(solution)/shard_map/all_to_all | solution.py:140
  311.8 5.8 %copy-start.2 = (bf16[16,8,16,128]{3,2,1,0:T(8,128)(2,1)S(1)}, bf16[16,8,16,128]{3,2,1,0:T(8,128)(2,1)}, u32[]{:S(2)}) copy-start(bf16[16,8,16,128]{3,2,1,0:T(8,128)(2,1)} %copy.16) | copy-start | bytes 1572868
  311.8 84.0 %all-to-all-start.1 = ((bf16[128,12,16,128]{3,2,1,0:T(8,128)(2,1)}), bf16[128,12,16,128]{3,2,1,0:T(8,128)(2,1)}, u32[]{:S(2)}, u32[]{:S(2)}) async-start(bf16[128,12,16,128]{3,2,1,0:T(8,128)(2,1)} %bitcast.65), calls=%async_computation.1 | async-start | bytes 12582912 | tf_op jit(solution)/shard_map/all_to_all | solution.py:136
  395.8 23.2 %copy-start.1 = (bf16[1,2048,768]{2,1,0:T(8,128)(2,1)S(1)}, bf16[1,2048,768]{2,1,0:T(8,128)(2,1)}, u32[]{:S(2)}) copy-start(bf16[1,2048,768]{2,1,0:T(8,128)(2,1)} %param.15) | copy-start | bytes 9437188
  407.2 10.5 %copy-start.3 = (bf16[128,16,128]{2,1,0:T(8,128)(2,1)S(1)}, bf16[128,16,128]{2,1,0:T(8,128)(2,1)}, u32[]{:S(2)}) copy-start(bf16[128,16,128]{2,1,0:T(8,128)(2,1)} %shard_map.114) | copy-start | bytes 1572868

commit v12 on v10

--- a/solution.py
+++ b/solution.py
@@ -38,18 +38,25 @@
 
 def combine_rows(place, rows, tok_rows, top_count):
     def kernel(place_ref, rows_ref, out_ref):
-        def one_token(t, carry):
+        def token_sum(t):
             acc = rows_ref[place_ref[t * top_count]].astype(jnp.float32)
             for k in range(1, top_count):
                 acc = acc + rows_ref[place_ref[t * top_count + k]].astype(jnp.float32)
-            out_ref[t] = acc.astype(out_ref.dtype)
+            return acc
+
+        def one_group(g, carry):
+            base = pl.multiple_of(g * 8, 8)
+            accs = [token_sum(base + j) for j in range(8)]
+            for a in range(accs[0].shape[0]):
+                block = jnp.concatenate([acc[a : a + 1, :] for acc in accs], axis=0)
+                out_ref[pl.ds(base, 8), pl.ds(a * LANES, LANES)] = block
             return carry
 
-        lax.fori_loop(0, tok_rows, one_token, 0, unroll=8)
+        lax.fori_loop(0, tok_rows // 8, one_group, 0)
 
     return pl.pallas_call(
         kernel,
-        out_shape=jax.ShapeDtypeStruct((tok_rows,) + rows.shape[1:], jnp.bfloat16),
+        out_shape=jax.ShapeDtypeStruct((tok_rows, rows.shape[1] * rows.shape[2]), jnp.float32),
         in_specs=[
             pl.BlockSpec(memory_space=pltpu.SMEM),
             pl.BlockSpec(memory_space=pltpu.VMEM),
@@ -148,7 +155,9 @@
     mixed = jnp.sum(gates[:, :, None, None] * out_pairs, axis=1).astype(jnp.bfloat16)
     cot_f = cotangent.reshape(tok_rows, 1, sub, LANES).astype(jnp.float32)
     gate_grad = jnp.sum(cot_f * out_pairs, axis=(2, 3))
-    in_grad = combine_rows(place, grad_back.reshape(-1, sub, LANES), tok_rows, top_count)
+    in_grad = combine_rows(place, grad_back.reshape(-1, sub, LANES), tok_rows, top_count).astype(
+        jnp.bfloat16
+    )
     return (mixed.reshape(tok_rows, width), in_grad.reshape(tok_rows, width), gate_grad)
 
 

time: 364 us -> 364 us (level)
    unnamed x29 -> x30, local copies, waits for them, and re-layouts: 19.7 us -> 20.6 us
where the time goes in v12:
time: 364 us; the launch traced here: 363 us
  waiting for transfers between devices  209 us (57%)
  matrix products  58.1 us (16%)
  local copies, waits for them, and re-layouts  32 us (9%)
  starting transfers between devices  28.1 us (8%)
  Pallas kernels  18.6 us (5%)
  other arithmetic  16.1 us (4%)
    all_to_all x1, waiting for transfers between devices, body(): lax.all_to_all(send_x, 'ep', split_axis=0, concat_axis=0, tiled=True)  67.8 us
    all_to_all x1, waiting for transfers between devices, body(): lax.all_to_all(pair_grad.reshape(count, slots, sub, LANES), 'ep', split_a...  57.4 us
    all_to_all x1, waiting for transfers between devices, body(): lax.all_to_all(send_c, 'ep', split_axis=0, concat_axis=0, tiled=True)  47.1 us
    all_to_all x1, waiting for transfers between devices, body(): lax.all_to_all(out_rows.reshape(count, slots, sub, LANES), 'ep', split_ax...  37 us
    unnamed x30, local copies, waits for them, and re-layouts  20.6 us
    dot_general x1, matrix products, project_back(): lax.dot_general(grad_a, wg, (((1,), (1,)), ((), ())), preferred_element_t...  14.7 us
    pallas_call x2, Pallas kernels, gather_tiles(): pl.pallas_call(kernel, out_shape=jax.ShapeDtypeStruct((total,) + src3.sha...  13.5 us
    dot_general x1, matrix products, project_back(): lax.dot_general(grad_b, wu, (((1,), (1,)), ((), ())), preferred_element_t...  11.3 us
  transfers between devices with their start and end apart: 4, of which 4 were waited for; matrix products, arithmetic and copies ran while one was open for 25% of the time, Pallas kernels for 2%

profile of v12, /device:TPU:27, one launch (start us, length us, event | category | flops | bytes accessed | tf_op | source)
XLA Modules:
  0.0 363.0 jit_solution(13304357859335631737)
XLA Ops:
  0.6 0.0 copy-start
  0.6 0.8 and_select_fusion.1
  1.5 0.9 select_reduce_fusion.3
  2.3 0.7 fusion.34
  3.0 0.8 copy.21
  3.8 0.1 eq.28
  3.9 0.4 select_reduce_fusion.2
  4.3 0.5 convert_reduce_fusion
  4.8 0.9 select_reduce_fusion.1
  5.7 0.6 fusion.29.row_ref
  6.3 1.9 copy.24
  8.3 6.5 %shard_map.112 = bf16[1536,16,128]{2,1,0:T(8,128)(2,1)} custom-call(s32[1536]{0:T(1024)} %fusion.29.row_ref, bf16[128,16,128]{2,1,0:T(8,128)(2,1)} %bitcast.64), custom_call_target="tpu_custom_call" | custom-call | tf_op jit(solution)/shard_map/pallas_call | solution.py:91
  14.8 10.9 %all-to-all-start = ((bf16[128,12,16,128]{3,2,1,0:T(8,128)(2,1)}), bf16[128,12,16,128]{3,2,1,0:T(8,128)(2,1)}, u32[]{:S(2)}, u32[]{:S(2)}) async-start(bf16[128,12,16,128]{3,2,1,0:T(8,128)(2,1)} %bitcast.61), calls=%async_computation | async-start | bytes 12582912 | tf_op jit(solution)/shard_map/all_to_all | solution.py:138
  25.8 0.1 copy.20
  25.9 0.1 broadcast_in_dim.70
  26.0 2.0 copy.28
  27.9 1.3 select_reduce_fusion.refs_0_
  29.2 7.0 %shard_map.113 = bf16[1536,16,128]{2,1,0:T(8,128)(2,1)} custom-call(s32[1536]{0:T(1024)} %fusion.29.row_ref, f32[1536]{0:T(1024)} %select_reduce_fusion.refs_0_, bf16[128,16,128]{2,1,0:T(8,128)(2,1)} %bitcast.62), custom_call_target="tpu_custom_call" | custom-call | tf_op jit(solution)/shard_map/pallas_call | solution.py:91
  36.2 67.8 %all-to-all-done = bf16[128,12,16,128]{3,2,1,0:T(8,128)(2,1)} async-done(((bf16[128,12,16,128]{3,2,1,0:T(8,128)(2,1)}), bf16[128,12,16,128]{3,2,1,0:T(8,128)(2,1)}, u32[]{:S(2)}, u32[]{:S(2)}) %all-to-all-start) | async-done | bytes 6291488 | tf_op jit(solution)/shard_map/all_to_all | solution.py:138
  104.0 5.8 %all-to-all-start.2 = ((bf16[128,12,16,128]{3,2,1,0:T(8,128)(2,1)}), bf16[128,12,16,128]{3,2,1,0:T(8,128)(2,1)}, u32[]{:S(2)}, u32[]{:S(2)}) async-start(bf16[128,12,16,128]{3,2,1,0:T(8,128)(2,1)} %bitcast.60), calls=%async_computation.2 | async-start | bytes 12582912 | tf_op jit(solution)/shard_map/all_to_all | solution.py:139
  109.8 0.0 copy-start.6
  109.8 9.0 %fusion.7 = f32[1536,768]{1,0:T(8,128)S(1)} fusion(bf16[192,8,16,128]{3,2,1,0:T(8,128)(2,1)} %bitcast.14, bf16[1,2048,768]{2,1,0:T(8,128)(2,1)} %param.15), kind=kOutput, calls=%fused_computation.12 | convolution fusion | flops 4831838208 | bytes 14155776 | tf_op jit(solution)/shard_map/dot_general | solution.py:12
  118.9 9.6 %fusion.5 = f32[1536,768]{1,0:T(8,128)S(1)} fusion(bf16[192,8,16,128]{3,2,1,0:T(8,128)(2,1)} %bitcast.14, bf16[1,2048,768]{2,1,0:T(8,128)(2,1)S(1)} %copy-done.6), kind=kOutput, calls=%fused_computation.10 | convolution fusion | flops 4831838208 | bytes 14155776 | tf_op jit(solution)/shard_map/dot_general | solution.py:13
  128.5 0.0 copy-done.8
  128.5 0.0 copy-start.9
  128.5 2.1 copy-done.9
  130.6 5.4 %fusion.22 = bf16[192,8,16,128]{3,1,2,0:T(8,128)(2,1)S(1)} fusion(bf16[1,768,2048]{2,1,0:T(8,128)(2,1)S(1)} %copy-done, f32[1536,768]{1,0:T(8,128)S(1)} %fusion.5, f32[1536,768]{1,0:T(8,128)S(1)} %fusion.7), kind=kOutput, calls=%fused_computation.34 | convolution fusion | flops 4842061824 | bytes 18874368 | tf_op jit(solution)/shard_map/dot_general | solution.py:20
  136.0 4.9 %copy.26 = bf16[192,8,16,128]{3,2,1,0:T(8,128)(2,1)} copy(bf16[192,8,16,128]{3,1,2,0:T(8,128)(2,1)S(1)} %fusion.22) | data formatting | bytes 12582912
  140.9 47.1 %all-to-all-done.2 = bf16[128,12,16,128]{3,2,1,0:T(8,128)(2,1)} async-done(((bf16[128,12,16,128]{3,2,1,0:T(8,128)(2,1)}), bf16[128,12,16,128]{3,2,1,0:T(8,128)(2,1)}, u32[]{:S(2)}, u32[]{:S(2)}) %all-to-all-start.2) | async-done | bytes 6291488 | tf_op jit(solution)/shard_map/all_to_all | solution.py:139
  188.0 5.7 %all-to-all-start.1 = ((bf16[128,12,16,128]{3,2,1,0:T(8,128)(2,1)}), bf16[128,12,16,128]{3,2,1,0:T(8,128)(2,1)}, u32[]{:S(2)}, u32[]{:S(2)}) async-start(bf16[128,12,16,128]{3,2,1,0:T(8,128)(2,1)} %bitcast.59), calls=%async_computation.1 | async-start | bytes 12582912 | tf_op jit(solution)/shard_map/all_to_all | solution.py:143
  193.7 0.0 copy-start.5
  193.7 8.1 %fusion.2 = f32[1536,768]{1,0:T(8,128)S(1)} fusion(bf16[192,8,16,128]{3,2,1,0:T(8,128)(2,1)} %bitcast.24, bf16[1,768,2048]{2,1,0:T(8,128)(2,1)S(1)} %copy-done), kind=kOutput, calls=%fused_computation.7 | convolution fusion | flops 4831838208 | bytes 14155776 | tf_op jit(solution)/shard_map/dot_general | solution.py:25
  201.8 2.1 copy-done.10
  204.0 14.7 %fusion.16 = f32[1536,2048]{1,0:T(8,128)} fusion(bf16[1,2048,768]{2,1,0:T(8,128)(2,1)S(1)} %copy-done.5, f32[1536,768]{1,0:T(8,128)} %copy-done.8, f32[1536,768]{1,0:T(8,128)S(1)} %fusion.2, f32[1536,768]{1,0:T(8,128)} %copy-done.9), kind=kOutput, calls=%fused_computation.30 | convolution fusion | flops 4843634688 | bytes 29884416 | tf_op jit(solution)/shard_map/dot_general | solution.py:30
  218.7 11.3 %fusion.19 = bf16[192,8,16,128]{3,1,2,0:T(8,128)(2,1)S(1)} fusion(f32[1536,2048]{1,0:T(8,128)} %fusion.16, bf16[1,2048,768]{2,1,0:T(8,128)(2,1)S(1)} %copy-done.7, f32[1536,768]{1,0:T(8,128)} %copy-done.10, f32[1536,768]{1,0:T(8,128)} %copy-done.8), kind=kOutput, calls=%fused_computation.33 | convolution fusion | flops 4845207552 | bytes 31457280 | tf_op jit(solution)/shard_map/dot_general | solution.py:33
  229.9 5.0 %copy.30 = bf16[192,8,16,128]{3,2,1,0:T(8,128)(2,1)} copy(bf16[192,8,16,128]{3,1,2,0:T(8,128)(2,1)S(1)} %fusion.19) | data formatting | bytes 12582912
  234.9 37.0 %all-to-all-done.1 = bf16[128,12,16,128]{3,2,1,0:T(8,128)(2,1)} async-done(((bf16[128,12,16,128]{3,2,1,0:T(8,128)(2,1)}), bf16[128,12,16,128]{3,2,1,0:T(8,128)(2,1)}, u32[]{:S(2)}, u32[]{:S(2)}) %all-to-all-start.1) | async-done | bytes 6291488 | tf_op jit(solution)/shard_map/all_to_all | solution.py:143
  271.9 5.7 %all-to-all-start.3 = ((bf16[128,12,16,128]{3,2,1,0:T(8,128)(2,1)}), bf16[128,12,16,128]{3,2,1,0:T(8,128)(2,1)}, u32[]{:S(2)}, u32[]{:S(2)}) async-start(bf16[128,12,16,128]{3,2,1,0:T(8,128)(2,1)} %bitcast.58), calls=%async_computation.3 | async-start | bytes 12582912 | tf_op jit(solution)/shard_map/all_to_all | solution.py:147
  277.6 0.1 bitcast_convert_fusion
  277.7 11.2 %gather_fusion = bf16[1024,16,128]{2,1,0:T(8,128)(2,1)} fusion(bf16[1536,16,128]{2,1,0:T(8,128)(2,1)} %bitcast.4, s32[1024]{0:T(1024)S(1)} %broadcast_clamp_fusion), kind=kCustom, calls=%fused_computation | custom fusion | bytes 8392704 | tf_op jit(solution)/shard_map/gather | solution.py:151
  288.9 4.6 %fusion.1 = f32[128,8]{1,0:T(8,128)S(1)} fusion(bf16[128,8,16,128]{3,2,1,0:T(8,128)(2,1)} %bitcast.57, f32[128,16,128]{2,1,0:T(8,128)S(1)} %bitcast_convert_fusion), kind=kLoop, calls=%fused_computation.5 | loop fusion | flops 6290432 | bytes 5246976 | tf_op jit(solution)/shard_map/reduce_sum | solution.py:157
  293.5 0.7 copy.23
  294.1 3.3 fusion
  297.4 0.0 copy-start.1
  297.5 0.9 copy.44
  298.4 57.4 %all-to-all-done.3 = bf16[128,12,16,128]{3,2,1,0:T(8,128)(2,1)} async-done(((bf16[128,12,16,128]{3,2,1,0:T(8,128)(2,1)}), bf16[128,12,16,128]{3,2,1,0:T(8,128)(2,1)}, u32[]{:S(2)}, u32[]{:S(2)}) %all-to-all-start.3) | async-done | bytes 6291488 | tf_op jit(solution)/shard_map/all_to_all | solution.py:147
  355.8 5.1 %shard_map.114 = f32[128,2048]{1,0:T(8,128)} custom-call(s32[1024]{0:T(1024)} %copy-done.3, bf16[1536,16,128]{2,1,0:T(8,128)(2,1)} %bitcast.9.rows_ref), custom_call_target="tpu_custom_call" | custom-call | tf_op jit(solution)/shard_map/pallas_call | solution.py:57
  360.9 2.1 convert_element_type.56
  (17 shorter events, 0.0 us)
Async XLA Ops:
  0.6 130.0 %copy-start = (bf16[1,768,2048]{2,1,0:T(8,128)(2,1)S(1)}, bf16[1,768,2048]{2,1,0:T(8,128)(2,1)}, u32[]{:S(2)}) copy-start(bf16[1,768,2048]{2,1,0:T(8,128)(2,1)} %param.17) | copy-start | bytes 9437188
  4.8 272.8 %copy-start.3 = (s32[1024]{0:T(1024)}, s32[1024]{0:T(1024)S(1)}, u32[]{:S(2)}) copy-start(s32[1024]{0:T(1024)S(1)} %multiply_add_fusion.place_ref) | copy-start | bytes 12292
  14.8 11.0 %copy-start.4 = (f32[128,8]{0,1:T(8,128)S(1)}, f32[128,8]{0,1:T(8,128)}, u32[]{:S(2)}) copy-start(f32[128,8]{0,1:T(8,128)} %param.11) | copy-start | bytes 12292
  14.8 89.2 %all-to-all-start = ((bf16[128,12,16,128]{3,2,1,0:T(8,128)(2,1)}), bf16[128,12,16,128]{3,2,1,0:T(8,128)(2,1)}, u32[]{:S(2)}, u32[]{:S(2)}) async-start(bf16[128,12,16,128]{3,2,1,0:T(8,128)(2,1)} %bitcast.61), calls=%async_computation | async-start | bytes 12582912 | tf_op jit(solution)/shard_map/all_to_all | solution.py:138
  104.0 84.0 %all-to-all-start.2 = ((bf16[128,12,16,128]{3,2,1,0:T(8,128)(2,1)}), bf16[128,12,16,128]{3,2,1,0:T(8,128)(2,1)}, u32[]{:S(2)}, u32[]{:S(2)}) async-start(bf16[128,12,16,128]{3,2,1,0:T(8,128)(2,1)} %bitcast.60), calls=%async_computation.2 | async-start | bytes 12582912 | tf_op jit(solution)/shard_map/all_to_all | solution.py:139
  109.8 9.1 %copy-start.6 = (bf16[1,2048,768]{2,1,0:T(8,128)(2,1)S(1)}, bf16[1,2048,768]{2,1,0:T(8,128)(2,1)}, u32[]{:S(2)}) copy-start(bf16[1,2048,768]{2,1,0:T(8,128)(2,1)} %param.16) | copy-start | bytes 9437188
  118.8 9.6 %copy-start.8 = (f32[1536,768]{1,0:T(8,128)}, f32[1536,768]{1,0:T(8,128)S(1)}, u32[]{:S(2)}) copy-start(f32[1536,768]{1,0:T(8,128)S(1)} %fusion.7) | copy-start | bytes 14155780
  128.5 2.1 copy-start.9
  188.0 83.9 %all-to-all-start.1 = ((bf16[128,12,16,128]{3,2,1,0:T(8,128)(2,1)}), bf16[128,12,16,128]{3,2,1,0:T(8,128)(2,1)}, u32[]{:S(2)}, u32[]{:S(2)}) async-start(bf16[128,12,16,128]{3,2,1,0:T(8,128)(2,1)} %bitcast.59), calls=%async_computation.1 | async-start | bytes 12582912 | tf_op jit(solution)/shard_map/all_to_all | solution.py:143
  193.7 10.3 %copy-start.5 = (bf16[1,2048,768]{2,1,0:T(8,128)(2,1)S(1)}, bf16[1,2048,768]{2,1,0:T(8,128)(2,1)}, u32[]{:S(2)}) copy-start(bf16[1,2048,768]{2,1,0:T(8,128)(2,1)} %param.15) | copy-start | bytes 9437188
  201.8 2.1 copy-start.10
  204.0 14.7 %copy-start.7 = (bf16[1,2048,768]{2,1,0:T(8,128)(2,1)S(1)}, bf16[1,2048,768]{2,1,0:T(8,128)(2,1)}, u32[]{:S(2)}) copy-start(bf16[1,2048,768]{2,1,0:T(8,128)(2,1)} %param.16) | copy-start | bytes 9437188
  271.9 5.7 %copy-start.2 = (bf16[16,8,16,128]{3,2,1,0:T(8,128)(2,1)S(1)}, bf16[16,8,16,128]{3,2,1,0:T(8,128)(2,1)}, u32[]{:S(2)}) copy-start(bf16[16,8,16,128]{3,2,1,0:T(8,128)(2,1)} %copy.28) | copy-start | bytes 1572868
  271.9 83.9 %all-to-all-start.3 = ((bf16[128,12,16,128]{3,2,1,0:T(8,128)(2,1)}), bf16[128,12,16,128]{3,2,1,0:T(8,128)(2,1)}, u32[]{:S(2)}, u32[]{:S(2)}) async-start(bf16[128,12,16,128]{3,2,1,0:T(8,128)(2,1)} %bitcast.58), calls=%async_computation.3 | async-start | bytes 12582912 | tf_op jit(solution)/shard_map/all_to_all | solution.py:147
  297.4 65.5 %copy-start.1 = (bf16[1,768,2048]{2,1,0:T(8,128)(2,1)S(1)}, bf16[1,768,2048]{2,1,0:T(8,128)(2,1)}, u32[]{:S(2)}) copy-start(bf16[1,768,2048]{2,1,0:T(8,128)(2,1)} %param.17) | copy-start | bytes 9437188

commit v13 on v12

--- a/solution.py
+++ b/solution.py
@@ -45,18 +45,18 @@
             return acc
 
         def one_group(g, carry):
-            base = pl.multiple_of(g * 8, 8)
-            accs = [token_sum(base + j) for j in range(8)]
+            base = pl.multiple_of(g * 16, 16)
+            accs = [token_sum(base + j) for j in range(16)]
             for a in range(accs[0].shape[0]):
                 block = jnp.concatenate([acc[a : a + 1, :] for acc in accs], axis=0)
-                out_ref[pl.ds(base, 8), pl.ds(a * LANES, LANES)] = block
+                out_ref[pl.ds(base, 16), pl.ds(a * LANES, LANES)] = block.astype(out_ref.dtype)
             return carry
 
-        lax.fori_loop(0, tok_rows // 8, one_group, 0)
+        lax.fori_loop(0, tok_rows // 16, one_group, 0)
 
     return pl.pallas_call(
         kernel,
-        out_shape=jax.ShapeDtypeStruct((tok_rows, rows.shape[1] * rows.shape[2]), jnp.float32),
+        out_shape=jax.ShapeDtypeStruct((tok_rows, rows.shape[1] * rows.shape[2]), jnp.bfloat16),
         in_specs=[
             pl.BlockSpec(memory_space=pltpu.SMEM),
             pl.BlockSpec(memory_space=pltpu.VMEM),
@@ -155,9 +155,7 @@
     mixed = jnp.sum(gates[:, :, None, None] * out_pairs, axis=1).astype(jnp.bfloat16)
     cot_f = cotangent.reshape(tok_rows, 1, sub, LANES).astype(jnp.float32)
     gate_grad = jnp.sum(cot_f * out_pairs, axis=(2, 3))
-    in_grad = combine_rows(place, grad_back.reshape(-1, sub, LANES), tok_rows, top_count).astype(
-        jnp.bfloat16
-    )
+    in_grad = combine_rows(place, grad_back.reshape(-1, sub, LANES), tok_rows, top_count)
     return (mixed.reshape(tok_rows, width), in_grad.reshape(tok_rows, width), gate_grad)
 
 

time: 364 us -> 362 us (level)
  transfers between devices with their start and end apart: 4 -> 4, of which waited for: 4 -> 4; matrix products, arithmetic and copies ran while one was open for 25% -> 26% of each run, Pallas kernels for 2% -> 2%
where the time goes in v13:
time: 362 us; the launch traced here: 361 us
  waiting for transfers between devices  209 us (58%)
  matrix products  58.1 us (16%)
  local copies, waits for them, and re-layouts  32 us (9%)
  starting transfers between devices  28.1 us (8%)
  Pallas kernels  18.8 us (5%)
  other arithmetic  14.2 us (4%)
    all_to_all x1, waiting for transfers between devices, body(): lax.all_to_all(send_x, 'ep', split_axis=0, concat_axis=0, tiled=True)  67.8 us
    all_to_all x1, waiting for transfers between devices, body(): lax.all_to_all(pair_grad.reshape(count, slots, sub, LANES), 'ep', split_a...  57.3 us
    all_to_all x1, waiting for transfers between devices, body(): lax.all_to_all(send_c, 'ep', split_axis=0, concat_axis=0, tiled=True)  47.1 us
    all_to_all x1, waiting for transfers between devices, body(): lax.all_to_all(out_rows.reshape(count, slots, sub, LANES), 'ep', split_ax...  37 us
    unnamed x30, local copies, waits for them, and re-layouts  20.6 us
    dot_general x1, matrix products, project_back(): lax.dot_general(grad_a, wg, (((1,), (1,)), ((), ())), preferred_element_t...  14.7 us
    pallas_call x2, Pallas kernels, gather_tiles(): pl.pallas_call(kernel, out_shape=jax.ShapeDtypeStruct((total,) + src3.sha...  13.5 us
    dot_general x1, matrix products, project_back(): lax.dot_general(grad_b, wu, (((1,), (1,)), ((), ())), preferred_element_t...  11.3 us
  transfers between devices with their start and end apart: 4, of which 4 were waited for; matrix products, arithmetic and copies ran while one was open for 26% of the time, Pallas kernels for 2%

profile of v13, /device:TPU:27, one launch (start us, length us, event | category | flops | bytes accessed | tf_op | source)
XLA Modules:
  0.0 361.0 jit_solution(13987633980218191879)
XLA Ops:
  0.6 0.0 copy-start
  0.6 0.8 and_select_fusion.1
  1.5 0.9 select_reduce_fusion.3
  2.3 0.7 fusion.34
  3.0 0.8 copy.21
  3.8 0.1 eq.28
  3.9 0.4 select_reduce_fusion.2
  4.3 0.5 convert_reduce_fusion
  4.8 0.9 select_reduce_fusion.1
  5.7 0.6 fusion.29.row_ref
  6.3 1.9 copy.24
  8.3 6.5 %shard_map.112 = bf16[1536,16,128]{2,1,0:T(8,128)(2,1)} custom-call(s32[1536]{0:T(1024)} %fusion.29.row_ref, bf16[128,16,128]{2,1,0:T(8,128)(2,1)} %bitcast.64), custom_call_target="tpu_custom_call" | custom-call | tf_op jit(solution)/shard_map/pallas_call | solution.py:91
  14.8 10.9 %all-to-all-start = ((bf16[128,12,16,128]{3,2,1,0:T(8,128)(2,1)}), bf16[128,12,16,128]{3,2,1,0:T(8,128)(2,1)}, u32[]{:S(2)}, u32[]{:S(2)}) async-start(bf16[128,12,16,128]{3,2,1,0:T(8,128)(2,1)} %bitcast.61), calls=%async_computation | async-start | bytes 12582912 | tf_op jit(solution)/shard_map/all_to_all | solution.py:138
  25.8 0.1 copy.20
  25.9 0.1 broadcast_in_dim.70
  26.0 2.0 copy.28
  27.9 1.3 select_reduce_fusion.refs_0_
  29.2 7.0 %shard_map.113 = bf16[1536,16,128]{2,1,0:T(8,128)(2,1)} custom-call(s32[1536]{0:T(1024)} %fusion.29.row_ref, f32[1536]{0:T(1024)} %select_reduce_fusion.refs_0_, bf16[128,16,128]{2,1,0:T(8,128)(2,1)} %bitcast.62), custom_call_target="tpu_custom_call" | custom-call | tf_op jit(solution)/shard_map/pallas_call | solution.py:91
  36.2 67.8 %all-to-all-done = bf16[128,12,16,128]{3,2,1,0:T(8,128)(2,1)} async-done(((bf16[128,12,16,128]{3,2,1,0:T(8,128)(2,1)}), bf16[128,12,16,128]{3,2,1,0:T(8,128)(2,1)}, u32[]{:S(2)}, u32[]{:S(2)}) %all-to-all-start) | async-done | bytes 6291488 | tf_op jit(solution)/shard_map/all_to_all | solution.py:138
  104.0 5.8 %all-to-all-start.2 = ((bf16[128,12,16,128]{3,2,1,0:T(8,128)(2,1)}), bf16[128,12,16,128]{3,2,1,0:T(8,128)(2,1)}, u32[]{:S(2)}, u32[]{:S(2)}) async-start(bf16[128,12,16,128]{3,2,1,0:T(8,128)(2,1)} %bitcast.60), calls=%async_computation.2 | async-start | bytes 12582912 | tf_op jit(solution)/shard_map/all_to_all | solution.py:139
  109.8 0.0 copy-start.6
  109.8 9.0 %fusion.7 = f32[1536,768]{1,0:T(8,128)S(1)} fusion(bf16[192,8,16,128]{3,2,1,0:T(8,128)(2,1)} %bitcast.14, bf16[1,2048,768]{2,1,0:T(8,128)(2,1)} %param.15), kind=kOutput, calls=%fused_computation.12 | convolution fusion | flops 4831838208 | bytes 14155776 | tf_op jit(solution)/shard_map/dot_general | solution.py:12
  118.9 9.6 %fusion.5 = f32[1536,768]{1,0:T(8,128)S(1)} fusion(bf16[192,8,16,128]{3,2,1,0:T(8,128)(2,1)} %bitcast.14, bf16[1,2048,768]{2,1,0:T(8,128)(2,1)S(1)} %copy-done.6), kind=kOutput, calls=%fused_computation.10 | convolution fusion | flops 4831838208 | bytes 14155776 | tf_op jit(solution)/shard_map/dot_general | solution.py:13
  128.5 0.0 copy-done.8
  128.5 0.0 copy-start.9
  128.5 2.1 copy-done.9
  130.6 5.4 %fusion.22 = bf16[192,8,16,128]{3,1,2,0:T(8,128)(2,1)S(1)} fusion(bf16[1,768,2048]{2,1,0:T(8,128)(2,1)S(1)} %copy-done, f32[1536,768]{1,0:T(8,128)S(1)} %fusion.5, f32[1536,768]{1,0:T(8,128)S(1)} %fusion.7), kind=kOutput, calls=%fused_computation.34 | convolution fusion | flops 4842061824 | bytes 18874368 | tf_op jit(solution)/shard_map/dot_general | solution.py:20
  136.0 4.9 %copy.26 = bf16[192,8,16,128]{3,2,1,0:T(8,128)(2,1)} copy(bf16[192,8,16,128]{3,1,2,0:T(8,128)(2,1)S(1)} %fusion.22) | data formatting | bytes 12582912
  140.9 47.1 %all-to-all-done.2 = bf16[128,12,16,128]{3,2,1,0:T(8,128)(2,1)} async-done(((bf16[128,12,16,128]{3,2,1,0:T(8,128)(2,1)}), bf16[128,12,16,128]{3,2,1,0:T(8,128)(2,1)}, u32[]{:S(2)}, u32[]{:S(2)}) %all-to-all-start.2) | async-done | bytes 6291488 | tf_op jit(solution)/shard_map/all_to_all | solution.py:139
  188.0 5.7 %all-to-all-start.1 = ((bf16[128,12,16,128]{3,2,1,0:T(8,128)(2,1)}), bf16[128,12,16,128]{3,2,1,0:T(8,128)(2,1)}, u32[]{:S(2)}, u32[]{:S(2)}) async-start(bf16[128,12,16,128]{3,2,1,0:T(8,128)(2,1)} %bitcast.59), calls=%async_computation.1 | async-start | bytes 12582912 | tf_op jit(solution)/shard_map/all_to_all | solution.py:143
  193.7 0.0 copy-start.5
  193.7 8.1 %fusion.2 = f32[1536,768]{1,0:T(8,128)S(1)} fusion(bf16[192,8,16,128]{3,2,1,0:T(8,128)(2,1)} %bitcast.24, bf16[1,768,2048]{2,1,0:T(8,128)(2,1)S(1)} %copy-done), kind=kOutput, calls=%fused_computation.7 | convolution fusion | flops 4831838208 | bytes 14155776 | tf_op jit(solution)/shard_map/dot_general | solution.py:25
  201.8 2.1 copy-done.10
  204.0 0.0 copy-done.5
  204.0 14.7 %fusion.16 = f32[1536,2048]{1,0:T(8,128)} fusion(bf16[1,2048,768]{2,1,0:T(8,128)(2,1)S(1)} %copy-done.5, f32[1536,768]{1,0:T(8,128)} %copy-done.8, f32[1536,768]{1,0:T(8,128)S(1)} %fusion.2, f32[1536,768]{1,0:T(8,128)} %copy-done.9), kind=kOutput, calls=%fused_computation.30 | convolution fusion | flops 4843634688 | bytes 29884416 | tf_op jit(solution)/shard_map/dot_general | solution.py:30
  218.7 11.3 %fusion.19 = bf16[192,8,16,128]{3,1,2,0:T(8,128)(2,1)S(1)} fusion(f32[1536,2048]{1,0:T(8,128)} %fusion.16, bf16[1,2048,768]{2,1,0:T(8,128)(2,1)S(1)} %copy-done.7, f32[1536,768]{1,0:T(8,128)} %copy-done.10, f32[1536,768]{1,0:T(8,128)} %copy-done.8), kind=kOutput, calls=%fused_computation.33 | convolution fusion | flops 4845207552 | bytes 31457280 | tf_op jit(solution)/shard_map/dot_general | solution.py:33
  229.9 5.0 %copy.30 = bf16[192,8,16,128]{3,2,1,0:T(8,128)(2,1)} copy(bf16[192,8,16,128]{3,1,2,0:T(8,128)(2,1)S(1)} %fusion.19) | data formatting | bytes 12582912
  234.9 37.0 %all-to-all-done.1 = bf16[128,12,16,128]{3,2,1,0:T(8,128)(2,1)} async-done(((bf16[128,12,16,128]{3,2,1,0:T(8,128)(2,1)}), bf16[128,12,16,128]{3,2,1,0:T(8,128)(2,1)}, u32[]{:S(2)}, u32[]{:S(2)}) %all-to-all-start.1) | async-done | bytes 6291488 | tf_op jit(solution)/shard_map/all_to_all | solution.py:143
  271.9 5.7 %all-to-all-start.3 = ((bf16[128,12,16,128]{3,2,1,0:T(8,128)(2,1)}), bf16[128,12,16,128]{3,2,1,0:T(8,128)(2,1)}, u32[]{:S(2)}, u32[]{:S(2)}) async-start(bf16[128,12,16,128]{3,2,1,0:T(8,128)(2,1)} %bitcast.58), calls=%async_computation.3 | async-start | bytes 12582912 | tf_op jit(solution)/shard_map/all_to_all | solution.py:147
  277.6 0.0 copy-done.3
  277.6 0.1 bitcast_convert_fusion
  277.7 11.2 %gather_fusion = bf16[1024,16,128]{2,1,0:T(8,128)(2,1)} fusion(bf16[1536,16,128]{2,1,0:T(8,128)(2,1)} %bitcast.4, s32[1024]{0:T(1024)S(1)} %broadcast_clamp_fusion), kind=kCustom, calls=%fused_computation | custom fusion | bytes 8392704 | tf_op jit(solution)/shard_map/gather | solution.py:151
  288.9 4.6 %fusion.1 = f32[128,8]{1,0:T(8,128)S(1)} fusion(bf16[128,8,16,128]{3,2,1,0:T(8,128)(2,1)} %bitcast.57, f32[128,16,128]{2,1,0:T(8,128)S(1)} %bitcast_convert_fusion), kind=kLoop, calls=%fused_computation.5 | loop fusion | flops 6290432 | bytes 5246976 | tf_op jit(solution)/shard_map/reduce_sum | solution.py:157
  293.5 0.7 copy.23
  294.1 3.5 fusion
  297.6 0.9 copy.44
  298.5 57.3 %all-to-all-done.3 = bf16[128,12,16,128]{3,2,1,0:T(8,128)(2,1)} async-done(((bf16[128,12,16,128]{3,2,1,0:T(8,128)(2,1)}), bf16[128,12,16,128]{3,2,1,0:T(8,128)(2,1)}, u32[]{:S(2)}, u32[]{:S(2)}) %all-to-all-start.3) | async-done | bytes 6291488 | tf_op jit(solution)/shard_map/all_to_all | solution.py:147
  355.8 5.2 %shard_map.114 = bf16[128,2048]{1,0:T(8,128)(2,1)} custom-call(s32[1024]{0:T(1024)} %copy-done.3, bf16[1536,16,128]{2,1,0:T(8,128)(2,1)} %bitcast.9.rows_ref), custom_call_target="tpu_custom_call" | custom-call | tf_op jit(solution)/shard_map/pallas_call | solution.py:57
  (16 shorter events, 0.0 us)
Async XLA Ops:
  0.6 130.0 %copy-start = (bf16[1,768,2048]{2,1,0:T(8,128)(2,1)S(1)}, bf16[1,768,2048]{2,1,0:T(8,128)(2,1)}, u32[]{:S(2)}) copy-start(bf16[1,768,2048]{2,1,0:T(8,128)(2,1)} %param.17) | copy-start | bytes 9437188
  4.8 272.8 %copy-start.3 = (s32[1024]{0:T(1024)}, s32[1024]{0:T(1024)S(1)}, u32[]{:S(2)}) copy-start(s32[1024]{0:T(1024)S(1)} %multiply_add_fusion.place_ref) | copy-start | bytes 12292
  14.8 11.0 %copy-start.4 = (f32[128,8]{0,1:T(8,128)S(1)}, f32[128,8]{0,1:T(8,128)}, u32[]{:S(2)}) copy-start(f32[128,8]{0,1:T(8,128)} %param.11) | copy-start | bytes 12292
  14.8 89.2 %all-to-all-start = ((bf16[128,12,16,128]{3,2,1,0:T(8,128)(2,1)}), bf16[128,12,16,128]{3,2,1,0:T(8,128)(2,1)}, u32[]{:S(2)}, u32[]{:S(2)}) async-start(bf16[128,12,16,128]{3,2,1,0:T(8,128)(2,1)} %bitcast.61), calls=%async_computation | async-start | bytes 12582912 | tf_op jit(solution)/shard_map/all_to_all | solution.py:138
  104.0 84.0 %all-to-all-start.2 = ((bf16[128,12,16,128]{3,2,1,0:T(8,128)(2,1)}), bf16[128,12,16,128]{3,2,1,0:T(8,128)(2,1)}, u32[]{:S(2)}, u32[]{:S(2)}) async-start(bf16[128,12,16,128]{3,2,1,0:T(8,128)(2,1)} %bitcast.60), calls=%async_computation.2 | async-start | bytes 12582912 | tf_op jit(solution)/shard_map/all_to_all | solution.py:139
  109.8 9.1 %copy-start.6 = (bf16[1,2048,768]{2,1,0:T(8,128)(2,1)S(1)}, bf16[1,2048,768]{2,1,0:T(8,128)(2,1)}, u32[]{:S(2)}) copy-start(bf16[1,2048,768]{2,1,0:T(8,128)(2,1)} %param.16) | copy-start | bytes 9437188
  118.8 9.6 %copy-start.8 = (f32[1536,768]{1,0:T(8,128)}, f32[1536,768]{1,0:T(8,128)S(1)}, u32[]{:S(2)}) copy-start(f32[1536,768]{1,0:T(8,128)S(1)} %fusion.7) | copy-start | bytes 14155780
  128.5 2.1 copy-start.9
  188.0 83.9 %all-to-all-start.1 = ((bf16[128,12,16,128]{3,2,1,0:T(8,128)(2,1)}), bf16[128,12,16,128]{3,2,1,0:T(8,128)(2,1)}, u32[]{:S(2)}, u32[]{:S(2)}) async-start(bf16[128,12,16,128]{3,2,1,0:T(8,128)(2,1)} %bitcast.59), calls=%async_computation.1 | async-start | bytes 12582912 | tf_op jit(solution)/shard_map/all_to_all | solution.py:143
  193.7 10.3 %copy-start.5 = (bf16[1,2048,768]{2,1,0:T(8,128)(2,1)S(1)}, bf16[1,2048,768]{2,1,0:T(8,128)(2,1)}, u32[]{:S(2)}) copy-start(bf16[1,2048,768]{2,1,0:T(8,128)(2,1)} %param.15) | copy-start | bytes 9437188
  201.8 2.1 copy-start.10
  204.0 14.7 %copy-start.7 = (bf16[1,2048,768]{2,1,0:T(8,128)(2,1)S(1)}, bf16[1,2048,768]{2,1,0:T(8,128)(2,1)}, u32[]{:S(2)}) copy-start(bf16[1,2048,768]{2,1,0:T(8,128)(2,1)} %param.16) | copy-start | bytes 9437188
  271.9 5.7 %copy-start.2 = (bf16[16,8,16,128]{3,2,1,0:T(8,128)(2,1)S(1)}, bf16[16,8,16,128]{3,2,1,0:T(8,128)(2,1)}, u32[]{:S(2)}) copy-start(bf16[16,8,16,128]{3,2,1,0:T(8,128)(2,1)} %copy.28) | copy-start | bytes 1572868
  271.9 83.9 %all-to-all-start.3 = ((bf16[128,12,16,128]{3,2,1,0:T(8,128)(2,1)}), bf16[128,12,16,128]{3,2,1,0:T(8,128)(2,1)}, u32[]{:S(2)}, u32[]{:S(2)}) async-start(bf16[128,12,16,128]{3,2,1,0:T(8,128)(2,1)} %bitcast.58), calls=%async_computation.3 | async-start | bytes 12582912 | tf_op jit(solution)/shard_map/all_to_all | solution.py:147
  294.1 66.9 %copy-start.1 = (bf16[1,768,2048]{2,1,0:T(8,128)(2,1)S(1)}, bf16[1,768,2048]{2,1,0:T(8,128)(2,1)}, u32[]{:S(2)}) copy-start(bf16[1,768,2048]{2,1,0:T(8,128)(2,1)} %param.17) | copy-start | bytes 9437188
